TPU v7x, 1024 devices: a whole 4x4x32 slice. The times are simulated.
1024 devices in a mesh: grp: 16 (over y, z_hi), dev: 64 (over z_lo, x, core).
Axes of the slice: x: 4, y: 4, z: 32 (z_hi: 4, z_lo: 8; z = z_hi * 8 + z_lo), core: 2. Of those that a mesh axis runs over, the one named last changes fastest.
Arguments:
- amplitudes: float32 [2, 16, 64, 8192], P(None, 'grp', 'dev'), may hold values from -6 to 6
- joined_gates: float32 [4, 2, 128, 128], replicated, may hold values from -0.375 to 0.375
- pair_gate: float32 [2, 4, 4], replicated, may hold values from -2 to 2
- layout_in: int32 [23], replicated, may hold values from 0 to 22, as said below
- layout_out: int32 [23], replicated, may hold values from 0 to 22, as said below
- gate_qubits: int32 [4, 7], replicated, may hold values from 0 to 22, as said below
- spare_values: int32 [10], replicated, may hold values from 0 to 1
Outputs:
- evolved: float32 [2, 16, 64, 8192], P(None, 'grp', 'dev')
Inputs may be any that keep to these rules, and one draw needn't show every extreme that they name: `layout_in`: a permutation of the qubits. `layout_out`: a permutation of the qubits; entries 13 + 6 onward equal those of layout_in; entries 13 to 18 are qubits that layout_in holds below position 13. `gate_qubits`: each row holds 7 different qubits; rows 0 and 1 name qubits that layout_in holds below position 13, rows 2 and 3 qubits that layout_out holds below position 13.
All inputs are finite; a program needn't handle non-finite values.
Results may differ from a plain program's by a relative error of at most 0.0001.
Values sent between devices are 32-bit elements; how exact they have to be, the bound alone decides.
No kernel may reach another device: no remote copies, remote signals or barrier semaphores. Data moves between devices by JAX's collectives and lax.ppermute only.
A program may use at most 32 MiB of HBM per device.

v0:
```python
import jax
import jax.numpy as jnp
from jax import lax
from jax.sharding import PartitionSpec as P

HIGHEST = lax.Precision.HIGHEST


def swapped(value, axis, bit):
    mask = 2**bit
    pairs = [(source, source ^ mask) for source in range(lax.axis_size(axis))]
    return lax.ppermute(value, axis, pairs)


def source_index(bit_order, bit_count):
    position = jnp.arange(2**bit_count, dtype=jnp.int32)
    source = jnp.zeros((2**bit_count,), jnp.int32)
    for place_bit in range(bit_count):
        source = source + jnp.left_shift(
            jnp.right_shift(position, place_bit) & 1, bit_order[place_bit]
        )
    return source


def reorder(values, source):
    return jnp.take(values, source_index(source, source.shape[0]), axis=1)


def complex_gate(values, matrix):
    real_part = jnp.dot(
        values[0], matrix[0].T, precision=HIGHEST, preferred_element_type=jnp.float32
    ) - jnp.dot(values[1], matrix[1].T, precision=HIGHEST, preferred_element_type=jnp.float32)
    imag_part = jnp.dot(
        values[0], matrix[1].T, precision=HIGHEST, preferred_element_type=jnp.float32
    ) + jnp.dot(values[1], matrix[0].T, precision=HIGHEST, preferred_element_type=jnp.float32)
    return jnp.stack([real_part, imag_part])


def pair_apply(values, pos_a, pos_c, matrix):
    count_all = values.shape[1]
    lower_pos = min(pos_a, pos_c)
    upper_pos = max(pos_a, pos_c)
    shaped = values.reshape(
        2, count_all >> upper_pos + 1, 2, 1 << upper_pos - lower_pos - 1, 2, 1 << lower_pos
    )
    tensor = matrix.reshape(2, 2, 2, 2, 2)
    pattern = "uvwx,hwmxl->humvl"
    real_part = jnp.einsum(pattern, tensor[0], shaped[0], precision=HIGHEST) - jnp.einsum(
        pattern, tensor[1], shaped[1], precision=HIGHEST
    )
    imag_part = jnp.einsum(pattern, tensor[1], shaped[0], precision=HIGHEST) + jnp.einsum(
        pattern, tensor[0], shaped[1], precision=HIGHEST
    )
    return jnp.stack([real_part, imag_part]).reshape(2, count_all)


def spare_sign(count_all, spare_values):
    position = jnp.arange(count_all, dtype=jnp.int32)
    parity = jnp.zeros((count_all,), jnp.int32)
    for place_bit in range(spare_values.shape[0]):
        parity = parity + spare_values[place_bit] * (jnp.right_shift(position, place_bit) & 1)
    return (1 - 2 * (parity & 1)).astype(jnp.float32)


def position_of(layout, wanted):
    places = jnp.arange(layout.shape[0], dtype=jnp.int32)
    return jnp.sum(jnp.where(layout[None, :] == wanted[:, None], places[None, :], 0), axis=1)


def arrange(layout, leading, trailing):
    layout_len = layout.shape[0]
    lead_count = leading.shape[0]
    trail_count = trailing.shape[0]
    in_lead = layout[:, None] == leading[None, :]
    in_trail = layout[:, None] == trailing[None, :]
    lead_any = jnp.any(in_lead, axis=1)
    trail_any = jnp.any(in_trail, axis=1)
    remaining = jnp.logical_not(jnp.logical_or(lead_any, trail_any)).astype(jnp.int32)
    lead_rank = jnp.sum(in_lead * jnp.arange(lead_count, dtype=jnp.int32)[None, :], axis=1)
    trail_rank = (
        layout_len
        - trail_count
        + jnp.sum(in_trail * jnp.arange(trail_count, dtype=jnp.int32)[None, :], axis=1)
    )
    target = jnp.where(
        lead_any,
        lead_rank,
        jnp.where(trail_any, trail_rank, lead_count + jnp.cumsum(remaining) - 1),
    )
    places = jnp.arange(layout_len, dtype=jnp.int32)
    source = jnp.zeros((layout_len,), jnp.int32).at[target].set(places)
    new_layout = jnp.zeros((layout_len,), jnp.int32).at[target].set(layout)
    return (new_layout, source)


def halves(values, place_bit):
    count_all = values.shape[1]
    shaped = values.reshape(2, count_all >> place_bit + 1, 2, 1 << place_bit)
    return (shaped[:, :, 0], shaped[:, :, 1])


def rejoin(lower_half, upper_half, received, own_bit):
    keep_lower = own_bit == 0
    new_lower = jnp.where(keep_lower, lower_half, received)
    new_upper = jnp.where(keep_lower, received, upper_half)
    return jnp.stack([new_lower, new_upper], axis=2).reshape(2, -1)


def trade_group(values, place_bit, bit_num):
    lower_half, upper_half = halves(values, place_bit)
    own_bit = jnp.right_shift(lax.axis_index("grp"), bit_num) & 1
    outgoing = jnp.where(own_bit == 0, upper_half, lower_half)
    received = swapped(outgoing, "grp", bit_num)
    return rejoin(lower_half, upper_half, received, own_bit)


def per_device(
    amplitudes, joined_gates, pair_gate, layout_in, layout_out, gate_qubits, spare_values
):
    length = amplitudes.shape[-1]
    local_bits = length.bit_length() - 1
    devices = lax.axis_size("dev")
    device_bits = devices.bit_length() - 1
    groups = lax.axis_size("grp")
    group_bits = groups.bit_length() - 1
    span_size = joined_gates.shape[-1]
    values = amplitudes.reshape(2, length)
    nothing = jnp.zeros((0,), jnp.int32)
    layout = layout_in[:local_bits]
    for gate_num in range(2):
        layout, source = arrange(layout, gate_qubits[gate_num], nothing)
        values = complex_gate(
            reorder(values, source).reshape(2, -1, span_size), joined_gates[gate_num]
        ).reshape(2, length)
    leaving = layout_out[local_bits : local_bits + device_bits]
    layout, source = arrange(layout, nothing, leaving)
    values = reorder(values, source)
    shaped = values.reshape(2, devices, length // devices)
    values = lax.all_to_all(shaped, "dev", split_axis=1, concat_axis=1, tiled=True).reshape(
        2, length
    )
    layout = jnp.concatenate(
        [layout[: local_bits - device_bits], layout_in[local_bits : local_bits + device_bits]]
    )
    for gate_num in range(2, 4):
        layout, source = arrange(layout, gate_qubits[gate_num], nothing)
        values = complex_gate(
            reorder(values, source).reshape(2, -1, span_size), joined_gates[gate_num]
        ).reshape(2, length)
    values = reorder(values, position_of(layout, layout_out[:local_bits]))
    values = values * spare_sign(length, spare_values)
    for bit_num in range(group_bits):
        place_bit = local_bits - 2 * group_bits + bit_num
        values = trade_group(values, place_bit, bit_num)
        values = pair_apply(values, place_bit, local_bits - 1 - bit_num, pair_gate)
        values = trade_group(values, place_bit, bit_num)
    return values.reshape(amplitudes.shape)


def solution(mesh):
    in_specs = (P(None, "grp", "dev", None), P(), P(), P(), P(), P(), P())
    out_specs = P(None, "grp", "dev", None)
    return jax.shard_map(
        per_device, mesh=mesh, in_specs=in_specs, out_specs=out_specs, check_vma=False
    )
```

profile of v0, /device:TPU:24, one launch (start us, length us, event | category | flops | bytes accessed | tf_op | source)
XLA Modules:
  0.0 515.1 jit_solution(2299605073766334633)
XLA Ops:
  0.0 0.8 slice_bitcast_fusion.4
  0.8 0.7 compare_reduce_fusion.4
  1.6 0.7 fusion.97
  3.1 0.7 fusion.163
  3.8 8.2 %broadcast_clamp_fusion.5 = s32[8192]{0:T(1024)S(1)} fusion(s32[]{:T(128)} %bitcast.96, s32[]{:T(128)} %bitcast.95, s32[]{:T(128)} %bitcast.94, s32[]{:T(128)} %bitcast.93, s32[]{:T(128)} %bitcast.92, s32[]{:T(128)} %bitcast.91, s32[]{:T(128)} %bitcast.90, s32[]{:T(128)} %bitcast.89, s32[]{:T(128)} %bitcast.88, s32[]{:T(128)} %bitcast.87, s32[]{:T(128)} %bitcast.86, ...), kind=kLoop, calls=%fused_computation.235 | loop fusion | flops 450560 | bytes 32820 | tf_op gather
  12.0 8.2 %compare_and_fusion.5 = pred[8192]{0:T(1024)(128)(4,1)S(1)} fusion(s32[]{:T(128)} %bitcast.96, s32[]{:T(128)} %bitcast.95, s32[]{:T(128)} %bitcast.94, s32[]{:T(128)} %bitcast.93, s32[]{:T(128)} %bitcast.92, s32[]{:T(128)} %bitcast.91, s32[]{:T(128)} %bitcast.90, s32[]{:T(128)} %bitcast.89, s32[]{:T(128)} %bitcast.88, s32[]{:T(128)} %bitcast.87, ...), kind=kLoop, calls=%fused_computation.221 | loop fusion | flops 466944 | bytes 8244 | tf_op jit(solution)/shard_map/jit(_take)/and | solution.py:26
  20.2 3.3 copy.220
  23.6 29.9 %gather_fusion = f32[8192,2]{1,0:T(8,128)} fusion(f32[2,8192]{0,1:T(8,128)} %bitcast.596, s32[8192]{0:T(1024)S(1)} %broadcast_clamp_fusion.5), kind=kCustom, calls=%fused_computation.clone | custom fusion | bytes 163840 | tf_op jit(solution)/shard_map/jit(_take)/gather | solution.py:26
  53.5 6.2 %select_bitcast_fusion.3 = f32[2,8192]{0,1:T(8,128)S(1)} fusion(f32[8192,2]{1,0:T(8,128)} %gather_fusion, pred[8192]{0:T(1024)(128)(4,1)S(1)} %compare_and_fusion.5), kind=kLoop, calls=%fused_computation.28 | loop fusion | flops 16384 | bytes 139264 | tf_op jit(solution)/shard_map/jit(_take)/select_n | solution.py:26
  59.7 3.3 slice_reduce_fusion.6
  65.9 8.2 %broadcast_clamp_fusion.4 = s32[8192]{0:T(1024)S(1)} fusion(s32[]{:T(128)} %bitcast.83, s32[]{:T(128)} %bitcast.82, s32[]{:T(128)} %bitcast.81, s32[]{:T(128)} %bitcast.80, s32[]{:T(128)} %bitcast.79, s32[]{:T(128)} %bitcast.78, s32[]{:T(128)} %bitcast.77, s32[]{:T(128)} %bitcast.76, s32[]{:T(128)} %bitcast.75, s32[]{:T(128)} %bitcast.74, s32[]{:T(128)} %bitcast.73, ...), kind=kLoop, calls=%fused_computation.234 | loop fusion | flops 450560 | bytes 32820 | tf_op gather
  74.1 8.2 %compare_and_fusion.4 = pred[8192]{0:T(1024)(128)(4,1)S(1)} fusion(s32[]{:T(128)} %bitcast.83, s32[]{:T(128)} %bitcast.82, s32[]{:T(128)} %bitcast.81, s32[]{:T(128)} %bitcast.80, s32[]{:T(128)} %bitcast.79, s32[]{:T(128)} %bitcast.78, s32[]{:T(128)} %bitcast.77, s32[]{:T(128)} %bitcast.76, s32[]{:T(128)} %bitcast.75, s32[]{:T(128)} %bitcast.74, ...), kind=kLoop, calls=%fused_computation.220 | loop fusion | flops 466944 | bytes 8244 | tf_op jit(solution)/shard_map/jit(_take)/and | solution.py:26
  82.9 2.6 copy.221
  85.5 29.9 %gather_fusion.1 = f32[8192,2]{1,0:T(8,128)} fusion(f32[2,8192]{0,1:T(8,128)} %copy.221, s32[8192]{0:T(1024)S(1)} %broadcast_clamp_fusion.4), kind=kCustom, calls=%fused_computation.1.clone | custom fusion | bytes 163840 | tf_op jit(solution)/shard_map/jit(_take)/gather | solution.py:26
  115.4 6.2 %select_bitcast_fusion.2 = f32[2,8192]{0,1:T(8,128)S(1)} fusion(f32[8192,2]{1,0:T(8,128)} %gather_fusion.1, pred[8192]{0:T(1024)(128)(4,1)S(1)} %compare_and_fusion.4), kind=kLoop, calls=%fused_computation.27 | loop fusion | flops 16384 | bytes 139264 | tf_op jit(solution)/shard_map/jit(_take)/select_n | solution.py:26
  121.7 3.3 slice_reduce_fusion.4
  126.6 0.8 scatter_custom_fusion.4
  127.4 0.7 fusion.161
  128.1 8.2 %broadcast_clamp_fusion.3 = s32[8192]{0:T(1024)S(1)} fusion(s32[]{:T(128)} %bitcast.70, s32[]{:T(128)} %bitcast.69, s32[]{:T(128)} %bitcast.68, s32[]{:T(128)} %bitcast.67, s32[]{:T(128)} %bitcast.66, s32[]{:T(128)} %bitcast.65, s32[]{:T(128)} %bitcast.64, s32[]{:T(128)} %bitcast.63, s32[]{:T(128)} %bitcast.62, s32[]{:T(128)} %bitcast.61, s32[]{:T(128)} %bitcast.60, ...), kind=kLoop, calls=%fused_computation.233 | loop fusion | flops 450560 | bytes 32820 | tf_op gather
  136.3 8.2 %compare_and_fusion.3 = pred[8192]{0:T(1024)(128)(4,1)S(1)} fusion(s32[]{:T(128)} %bitcast.70, s32[]{:T(128)} %bitcast.69, s32[]{:T(128)} %bitcast.68, s32[]{:T(128)} %bitcast.67, s32[]{:T(128)} %bitcast.66, s32[]{:T(128)} %bitcast.65, s32[]{:T(128)} %bitcast.64, s32[]{:T(128)} %bitcast.63, s32[]{:T(128)} %bitcast.62, s32[]{:T(128)} %bitcast.61, ...), kind=kLoop, calls=%fused_computation.219 | loop fusion | flops 466944 | bytes 8244 | tf_op jit(solution)/shard_map/jit(_take)/and | solution.py:26
  145.0 2.6 copy.222
  147.7 29.9 %gather_fusion.2 = f32[8192,2]{1,0:T(8,128)} fusion(f32[2,8192]{0,1:T(8,128)} %copy.222, s32[8192]{0:T(1024)S(1)} %broadcast_clamp_fusion.3), kind=kCustom, calls=%fused_computation.2.clone | custom fusion | bytes 163840 | tf_op jit(solution)/shard_map/jit(_take)/gather | solution.py:26
  177.6 7.5 %broadcast_select_fusion = f32[8192,2]{1,0:T(8,128)} fusion(f32[8192,2]{1,0:T(8,128)} %gather_fusion.2, pred[8192]{0:T(1024)(128)(4,1)S(1)} %compare_and_fusion.3), kind=kLoop, calls=%fused_computation.29 | loop fusion | flops 16384 | bytes 139264 | tf_op jit(solution)/shard_map/jit(_take)/select_n | solution.py:26
  185.0 3.5 copy.223
  188.5 16.0 %all-to-all-start = ((f32[2,64,128]{2,0,1:T(2,128)}), f32[2,64,128]{2,0,1:T(2,128)S(1)}, u32[]{:S(2)}, u32[]{:S(2)}) async-start(f32[2,64,128]{2,0,1:T(2,128)} %copy.223), calls=%async_computation | async-start | bytes 131072 | tf_op jit(solution)/shard_map/all_to_all | solution.py:139
  210.1 0.7 fusion.158
  211.5 8.2 %compare_and_fusion.2 = pred[8192]{0:T(1024)(128)(4,1)S(1)} fusion(s32[]{:T(128)} %bitcast.57, s32[]{:T(128)} %bitcast.56, s32[]{:T(128)} %bitcast.55, s32[]{:T(128)} %bitcast.54, s32[]{:T(128)} %bitcast.53, s32[]{:T(128)} %bitcast.52, s32[]{:T(128)} %bitcast.51, s32[]{:T(128)} %bitcast.50, s32[]{:T(128)} %bitcast.49, s32[]{:T(128)} %bitcast.48, ...), kind=kLoop, calls=%fused_computation.218 | loop fusion | flops 466944 | bytes 8244 | tf_op jit(solution)/shard_map/jit(_take)/and | solution.py:26
  219.7 8.1 %compare_and_fusion.1 = pred[8192]{0:T(1024)(128)(4,1)S(1)} fusion(s32[]{:T(128)} %bitcast.44, s32[]{:T(128)} %bitcast.43, s32[]{:T(128)} %bitcast.42, s32[]{:T(128)} %bitcast.41, s32[]{:T(128)} %bitcast.40, s32[]{:T(128)} %bitcast.39, s32[]{:T(128)} %bitcast.38, s32[]{:T(128)} %bitcast.37, s32[]{:T(128)} %bitcast.36, s32[]{:T(128)} %bitcast.35, ...), kind=kLoop, calls=%fused_computation.217 | loop fusion | flops 466944 | bytes 8244 | tf_op jit(solution)/shard_map/jit(_take)/and | solution.py:26
  227.8 8.3 %compare_and_fusion = pred[8192]{0:T(1024)(128)(4,1)S(1)} fusion(s32[]{:T(128)} %bitcast.31, s32[]{:T(128)} %bitcast.30, s32[]{:T(128)} %bitcast.29, s32[]{:T(128)} %bitcast.28, s32[]{:T(128)} %bitcast.27, s32[]{:T(128)} %bitcast.26, s32[]{:T(128)} %bitcast.25, s32[]{:T(128)} %bitcast.24, s32[]{:T(128)} %bitcast.23, s32[]{:T(128)} %bitcast.22, s32[]{:T(128)} %bitcast.21, ...), kind=kLoop, calls=%fused_computation.216 | loop fusion | flops 466944 | bytes 8244 | tf_op jit(solution)/shard_map/jit(_take)/and | solution.py:26
  236.1 8.2 %broadcast_clamp_fusion.2 = s32[8192]{0:T(1024)S(1)} fusion(s32[]{:T(128)} %bitcast.57, s32[]{:T(128)} %bitcast.56, s32[]{:T(128)} %bitcast.55, s32[]{:T(128)} %bitcast.54, s32[]{:T(128)} %bitcast.53, s32[]{:T(128)} %bitcast.52, s32[]{:T(128)} %bitcast.51, s32[]{:T(128)} %bitcast.50, s32[]{:T(128)} %bitcast.49, s32[]{:T(128)} %bitcast.48, s32[]{:T(128)} %bitcast.47, ...), kind=kLoop, calls=%fused_computation.232 | loop fusion | flops 450560 | bytes 32820 | tf_op gather
  244.3 8.1 %broadcast_clamp_fusion.1 = s32[8192]{0:T(1024)S(1)} fusion(s32[]{:T(128)} %bitcast.44, s32[]{:T(128)} %bitcast.43, s32[]{:T(128)} %bitcast.42, s32[]{:T(128)} %bitcast.41, s32[]{:T(128)} %bitcast.40, s32[]{:T(128)} %bitcast.39, s32[]{:T(128)} %bitcast.38, s32[]{:T(128)} %bitcast.37, s32[]{:T(128)} %bitcast.36, s32[]{:T(128)} %bitcast.35, s32[]{:T(128)} %bitcast.34, ...), kind=kLoop, calls=%fused_computation.231 | loop fusion | flops 450560 | bytes 32820 | tf_op gather
  252.4 8.3 %broadcast_clamp_fusion = s32[8192]{0:T(1024)S(1)} fusion(s32[]{:T(128)} %bitcast.31, s32[]{:T(128)} %bitcast.30, s32[]{:T(128)} %bitcast.29, s32[]{:T(128)} %bitcast.28, s32[]{:T(128)} %bitcast.27, s32[]{:T(128)} %bitcast.26, s32[]{:T(128)} %bitcast.25, s32[]{:T(128)} %bitcast.24, s32[]{:T(128)} %bitcast.23, s32[]{:T(128)} %bitcast.22, s32[]{:T(128)} %bitcast.21, ...), kind=kLoop, calls=%fused_computation.230 | loop fusion | flops 450560 | bytes 32820 | tf_op gather
  260.8 6.2 %subtract_convert_fusion = f32[8192]{0:T(1024)S(1)} fusion(s32[]{:T(128)} %bitcast.131, s32[]{:T(128)} %bitcast.130, s32[]{:T(128)} %bitcast.129, s32[]{:T(128)} %bitcast.128, s32[]{:T(128)} %bitcast.127, s32[]{:T(128)} %bitcast.126, s32[]{:T(128)} %bitcast.125, s32[]{:T(128)} %bitcast.124, s32[]{:T(128)} %bitcast.123, s32[]{:T(128)} %bitcast.122), kind=kLoop, calls=%fused_computation.202 | loop fusion | flops 352256 | bytes 32808 | tf_op jit(solution)/shard_map/convert_element_type | solution.py:62
  266.9 2.6 copy.224
  269.5 29.9 %gather_fusion.3 = f32[8192,2]{1,0:T(8,128)} fusion(f32[2,8192]{0,1:T(8,128)} %bitcast.595, s32[8192]{0:T(1024)S(1)} %broadcast_clamp_fusion.2), kind=kCustom, calls=%fused_computation.3.clone | custom fusion | bytes 163840 | tf_op jit(solution)/shard_map/jit(_take)/gather | solution.py:26
  299.5 6.2 %select_bitcast_fusion.1 = f32[2,8192]{0,1:T(8,128)S(1)} fusion(f32[8192,2]{1,0:T(8,128)} %gather_fusion.3, pred[8192]{0:T(1024)(128)(4,1)S(1)} %compare_and_fusion.2), kind=kLoop, calls=%fused_computation.26 | loop fusion | flops 16384 | bytes 139264 | tf_op jit(solution)/shard_map/jit(_take)/select_n | solution.py:26
  305.7 3.3 slice_reduce_fusion.2
  310.1 2.6 copy.225
  312.7 29.9 %gather_fusion.4 = f32[8192,2]{1,0:T(8,128)} fusion(f32[2,8192]{0,1:T(8,128)} %copy.225, s32[8192]{0:T(1024)S(1)} %broadcast_clamp_fusion.1), kind=kCustom, calls=%fused_computation.4.clone | custom fusion | bytes 163840 | tf_op jit(solution)/shard_map/jit(_take)/gather | solution.py:26
  342.6 6.2 %select_bitcast_fusion = f32[2,8192]{0,1:T(8,128)S(1)} fusion(f32[8192,2]{1,0:T(8,128)} %gather_fusion.4, pred[8192]{0:T(1024)(128)(4,1)S(1)} %compare_and_fusion.1), kind=kLoop, calls=%fused_computation.25 | loop fusion | flops 16384 | bytes 139264 | tf_op jit(solution)/shard_map/jit(_take)/select_n | solution.py:26
  348.8 3.3 slice_reduce_fusion
  353.2 2.6 copy.226
  355.8 29.9 %gather_fusion.5 = f32[8192,2]{1,0:T(8,128)} fusion(f32[2,8192]{0,1:T(8,128)} %copy.226, s32[8192]{0:T(1024)S(1)} %broadcast_clamp_fusion), kind=kCustom, calls=%fused_computation.5.clone | custom fusion | bytes 163840 | tf_op jit(solution)/shard_map/jit(_take)/gather | solution.py:26
  385.8 6.2 %bitcast_multiply_fusion = f32[2,8192]{0,1:T(8,128)S(1)} fusion(f32[8192,2]{1,0:T(8,128)} %gather_fusion.5, f32[8192]{0:T(1024)S(1)} %subtract_convert_fusion, pred[8192]{0:T(1024)(128)(4,1)S(1)} %compare_and_fusion), kind=kLoop, calls=%fused_computation.24 | loop fusion | flops 32768 | bytes 172032 | tf_op jit(solution)/shard_map/mul | solution.py:151
  392.0 1.9 fusion.152
  393.9 2.7 copy.359
  396.5 1.3 copy.360
  397.9 15.7 %collective-permute-start = (f32[2,128,32]{1,2,0:T(8,128)S(1)}, f32[2,128,32]{1,2,0:T(8,128)S(1)}, u32[]{:S(2)}, u32[]{:S(2)}) collective-permute-start(f32[2,128,32]{1,2,0:T(8,128)S(1)} %bitcast_select_fusion.3), channel_id=1, source_target_pairs={{0,64},{64,0},{128,192},{192,128},{256,320},{320,256},{384,448},{4... | collective-permute-start | bytes 98312 | tf_op jit(solution)/shard_map/ppermute | solution.py:12
  414.0 1.5 collective-permute-done
  417.7 13.2 %collective-permute-start.1 = (f32[2,128,32]{1,2,0:T(8,128)S(1)}, f32[2,128,32]{1,2,0:T(8,128)S(1)}, u32[]{:S(2)}, u32[]{:S(2)}) collective-permute-start(f32[2,128,32]{1,2,0:T(8,128)S(1)} %fusion.91), channel_id=1, source_target_pairs={{0,64},{64,0},{128,192},{192,128},{256,320},{320,256},{384,448},{4... | collective-permute-start | bytes 98312 | tf_op jit(solution)/shard_map/ppermute | solution.py:12
  430.9 1.9 collective-permute-done.1
  433.4 18.2 %collective-permute-start.2 = (f32[2,64,64]{2,1,0:T(8,128)S(1)}, f32[2,64,64]{2,1,0:T(8,128)S(1)}, u32[]{:S(2)}, u32[]{:S(2)}) collective-permute-start(f32[2,64,64]{2,1,0:T(8,128)S(1)} %broadcast_select_fusion.2), channel_id=1, source_target_pairs={{0,128},{64,192},{128,0},{192,64},{256,384},{320,448},{384,256},{4... | collective-permute-start | bytes 98312 | tf_op jit(solution)/shard_map/ppermute | solution.py:12
  451.6 6.3 %collective-permute-done.2 = f32[2,64,64]{2,1,0:T(8,128)S(1)} collective-permute-done((f32[2,64,64]{2,1,0:T(8,128)S(1)}, f32[2,64,64]{2,1,0:T(8,128)S(1)}, u32[]{:S(2)}, u32[]{:S(2)}) %collective-permute-start.2) | collective-permute-done | bytes 32800 | tf_op jit(solution)/shard_map/ppermute | solution.py:12
  459.8 18.4 %collective-permute-start.3 = (f32[2,64,64]{2,1,0:T(8,128)S(1)}, f32[2,64,64]{2,1,0:T(8,128)S(1)}, u32[]{:S(2)}, u32[]{:S(2)}) collective-permute-start(f32[2,64,64]{2,1,0:T(8,128)S(1)} %broadcast_select_fusion.1), channel_id=1, source_target_pairs={{0,128},{64,192},{128,0},{192,64},{256,384},{320,448},{384,256},{4... | collective-permute-start | bytes 98312 | tf_op jit(solution)/shard_map/ppermute | solution.py:12
  478.1 6.1 %collective-permute-done.3 = f32[2,64,64]{2,1,0:T(8,128)S(1)} collective-permute-done((f32[2,64,64]{2,1,0:T(8,128)S(1)}, f32[2,64,64]{2,1,0:T(8,128)S(1)}, u32[]{:S(2)}, u32[]{:S(2)}) %collective-permute-start.3) | collective-permute-done | bytes 32800 | tf_op jit(solution)/shard_map/ppermute | solution.py:12
  484.6 2.7 collective-permute-start.4
  487.3 3.2 collective-permute-done.4
  491.9 2.7 collective-permute-start.5
  494.5 3.1 collective-permute-done.5
  497.9 3.2 collective-permute-start.6
  501.1 4.4 collective-permute-done.6
  506.9 2.9 collective-permute-start.7
  509.9 4.4 collective-permute-done.7
  514.3 0.7 reshape_reshape.24
  (147 shorter events, 22.7 us)
Async XLA Ops:
  59.7 3.4 copy-start
  59.7 3.9 copy-start.3
  121.6 4.5 copy-start.4
  185.0 25.8 %copy-start.1 = (s32[10]{0:T(128)S(1)}, s32[10]{0:T(128)}, u32[]{:S(2)}) copy-start(s32[10]{0:T(128)} %param.15) | copy-start | bytes 124
  188.5 78.4 %all-to-all-start = ((f32[2,64,128]{2,0,1:T(2,128)}), f32[2,64,128]{2,0,1:T(2,128)S(1)}, u32[]{:S(2)}, u32[]{:S(2)}) async-start(f32[2,64,128]{2,0,1:T(2,128)} %copy.223), calls=%async_computation | async-start | bytes 131072 | tf_op jit(solution)/shard_map/all_to_all | solution.py:139
  393.9 19.7 %copy-start.2 = (f32[2,4,4]{2,1,0:T(4,128)S(1)}, f32[2,4,4]{2,1,0:T(4,128)}, u32[]{:S(2)}) copy-start(f32[2,4,4]{2,1,0:T(4,128)} %param.11) | copy-start | bytes 388
  397.9 17.6 %collective-permute-start = (f32[2,128,32]{1,2,0:T(8,128)S(1)}, f32[2,128,32]{1,2,0:T(8,128)S(1)}, u32[]{:S(2)}, u32[]{:S(2)}) collective-permute-start(f32[2,128,32]{1,2,0:T(8,128)S(1)} %bitcast_select_fusion.3), channel_id=1, source_target_pairs={{0,64},{64,0},{128,192},{192,128},{256,320},{320,256},{384,448},{4... | collective-permute-start | bytes 98312 | tf_op jit(solution)/shard_map/ppermute | solution.py:12
  417.7 15.0 %collective-permute-start.1 = (f32[2,128,32]{1,2,0:T(8,128)S(1)}, f32[2,128,32]{1,2,0:T(8,128)S(1)}, u32[]{:S(2)}, u32[]{:S(2)}) collective-permute-start(f32[2,128,32]{1,2,0:T(8,128)S(1)} %fusion.91), channel_id=1, source_target_pairs={{0,64},{64,0},{128,192},{192,128},{256,320},{320,256},{384,448},{4... | collective-permute-start | bytes 98312 | tf_op jit(solution)/shard_map/ppermute | solution.py:12
  433.4 24.6 %collective-permute-start.2 = (f32[2,64,64]{2,1,0:T(8,128)S(1)}, f32[2,64,64]{2,1,0:T(8,128)S(1)}, u32[]{:S(2)}, u32[]{:S(2)}) collective-permute-start(f32[2,64,64]{2,1,0:T(8,128)S(1)} %broadcast_select_fusion.2), channel_id=1, source_target_pairs={{0,128},{64,192},{128,0},{192,64},{256,384},{320,448},{384,256},{4... | collective-permute-start | bytes 98312 | tf_op jit(solution)/shard_map/ppermute | solution.py:12
  459.8 24.5 %collective-permute-start.3 = (f32[2,64,64]{2,1,0:T(8,128)S(1)}, f32[2,64,64]{2,1,0:T(8,128)S(1)}, u32[]{:S(2)}, u32[]{:S(2)}) collective-permute-start(f32[2,64,64]{2,1,0:T(8,128)S(1)} %broadcast_select_fusion.1), channel_id=1, source_target_pairs={{0,128},{64,192},{128,0},{192,64},{256,384},{320,448},{384,256},{4... | collective-permute-start | bytes 98312 | tf_op jit(solution)/shard_map/ppermute | solution.py:12
  484.6 5.9 %collective-permute-start.4 = (f32[2,32,128]{2,1,0:T(8,128)S(1)}, f32[2,32,128]{2,1,0:T(8,128)S(1)}, u32[]{:S(2)}, u32[]{:S(2)}) collective-permute-start(f32[2,32,128]{2,1,0:T(8,128)S(1)} %broadcast_select_fusion.4), channel_id=1, source_target_pairs={{0,256},{64,320},{128,384},{192,448},{256,0},{320,64},{384,128},{4... | collective-permute-start | bytes 98312 | tf_op jit(solution)/shard_map/ppermute | solution.py:12
  491.9 5.8 %collective-permute-start.5 = (f32[2,32,128]{2,1,0:T(8,128)S(1)}, f32[2,32,128]{2,1,0:T(8,128)S(1)}, u32[]{:S(2)}, u32[]{:S(2)}) collective-permute-start(f32[2,32,128]{2,1,0:T(8,128)S(1)} %broadcast_select_fusion.3), channel_id=1, source_target_pairs={{0,256},{64,320},{128,384},{192,448},{256,0},{320,64},{384,128},{4... | collective-permute-start | bytes 98312 | tf_op jit(solution)/shard_map/ppermute | solution.py:12
  497.9 7.6 %collective-permute-start.6 = (f32[2,16,256]{2,1,0:T(8,128)S(1)}, f32[2,16,256]{2,1,0:T(8,128)S(1)}, u32[]{:S(2)}, u32[]{:S(2)}) collective-permute-start(f32[2,16,256]{2,1,0:T(8,128)S(1)} %bitcast_select_fusion.1), channel_id=1, source_target_pairs={{0,512},{64,576},{128,640},{192,704},{256,768},{320,832},{384,896}... | collective-permute-start | bytes 98312 | tf_op jit(solution)/shard_map/ppermute | solution.py:12
  506.9 7.3 %collective-permute-start.7 = (f32[2,16,256]{2,1,0:T(8,128)S(1)}, f32[2,16,256]{2,1,0:T(8,128)S(1)}, u32[]{:S(2)}, u32[]{:S(2)}) collective-permute-start(f32[2,16,256]{2,1,0:T(8,128)S(1)} %fusion.92), channel_id=1, source_target_pairs={{0,512},{64,576},{128,640},{192,704},{256,768},{320,832},{384,896}... | collective-permute-start | bytes 98312 | tf_op jit(solution)/shard_map/ppermute | solution.py:12
where the time goes:
time: 524 us; the launch traced here: 515 us
  local copies, waits for them, and re-layouts  234 us (45%)
  other arithmetic  147 us (28%)
  starting transfers between devices  92.8 us (18%)
  waiting for transfers between devices  31 us (6%)
  matrix products  9.72 us (2%)
    gather x6, local copies, waits for them, and re-layouts, reorder(): return jnp.take(values, source_index(source, source.shape[0]), axis=1)  179 us
    ppermute x8, starting transfers between devices, swapped(): return lax.ppermute(value, axis, pairs)  76.8 us
    and x6, other arithmetic, reorder(): return jnp.take(values, source_index(source, source.shape[0]), axis=1)  49.2 us
    gather x6, other arithmetic  49.2 us
    select_n x5, other arithmetic, reorder(): return jnp.take(values, source_index(source, source.shape[0]), axis=1)  32.3 us
    ppermute x8, waiting for transfers between devices, swapped(): return lax.ppermute(value, axis, pairs)  31 us
    all_to_all x1, starting transfers between devices, per_device(): lax.all_to_all(shaped, 'dev', split_axis=1, concat_axis=1, tiled=True)  16 us
    slice x4, local copies, waits for them, and re-layouts, complex_gate(): values[1]  13.3 us
  transfers between devices with their start and end apart: 9, of which 8 were waited for; matrix products, arithmetic and copies ran while one was open for 12% of the time, Pallas kernels for 0%

commit v1 on v0

--- a/solution.py
+++ b/solution.py
@@ -23,7 +23,25 @@
 
 
 def reorder(values, source):
-    return jnp.take(values, source_index(source, source.shape[0]), axis=1)
+    bit_count = source.shape[0]
+    length = 2**bit_count
+    lane_bits = 7
+    lanes = 2**lane_bits
+    rows = length // lanes
+    picked = source_index(source, bit_count)
+    one_hot = (
+        lax.broadcasted_iota(jnp.int32, (lanes, length), 0) == (picked & lanes - 1)[None, :]
+    ).astype(jnp.float32)
+    spread = jnp.dot(
+        values.reshape(2 * rows, lanes),
+        one_hot,
+        precision=HIGHEST,
+        preferred_element_type=jnp.float32,
+    ).reshape(2, rows, length)
+    row_hit = lax.broadcasted_iota(jnp.int32, (rows, length), 0) == jnp.right_shift(
+        picked, lane_bits
+    )[None, :]
+    return jnp.sum(jnp.where(row_hit[None], spread, 0.0), axis=1)
 
 
 def complex_gate(values, matrix):
@@ -112,6 +130,31 @@
     outgoing = jnp.where(own_bit == 0, upper_half, lower_half)
     received = swapped(outgoing, "grp", bit_num)
     return rejoin(lower_half, upper_half, received, own_bit)
+
+
+def pair_exchange(values, place_bit, bit_num, matrix):
+    count_all = values.shape[1]
+    own_bit = jnp.right_shift(lax.axis_index("grp"), bit_num) & 1
+    received = swapped(values, "grp", bit_num)
+    shape = (2, count_all >> place_bit + 1, 2, 1 << place_bit)
+    own = values.reshape(shape)
+    other = received.reshape(shape)
+    same = jnp.where(own_bit == 0, matrix[:, 0::2, 0::2], matrix[:, 1::2, 1::2])
+    cross = jnp.where(own_bit == 0, matrix[:, 0::2, 1::2], matrix[:, 1::2, 0::2])
+    parts = []
+    for out_c in range(2):
+        real_part = 0.0
+        imag_part = 0.0
+        for in_c in range(2):
+            for coef, src in ((same, own), (cross, other)):
+                cr = coef[0, out_c, in_c]
+                ci = coef[1, out_c, in_c]
+                xr = src[0, :, in_c]
+                xi = src[1, :, in_c]
+                real_part = real_part + (cr * xr - ci * xi)
+                imag_part = imag_part + (cr * xi + ci * xr)
+        parts.append(jnp.stack([real_part, imag_part]))
+    return jnp.stack(parts, axis=2).reshape(2, count_all)
 
 
 def per_device(
@@ -150,10 +193,7 @@
     values = reorder(values, position_of(layout, layout_out[:local_bits]))
     values = values * spare_sign(length, spare_values)
     for bit_num in range(group_bits):
-        place_bit = local_bits - 2 * group_bits + bit_num
-        values = trade_group(values, place_bit, bit_num)
-        values = pair_apply(values, place_bit, local_bits - 1 - bit_num, pair_gate)
-        values = trade_group(values, place_bit, bit_num)
+        values = pair_exchange(values, local_bits - 1 - bit_num, bit_num, pair_gate)
     return values.reshape(amplitudes.shape)
 
 

time: 524 us -> 252 us (0.48); the launches traced: 515 us -> 250 us
  local copies, waits for them, and re-layouts: 234 us -> 20 us
  starting transfers between devices: 92.8 us -> 56.1 us
  other arithmetic: 147 us -> 128 us
  matrix products: 9.72 us -> 18.9 us
    gather x6 -> x0, local copies, waits for them, and re-layouts: 179 us -> none  [reorder(): return jnp.take(values, source_index(source, source.shape[0]), axis=1)]
    add x0 -> x12, other arithmetic: none -> 60.6 us  [the longest x8 40.2 us: pair_exchange(): real_part = real_part + (cr * xr - ci * xi)]
    gather x6 -> x0, other arithmetic: 49.2 us -> none
    ppermute x8 -> x4, starting transfers between devices: 76.8 us -> 40.1 us  [swapped(): return lax.ppermute(value, axis, pairs)]
    select_n x18 -> x6, other arithmetic: 32.4 us -> 0.05 us  [the longest x5 0.04 us: arrange(): new_layout = jnp.zeros((layout_len,), jnp.int32).at[target].set(layout)]
    slice x4, local copies, waits for them, and re-layouts: 13.3 us -> 0.21 us  [complex_gate(): values[1]]
    another operation x17 -> x5, local copies, waits for them, and re-layouts: 11.7 us -> 0.32 us  [the longest x2 0.16 us: pair_exchange(): own = values.reshape(shape)]
    dot_general x16 -> x6, matrix products: 5.89 us -> 15 us  [reorder(): jnp.dot(values.reshape(2 * rows, lanes), one_hot, precision=HIGHEST, pref...]
  transfers between devices with their start and end apart: 9 -> 5, of which waited for: 8 -> 4; matrix products, arithmetic and copies ran while one was open for 12% -> 20% of each run, Pallas kernels for 0% -> 0%
where the time goes in v1:
time: 252 us; the launch traced here: 250 us
  other arithmetic  128 us (51%)
  starting transfers between devices  56.1 us (22%)
  waiting for transfers between devices  26 us (10%)
  local copies, waits for them, and re-layouts  20 us (8%)
  matrix products  18.9 us (7%)
    and x6, other arithmetic, reorder(): picked & lanes - 1  49 us
    add x8, other arithmetic, pair_exchange(): real_part = real_part + (cr * xr - ci * xi)  40.2 us
    ppermute x4, starting transfers between devices, swapped(): return lax.ppermute(value, axis, pairs)  40.1 us
    ppermute x4, waiting for transfers between devices, swapped(): return lax.ppermute(value, axis, pairs)  26 us
    add x4, other arithmetic, pair_exchange(): imag_part = imag_part + (cr * xi + ci * xr)  20.3 us
    all_to_all x1, starting transfers between devices, per_device(): lax.all_to_all(shaped, 'dev', split_axis=1, concat_axis=1, tiled=True)  16 us
    dot_general x6, matrix products, reorder(): jnp.dot(values.reshape(2 * rows, lanes), one_hot, precision=HIGHEST, pref...  15 us
    convert_element_type x2, other arithmetic, spare_sign(): return (1 - 2 * (parity & 1)).astype(jnp.float32)  12.7 us
  transfers between devices with their start and end apart: 5, of which 4 were waited for; matrix products, arithmetic and copies ran while one was open for 20% of the time, Pallas kernels for 0%

profile of v1, /device:TPU:24, one launch (start us, length us, event | category | flops | bytes accessed | tf_op | source)
XLA Modules:
  0.0 249.5 jit_solution(17571898093272265473)
XLA Ops:
  0.0 0.8 slice_bitcast_fusion
  0.8 0.7 compare_reduce_fusion.4
  1.6 0.7 fusion.93
  2.5 0.6 scatter_custom_fusion.9
  3.1 0.7 fusion.150
  3.8 8.2 %broadcast_and_fusion.5 = (s32[8192]{0:T(1024)S(1)}, s32[8192]{0:T(1024)S(1)}) fusion(s32[]{:T(128)} %bitcast.100, s32[]{:T(128)} %bitcast.99, s32[]{:T(128)} %bitcast.98, s32[]{:T(128)} %bitcast.97, s32[]{:T(128)} %bitcast.96, s32[]{:T(128)} %bitcast.95, s32[]{:T(128)} %bitcast.94, s32[]{:T(128)} %bitcast.93, s32[]{:T(128)} %bitcast.92, s32[]{:T(128)} %bitcast.91, ...), kind=kLoop, calls=%fused_computation.171 | loop fusion | flops 434176 | bytes 65588 | tf_op jit(solution)/shard_map/and | solution.py:33
  12.4 2.4 select_reduce_fusion
  15.3 0.6 scatter_custom_fusion
  16.8 0.6 scatter_custom_fusion.8
  17.5 0.7 fusion.151
  18.2 8.2 %broadcast_and_fusion.4 = (s32[8192]{0:T(1024)S(1)}, s32[8192]{0:T(1024)S(1)}) fusion(s32[]{:T(128)} %bitcast.87, s32[]{:T(128)} %bitcast.86, s32[]{:T(128)} %bitcast.85, s32[]{:T(128)} %bitcast.84, s32[]{:T(128)} %bitcast.83, s32[]{:T(128)} %bitcast.82, s32[]{:T(128)} %bitcast.81, s32[]{:T(128)} %bitcast.80, s32[]{:T(128)} %bitcast.79, s32[]{:T(128)} %bitcast.78, ...), kind=kLoop, calls=%fused_computation.170 | loop fusion | flops 434176 | bytes 65588 | tf_op jit(solution)/shard_map/and | solution.py:33
  26.7 2.4 fusion.17
  29.6 0.6 scatter_custom_fusion.1
  31.2 0.6 scatter_custom_fusion.7
  31.8 0.7 fusion.152
  32.5 8.2 %broadcast_and_fusion.3 = (s32[8192]{0:T(1024)S(1)}, s32[8192]{0:T(1024)S(1)}) fusion(s32[]{:T(128)} %bitcast.74, s32[]{:T(128)} %bitcast.73, s32[]{:T(128)} %bitcast.72, s32[]{:T(128)} %bitcast.71, s32[]{:T(128)} %bitcast.70, s32[]{:T(128)} %bitcast.69, s32[]{:T(128)} %bitcast.68, s32[]{:T(128)} %bitcast.67, s32[]{:T(128)} %bitcast.66, s32[]{:T(128)} %bitcast.65, ...), kind=kLoop, calls=%fused_computation.169 | loop fusion | flops 434176 | bytes 65588 | tf_op jit(solution)/shard_map/and | solution.py:33
  41.0 3.0 %fusion.20 = f32[2,8192]{1,0:T(2,128)} fusion(s32[8192]{0:T(1024)S(1)} %get-tuple-element.215, pred[64,8192]{1,0:T(8,128)(4,1)S(1)} %iota_compare_fusion.9, f32[1,64,128]{2,1,0:T(8,128)S(1)} %fusion.36, f32[1,64,128]{2,1,0:T(8,128)S(1)} %fusion.37), kind=kOutput, calls=%fused_computation.41 | convolution fusion | flops 1613758464 | bytes 688128 | tf_op jit(solution)/shard_map/dot_general | solution.py:35
  44.1 16.0 %all-to-all-start = ((f32[2,64,128]{2,0,1:T(2,128)}), f32[2,64,128]{2,0,1:T(2,128)S(1)}, u32[]{:S(2)}, u32[]{:S(2)}) async-start(f32[2,64,128]{2,0,1:T(2,128)} %bitcast.118), calls=%async_computation | async-start | bytes 131072 | tf_op jit(solution)/shard_map/all_to_all | solution.py:182
  60.1 0.8 scatter_custom_fusion.2
  61.4 0.6 scatter_custom_fusion.3
  62.6 0.6 scatter_custom_fusion.6
  63.2 0.7 fusion.153
  63.9 8.2 %broadcast_and_fusion.2 = (s32[8192]{0:T(1024)S(1)}, s32[8192]{0:T(1024)S(1)}) fusion(s32[]{:T(128)} %bitcast.61, s32[]{:T(128)} %bitcast.60, s32[]{:T(128)} %bitcast.59, s32[]{:T(128)} %bitcast.58, s32[]{:T(128)} %bitcast.57, s32[]{:T(128)} %bitcast.56, s32[]{:T(128)} %bitcast.55, s32[]{:T(128)} %bitcast.54, s32[]{:T(128)} %bitcast.53, s32[]{:T(128)} %bitcast.52, ...), kind=kLoop, calls=%fused_computation.168 | loop fusion | flops 434176 | bytes 65588 | tf_op jit(solution)/shard_map/and | solution.py:33
  72.5 0.6 scatter_custom_fusion.4
  73.2 0.6 scatter_custom_fusion.5
  73.8 0.7 fusion.154
  74.5 8.2 %broadcast_and_fusion.1 = (s32[8192]{0:T(1024)S(1)}, s32[8192]{0:T(1024)S(1)}) fusion(s32[]{:T(128)} %bitcast.48, s32[]{:T(128)} %bitcast.47, s32[]{:T(128)} %bitcast.46, s32[]{:T(128)} %bitcast.45, s32[]{:T(128)} %bitcast.44, s32[]{:T(128)} %bitcast.43, s32[]{:T(128)} %bitcast.42, s32[]{:T(128)} %bitcast.41, s32[]{:T(128)} %bitcast.40, s32[]{:T(128)} %bitcast.39, ...), kind=kLoop, calls=%fused_computation.167 | loop fusion | flops 434176 | bytes 65588 | tf_op jit(solution)/shard_map/and | solution.py:33
  83.1 0.7 fusion.155
  83.8 8.2 %broadcast_and_fusion = (s32[8192]{0:T(1024)S(1)}, s32[8192]{0:T(1024)S(1)}) fusion(s32[]{:T(128)} %bitcast.35, s32[]{:T(128)} %bitcast.34, s32[]{:T(128)} %bitcast.33, s32[]{:T(128)} %bitcast.32, s32[]{:T(128)} %bitcast.31, s32[]{:T(128)} %bitcast.30, s32[]{:T(128)} %bitcast.29, s32[]{:T(128)} %bitcast.28, s32[]{:T(128)} %bitcast.27, s32[]{:T(128)} %bitcast.26, ...), kind=kLoop, calls=%fused_computation.166 | loop fusion | flops 434176 | bytes 65588 | tf_op jit(solution)/shard_map/and | solution.py:33
  92.3 0.7 fusion.149
  93.0 0.7 fusion.147
  93.6 0.7 fusion.148
  94.3 0.7 fusion.145
  95.0 0.7 fusion.146
  95.7 0.7 fusion.143
  96.3 0.7 fusion.144
  97.0 0.7 fusion.141
  97.6 6.3 %subtract_convert_fusion = f32[8192]{0:T(1024)S(1)} fusion(s32[]{:T(128)} %bitcast.143, s32[]{:T(128)} %bitcast.142, s32[]{:T(128)} %bitcast.141, s32[]{:T(128)} %bitcast.140, s32[]{:T(128)} %bitcast.139, s32[]{:T(128)} %bitcast.138, s32[]{:T(128)} %bitcast.137, s32[]{:T(128)} %bitcast.136, s32[]{:T(128)} %bitcast.135, s32[]{:T(128)} %bitcast.134), kind=kLoop, calls=%fused_computation.128 | loop fusion | flops 352256 | bytes 32808 | tf_op jit(solution)/shard_map/convert_element_type | solution.py:80
  103.9 0.7 fusion.142
  104.6 6.4 %subtract_convert_fusion.1 = f32[2,4096]{1,0:T(2,128)S(1)} fusion(s32[]{:T(128)} %bitcast.143, s32[]{:T(128)} %bitcast.142, s32[]{:T(128)} %bitcast.141, s32[]{:T(128)} %bitcast.140, s32[]{:T(128)} %bitcast.139, s32[]{:T(128)} %bitcast.138, s32[]{:T(128)} %bitcast.137, s32[]{:T(128)} %bitcast.136, s32[]{:T(128)} %bitcast.135, s32[]{:T(128)} %bitcast.134), kind=kLoop, calls=%fused_computation.130 | loop fusion | flops 368640 | bytes 32808 | tf_op jit(solution)/shard_map/convert_element_type | solution.py:80
  111.0 2.4 fusion.23
  114.4 2.4 fusion.26
  117.9 2.4 fusion.29
  120.4 15.9 %collective-permute-start = (f32[2,8192]{1,0:T(2,128)S(1)}, f32[2,8192]{1,0:T(2,128)S(1)}, u32[]{:S(2)}, u32[]{:S(2)}) collective-permute-start(f32[2,8192]{1,0:T(2,128)S(1)} %broadcast_multiply_fusion), channel_id=1, source_target_pairs={{0,64},{64,0},{128,192},{192,128},{256,320},{320,256},{384,448},{4... | collective-permute-start | bytes 196616 | tf_op jit(solution)/shard_map/ppermute | solution.py:12
  136.4 11.9 %collective-permute-done = f32[2,8192]{1,0:T(2,128)S(1)} collective-permute-done((f32[2,8192]{1,0:T(2,128)S(1)}, f32[2,8192]{1,0:T(2,128)S(1)}, u32[]{:S(2)}, u32[]{:S(2)}) %collective-permute-start) | collective-permute-done | bytes 65568 | tf_op jit(solution)/shard_map/ppermute | solution.py:12
  148.3 5.2 %subtract_add_fusion.1 = f32[1,1,1,4096]{3,2,1,0:T(1,128)S(1)} fusion(f32[]{:T(128)} %bitcast.150, f32[]{:T(128)} %bitcast.149, f32[]{:T(128)} %bitcast.148, f32[]{:T(128)} %bitcast.147, f32[]{:T(128)} %bitcast.146, f32[]{:T(128)} %bitcast.145, f32[]{:T(128)} %bitcast.144, f32[]{:T(128)} %bitcast.3, f32[2,1,2,4096]{3,2,1,0:T(2,128)S(1)} %reshape.3137, ...), kind=kLoop, calls=%fused_computation.165 | loop fusion | flops 61440 | bytes 147488 | tf_op jit(solution)/shard_map/add | solution.py:154
  153.5 5.2 %add_add_fusion.1 = f32[1,1,1,4096]{3,2,1,0:T(1,128)S(1)} fusion(f32[]{:T(128)} %bitcast.150, f32[]{:T(128)} %bitcast.149, f32[]{:T(128)} %bitcast.148, f32[]{:T(128)} %bitcast.147, f32[]{:T(128)} %bitcast.146, f32[]{:T(128)} %bitcast.145, f32[]{:T(128)} %bitcast.144, f32[]{:T(128)} %bitcast.3, f32[2,1,2,4096]{3,2,1,0:T(2,128)S(1)} %reshape.3137, ...), kind=kLoop, calls=%fused_computation.164 | loop fusion | flops 61440 | bytes 147488 | tf_op jit(solution)/shard_map/add | solution.py:155
  158.7 5.1 %subtract_add_fusion = f32[1,1,1,4096]{3,2,1,0:T(1,128)S(1)} fusion(f32[]{:T(128)} %bitcast.160, f32[]{:T(128)} %bitcast.159, f32[]{:T(128)} %bitcast.158, f32[]{:T(128)} %bitcast.157, f32[]{:T(128)} %bitcast.156, f32[]{:T(128)} %bitcast.155, f32[]{:T(128)} %bitcast.154, f32[]{:T(128)} %bitcast.153, f32[2,1,2,4096]{3,2,1,0:T(2,128)S(1)} %reshape.3137, ...), kind=kLoop, calls=%fused_computation.163 | loop fusion | flops 61440 | bytes 147488 | tf_op jit(solution)/shard_map/add | solution.py:154
  163.8 5.1 %add_add_fusion = f32[1,1,1,4096]{3,2,1,0:T(1,128)S(1)} fusion(f32[]{:T(128)} %bitcast.160, f32[]{:T(128)} %bitcast.159, f32[]{:T(128)} %bitcast.158, f32[]{:T(128)} %bitcast.157, f32[]{:T(128)} %bitcast.156, f32[]{:T(128)} %bitcast.155, f32[]{:T(128)} %bitcast.154, f32[]{:T(128)} %bitcast.153, f32[2,1,2,4096]{3,2,1,0:T(2,128)S(1)} %reshape.3137, ...), kind=kLoop, calls=%fused_computation.162 | loop fusion | flops 61440 | bytes 147488 | tf_op jit(solution)/shard_map/add | solution.py:155
  169.1 18.3 %collective-permute-start.1 = (f32[2,8192]{1,0:T(2,128)S(1)}, f32[2,8192]{1,0:T(2,128)S(1)}, u32[]{:S(2)}, u32[]{:S(2)}) collective-permute-start(f32[2,8192]{1,0:T(2,128)S(1)} %bitcast.428), channel_id=1, source_target_pairs={{0,128},{64,192},{128,0},{192,64},{256,384},{320,448},{384,256},{4... | collective-permute-start | bytes 196616 | tf_op jit(solution)/shard_map/ppermute | solution.py:12
  187.5 6.2 %collective-permute-done.1 = f32[2,8192]{1,0:T(2,128)S(1)} collective-permute-done((f32[2,8192]{1,0:T(2,128)S(1)}, f32[2,8192]{1,0:T(2,128)S(1)}, u32[]{:S(2)}, u32[]{:S(2)}) %collective-permute-start.1) | collective-permute-done | bytes 65568 | tf_op jit(solution)/shard_map/ppermute | solution.py:12
  193.9 5.0 %add_bitcast_fusion.11 = f32[1,2,2048]{2,1,0:T(2,128)S(1)} fusion(f32[]{:T(128)} %bitcast.175, f32[]{:T(128)} %bitcast.174, f32[]{:T(128)} %bitcast.173, f32[]{:T(128)} %bitcast.172, f32[]{:T(128)} %bitcast.171, f32[]{:T(128)} %bitcast.164, f32[]{:T(128)} %bitcast.163, f32[]{:T(128)} %bitcast.2, f32[2,2,2,2048]{3,1,2,0:T(2,128)S(1)} %maximum_maximum_fusion, ...), kind=kLoop, calls=%fused_computation.161 | loop fusion | flops 61440 | bytes 147488 | tf_op jit(solution)/shard_map/add | solution.py:154
  198.9 5.0 %add_bitcast_fusion.10 = f32[1,2,2048]{2,1,0:T(2,128)S(1)} fusion(f32[]{:T(128)} %bitcast.175, f32[]{:T(128)} %bitcast.174, f32[]{:T(128)} %bitcast.173, f32[]{:T(128)} %bitcast.172, f32[]{:T(128)} %bitcast.171, f32[]{:T(128)} %bitcast.164, f32[]{:T(128)} %bitcast.163, f32[]{:T(128)} %bitcast.2, f32[2,2,2,2048]{3,1,2,0:T(2,128)S(1)} %maximum_maximum_fusion, ...), kind=kLoop, calls=%fused_computation.160 | loop fusion | flops 61440 | bytes 147488 | tf_op jit(solution)/shard_map/add | solution.py:155
  203.9 5.0 %add_bitcast_fusion.9 = f32[1,2,2048]{2,1,0:T(2,128)S(1)} fusion(f32[]{:T(128)} %bitcast.186, f32[]{:T(128)} %bitcast.185, f32[]{:T(128)} %bitcast.184, f32[]{:T(128)} %bitcast.183, f32[]{:T(128)} %bitcast.182, f32[]{:T(128)} %bitcast.181, f32[]{:T(128)} %bitcast.180, f32[]{:T(128)} %bitcast.179, f32[2,2,2,2048]{3,1,2,0:T(2,128)S(1)} %maximum_maximum_fusion, ...), kind=kLoop, calls=%fused_computation.159 | loop fusion | flops 61440 | bytes 147488 | tf_op jit(solution)/shard_map/add | solution.py:154
  209.0 5.0 %add_bitcast_fusion.8 = f32[1,2,2048]{2,1,0:T(2,128)S(1)} fusion(f32[]{:T(128)} %bitcast.186, f32[]{:T(128)} %bitcast.185, f32[]{:T(128)} %bitcast.184, f32[]{:T(128)} %bitcast.183, f32[]{:T(128)} %bitcast.182, f32[]{:T(128)} %bitcast.181, f32[]{:T(128)} %bitcast.180, f32[]{:T(128)} %bitcast.179, f32[2,2,2,2048]{3,1,2,0:T(2,128)S(1)} %maximum_maximum_fusion, ...), kind=kLoop, calls=%fused_computation.158 | loop fusion | flops 61440 | bytes 147488 | tf_op jit(solution)/shard_map/add | solution.py:155
  214.3 2.7 %collective-permute-start.2 = (f32[2,8192]{1,0:T(2,128)S(1)}, f32[2,8192]{1,0:T(2,128)S(1)}, u32[]{:S(2)}, u32[]{:S(2)}) collective-permute-start(f32[2,8192]{1,0:T(2,128)S(1)} %reshape.3140), channel_id=1, source_target_pairs={{0,256},{64,320},{128,384},{192,448},{256,0},{320,64},{384,128},{4... | collective-permute-start | bytes 196616 | tf_op jit(solution)/shard_map/ppermute | solution.py:12
  217.0 3.4 %collective-permute-done.2 = f32[2,8192]{1,0:T(2,128)S(1)} collective-permute-done((f32[2,8192]{1,0:T(2,128)S(1)}, f32[2,8192]{1,0:T(2,128)S(1)}, u32[]{:S(2)}, u32[]{:S(2)}) %collective-permute-start.2) | collective-permute-done | bytes 65568 | tf_op jit(solution)/shard_map/ppermute | solution.py:12
  220.6 4.9 %add_bitcast_fusion.7 = (f32[1,4,1024]{2,1,0:T(4,128)S(1)}, f32[1,4,1024]{2,1,0:T(4,128)S(1)}) fusion(f32[1,4,1,1024]{3,2,1,0:T(1,128)S(1)} %get-tuple-element.28, f32[1,4,1,1024]{3,2,1,0:T(1,128)S(1)} %get-tuple-element.26, f32[1,4,1,1024]{3,2,1,0:T(1,128)S(1)} %get-tuple-element.24, f32[1,4,1,1024]{3,2,1,0:T(1,128)S(1)} %get-tuple-element.22, ...), kind=kLoop, calls=%fused_computation.157 | loop fusion | flops 122880 | bytes 163872 | tf_op jit(solution)/shard_map/add | solution.py:154
  225.6 5.0 %add_bitcast_fusion.5 = (f32[1,4,1024]{2,1,0:T(4,128)S(1)}, f32[1,4,1024]{2,1,0:T(4,128)S(1)}) fusion(f32[1,4,1,1024]{3,2,1,0:T(1,128)S(1)} %get-tuple-element.28, f32[1,4,1,1024]{3,2,1,0:T(1,128)S(1)} %get-tuple-element.26, f32[1,4,1,1024]{3,2,1,0:T(1,128)S(1)} %get-tuple-element.24, f32[1,4,1,1024]{3,2,1,0:T(1,128)S(1)} %get-tuple-element.22, ...), kind=kLoop, calls=%fused_computation.155 | loop fusion | flops 122880 | bytes 163872 | tf_op jit(solution)/shard_map/add | solution.py:154
  230.9 3.1 %collective-permute-start.3 = (f32[2,8192]{1,0:T(2,128)S(1)}, f32[2,8192]{1,0:T(2,128)S(1)}, u32[]{:S(2)}, u32[]{:S(2)}) collective-permute-start(f32[2,8192]{1,0:T(2,128)S(1)} %reshape.3142), channel_id=1, source_target_pairs={{0,512},{64,576},{128,640},{192,704},{256,768},{320,832},{384,896}... | collective-permute-start | bytes 196616 | tf_op jit(solution)/shard_map/ppermute | solution.py:12
  234.1 4.4 %collective-permute-done.3 = f32[2,8192]{1,0:T(2,128)S(1)} collective-permute-done((f32[2,8192]{1,0:T(2,128)S(1)}, f32[2,8192]{1,0:T(2,128)S(1)}, u32[]{:S(2)}, u32[]{:S(2)}) %collective-permute-start.3) | collective-permute-done | bytes 65568 | tf_op jit(solution)/shard_map/ppermute | solution.py:12
  238.7 5.0 %add_bitcast_fusion.3 = (f32[1,8,512]{2,1,0:T(8,128)S(1)}, f32[1,8,512]{2,1,0:T(8,128)S(1)}) fusion(f32[1,8,1,512]{3,2,1,0:T(1,128)S(1)} %get-tuple-element.20, f32[1,8,1,512]{3,2,1,0:T(1,128)S(1)} %get-tuple-element.18, f32[1,8,1,512]{3,2,1,0:T(1,128)S(1)} %get-tuple-element.16, f32[1,8,1,512]{3,2,1,0:T(1,128)S(1)} %get-tuple-element.14, ...), kind=kLoop, calls=%fused_computation.153 | loop fusion | flops 122880 | bytes 163872 | tf_op jit(solution)/shard_map/add | solution.py:154
  243.7 5.0 %add_bitcast_fusion.1 = (f32[1,8,512]{2,1,0:T(8,128)S(1)}, f32[1,8,512]{2,1,0:T(8,128)S(1)}) fusion(f32[1,8,1,512]{3,2,1,0:T(1,128)S(1)} %get-tuple-element.20, f32[1,8,1,512]{3,2,1,0:T(1,128)S(1)} %get-tuple-element.18, f32[1,8,1,512]{3,2,1,0:T(1,128)S(1)} %get-tuple-element.16, f32[1,8,1,512]{3,2,1,0:T(1,128)S(1)} %get-tuple-element.14, ...), kind=kLoop, calls=%fused_computation.151 | loop fusion | flops 122880 | bytes 163872 | tf_op jit(solution)/shard_map/add | solution.py:154
  248.8 0.7 reshape_reshape.22
  (109 shorter events, 9.8 us)
Async XLA Ops:
  0.0 12.3 %copy-start = (f32[2,1,1,8192]{3,2,1,0:T(1,128)S(1)}, f32[2,1,1,8192]{3,2,1,0:T(1,128)}, u32[]{:S(2)}) copy-start(f32[2,1,1,8192]{3,2,1,0:T(1,128)} %param.7) | copy-start | bytes 196612
  12.3 2.5 %copy-start.1 = (f32[4,2,128,128]{3,2,1,0:T(8,128)S(1)}, f32[4,2,128,128]{3,2,1,0:T(8,128)}, u32[]{:S(2)}) copy-start(f32[4,2,128,128]{3,2,1,0:T(8,128)} %param.8) | copy-start | bytes 1572868
  12.3 3.0 %copy-start.4 = (s32[23]{0:T(128)S(1)}, s32[23]{0:T(128)}, u32[]{:S(2)}) copy-start(s32[23]{0:T(128)} %param.10) | copy-start | bytes 280
  26.6 3.6 %copy-start.5 = (s32[23]{0:T(128)S(1)}, s32[23]{0:T(128)}, u32[]{:S(2)}) copy-start(s32[23]{0:T(128)} %param.11) | copy-start | bytes 280
  41.0 21.2 %copy-start.3 = (f32[2,4,4]{2,1,0:T(4,128)S(1)}, f32[2,4,4]{2,1,0:T(4,128)}, u32[]{:S(2)}) copy-start(f32[2,4,4]{2,1,0:T(4,128)} %param.9) | copy-start | bytes 388
  44.1 66.9 %all-to-all-start = ((f32[2,64,128]{2,0,1:T(2,128)}), f32[2,64,128]{2,0,1:T(2,128)S(1)}, u32[]{:S(2)}, u32[]{:S(2)}) async-start(f32[2,64,128]{2,0,1:T(2,128)} %bitcast.118), calls=%async_computation | async-start | bytes 131072 | tf_op jit(solution)/shard_map/all_to_all | solution.py:182
  82.6 9.6 %copy-start.2 = (s32[10]{0:T(128)S(1)}, s32[10]{0:T(128)}, u32[]{:S(2)}) copy-start(s32[10]{0:T(128)} %param.13) | copy-start | bytes 124
  120.4 27.9 %collective-permute-start = (f32[2,8192]{1,0:T(2,128)S(1)}, f32[2,8192]{1,0:T(2,128)S(1)}, u32[]{:S(2)}, u32[]{:S(2)}) collective-permute-start(f32[2,8192]{1,0:T(2,128)S(1)} %broadcast_multiply_fusion), channel_id=1, source_target_pairs={{0,64},{64,0},{128,192},{192,128},{256,320},{320,256},{384,448},{4... | collective-permute-start | bytes 196616 | tf_op jit(solution)/shard_map/ppermute | solution.py:12
  169.1 24.6 %collective-permute-start.1 = (f32[2,8192]{1,0:T(2,128)S(1)}, f32[2,8192]{1,0:T(2,128)S(1)}, u32[]{:S(2)}, u32[]{:S(2)}) collective-permute-start(f32[2,8192]{1,0:T(2,128)S(1)} %bitcast.428), channel_id=1, source_target_pairs={{0,128},{64,192},{128,0},{192,64},{256,384},{320,448},{384,256},{4... | collective-permute-start | bytes 196616 | tf_op jit(solution)/shard_map/ppermute | solution.py:12
  214.3 6.2 %collective-permute-start.2 = (f32[2,8192]{1,0:T(2,128)S(1)}, f32[2,8192]{1,0:T(2,128)S(1)}, u32[]{:S(2)}, u32[]{:S(2)}) collective-permute-start(f32[2,8192]{1,0:T(2,128)S(1)} %reshape.3140), channel_id=1, source_target_pairs={{0,256},{64,320},{128,384},{192,448},{256,0},{320,64},{384,128},{4... | collective-permute-start | bytes 196616 | tf_op jit(solution)/shard_map/ppermute | solution.py:12
  230.9 7.7 %collective-permute-start.3 = (f32[2,8192]{1,0:T(2,128)S(1)}, f32[2,8192]{1,0:T(2,128)S(1)}, u32[]{:S(2)}, u32[]{:S(2)}) collective-permute-start(f32[2,8192]{1,0:T(2,128)S(1)} %reshape.3142), channel_id=1, source_target_pairs={{0,512},{64,576},{128,640},{192,704},{256,768},{320,832},{384,896}... | collective-permute-start | bytes 196616 | tf_op jit(solution)/shard_map/ppermute | solution.py:12

commit v2 on v1

--- a/solution.py
+++ b/solution.py
@@ -73,11 +73,24 @@
 
 
 def spare_sign(count_all, spare_values):
-    position = jnp.arange(count_all, dtype=jnp.int32)
-    parity = jnp.zeros((count_all,), jnp.int32)
+    lane_bits = 7
+    lanes = 2**lane_bits
+    rows = count_all // lanes
+    lane_pos = jnp.arange(lanes, dtype=jnp.int32)
+    row_pos = jnp.arange(rows, dtype=jnp.int32)
+    lane_parity = jnp.zeros((lanes,), jnp.int32)
+    row_parity = jnp.zeros((rows,), jnp.int32)
     for place_bit in range(spare_values.shape[0]):
-        parity = parity + spare_values[place_bit] * (jnp.right_shift(position, place_bit) & 1)
-    return (1 - 2 * (parity & 1)).astype(jnp.float32)
+        if place_bit < lane_bits:
+            lane_parity = lane_parity + spare_values[place_bit] * (
+                jnp.right_shift(lane_pos, place_bit) & 1
+            )
+        else:
+            row_parity = row_parity + spare_values[place_bit] * (
+                jnp.right_shift(row_pos, place_bit - lane_bits) & 1
+            )
+    parity = row_parity[:, None] + lane_parity[None, :]
+    return (1 - 2 * (parity & 1)).astype(jnp.float32).reshape(count_all)
 
 
 def position_of(layout, wanted):
@@ -155,6 +168,52 @@
                 imag_part = imag_part + (cr * xi + ci * xr)
         parts.append(jnp.stack([real_part, imag_part]))
     return jnp.stack(parts, axis=2).reshape(2, count_all)
+
+
+def pair_operator(matrix, group_bits):
+    size = 2 ** (2 * group_bits)
+    place = jnp.arange(size, dtype=jnp.int32)
+    states = jnp.arange(4, dtype=jnp.int32)
+    real_part = None
+    imag_part = None
+    for bit_num in range(group_bits):
+        pair_state = (jnp.right_shift(place, bit_num) & 1) + 2 * (
+            jnp.right_shift(place, 2 * group_bits - 1 - bit_num) & 1
+        )
+        pick = (pair_state[:, None] == states[None, :]).astype(jnp.float32)
+        factor_re = jnp.dot(
+            jnp.dot(pick, matrix[0], precision=HIGHEST), pick.T, precision=HIGHEST
+        )
+        factor_im = jnp.dot(
+            jnp.dot(pick, matrix[1], precision=HIGHEST), pick.T, precision=HIGHEST
+        )
+        if real_part is None:
+            real_part, imag_part = factor_re, factor_im
+        else:
+            real_part, imag_part = (
+                real_part * factor_re - imag_part * factor_im,
+                real_part * factor_im + imag_part * factor_re,
+            )
+    return (real_part, imag_part)
+
+
+def group_gates(values, local_bits, group_bits, matrix):
+    length = values.shape[1]
+    groups = 2**group_bits
+    low = local_bits - 2 * group_bits
+    shaped = values.reshape(2, groups, groups, 2**low)
+    shaped = lax.all_to_all(shaped, "grp", split_axis=2, concat_axis=2, tiled=True)
+    real_op, imag_op = pair_operator(matrix, group_bits)
+    block = shaped.reshape(2, groups * groups, 2**low)
+    real_part = jnp.dot(
+        real_op, block[0], precision=HIGHEST, preferred_element_type=jnp.float32
+    ) - jnp.dot(imag_op, block[1], precision=HIGHEST, preferred_element_type=jnp.float32)
+    imag_part = jnp.dot(
+        real_op, block[1], precision=HIGHEST, preferred_element_type=jnp.float32
+    ) + jnp.dot(imag_op, block[0], precision=HIGHEST, preferred_element_type=jnp.float32)
+    shaped = jnp.stack([real_part, imag_part]).reshape(2, groups, groups, 2**low)
+    shaped = lax.all_to_all(shaped, "grp", split_axis=2, concat_axis=2, tiled=True)
+    return shaped.reshape(2, length)
 
 
 def per_device(
@@ -192,8 +251,7 @@
         ).reshape(2, length)
     values = reorder(values, position_of(layout, layout_out[:local_bits]))
     values = values * spare_sign(length, spare_values)
-    for bit_num in range(group_bits):
-        values = pair_exchange(values, local_bits - 1 - bit_num, bit_num, pair_gate)
+    values = group_gates(values, local_bits, group_bits, pair_gate)
     return values.reshape(amplitudes.shape)
 
 

time: 252 us -> 202 us (0.80)
  other arithmetic: 128 us -> 63.1 us
  blocking collectives: 0 us -> 29 us
  starting transfers between devices: 56.1 us -> 39.7 us
  matrix products: 18.9 us -> 25.3 us
  local copies, waits for them, and re-layouts: 20 us -> 15.8 us
    add x12 -> x6, other arithmetic: 60.6 us -> 6.31 us  [the longest x1 4.29 us: spare_sign(): lane_parity + spare_values[place_bit] * (jnp.right_shift(lane_pos, place_...]
    ppermute x4 -> x0, starting transfers between devices: 40.1 us -> none  [swapped(): return lax.ppermute(value, axis, pairs)]
    all_to_all x0 -> x1, blocking collectives: none -> 29 us  [group_gates(): lax.all_to_all(shaped, 'grp', split_axis=2, concat_axis=2, tiled=True)]
    ppermute x4 -> x0, waiting for transfers between devices: 26 us -> none  [swapped(): return lax.ppermute(value, axis, pairs)]
    all_to_all x0 -> x1, waiting for transfers between devices: none -> 24.7 us  [group_gates(): lax.all_to_all(shaped, 'grp', split_axis=2, concat_axis=2, tiled=True)]
    all_to_all x0 -> x1, starting transfers between devices: none -> 23.7 us  [group_gates(): lax.all_to_all(shaped, 'grp', split_axis=2, concat_axis=2, tiled=True)]
    convert_element_type x2 -> x1, other arithmetic: 12.7 us -> 0.1 us  [spare_sign(): return (1 - 2 * (parity & 1)).astype(jnp.float32).reshape(count_all)]
    dot_general x0 -> x20, matrix products: none -> 6.43 us  [the longest x4 1.53 us: pair_operator(): jnp.dot(jnp.dot(pick, matrix[1], precision=HIGHEST), pick.T, precision=HI...]
  transfers between devices with their start and end apart: 5 -> 2, of which waited for: 4 -> 1; matrix products, arithmetic and copies ran while one was open for 20% -> 23% of each run, Pallas kernels for 0% -> 0%
where the time goes in v2:
time: 202 us; the launch traced here: 198 us
  other arithmetic  63.1 us (31%)
  starting transfers between devices  39.7 us (20%)
  blocking collectives  29 us (14%)
  matrix products  25.3 us (13%)
  waiting for transfers between devices  24.7 us (12%)
  local copies, waits for them, and re-layouts  15.8 us (8%)
    and x6, other arithmetic, reorder(): picked & lanes - 1  49 us
    all_to_all x1, blocking collectives, group_gates(): lax.all_to_all(shaped, 'grp', split_axis=2, concat_axis=2, tiled=True)  29 us
    all_to_all x1, waiting for transfers between devices, group_gates(): lax.all_to_all(shaped, 'grp', split_axis=2, concat_axis=2, tiled=True)  24.7 us
    all_to_all x1, starting transfers between devices, group_gates(): lax.all_to_all(shaped, 'grp', split_axis=2, concat_axis=2, tiled=True)  23.7 us
    all_to_all x1, starting transfers between devices, per_device(): lax.all_to_all(shaped, 'dev', split_axis=1, concat_axis=1, tiled=True)  16 us
    dot_general x6, matrix products, reorder(): jnp.dot(values.reshape(2 * rows, lanes), one_hot, precision=HIGHEST, pref...  15 us
    add x1, other arithmetic, spare_sign(): lane_parity + spare_values[place_bit] * (jnp.right_shift(lane_pos, place_...  4.29 us
    slice x6, local copies, waits for them, and re-layouts, source_index(): bit_order[place_bit]  4.2 us
  transfers between devices with their start and end apart: 2, of which 1 were waited for; matrix products, arithmetic and copies ran while one was open for 23% of the time, Pallas kernels for 0%

profile of v2, /device:TPU:24, one launch (start us, length us, event | category | flops | bytes accessed | tf_op | source)
XLA Modules:
  0.0 198.3 jit_solution(4896017825038719935)
XLA Ops:
  0.0 0.8 slice_bitcast_fusion
  0.8 0.7 compare_reduce_fusion.4
  1.6 0.7 fusion.125
  2.5 0.6 scatter_custom_fusion.9
  3.1 0.7 fusion.202
  3.8 8.2 %broadcast_and_fusion.5 = (s32[8192]{0:T(1024)S(1)}, s32[8192]{0:T(1024)S(1)}) fusion(s32[]{:T(128)} %bitcast.98, s32[]{:T(128)} %bitcast.97, s32[]{:T(128)} %bitcast.96, s32[]{:T(128)} %bitcast.95, s32[]{:T(128)} %bitcast.94, s32[]{:T(128)} %bitcast.93, s32[]{:T(128)} %bitcast.92, s32[]{:T(128)} %bitcast.91, s32[]{:T(128)} %bitcast.90, s32[]{:T(128)} %bitcast.89, ...), kind=kLoop, calls=%fused_computation.185 | loop fusion | flops 434176 | bytes 65588 | tf_op jit(solution)/shard_map/and | solution.py:33
  12.0 0.3 iota_compare_fusion.7
  12.4 2.4 %select_reduce_fusion = f32[2,8192]{1,0:T(2,128)S(1)} fusion(pred[64,8192]{1,0:T(8,128)(4,1)S(1)} %iota_compare_fusion.7, f32[128,128]{1,0:T(8,128)S(1)} %bitcast.336, s32[8192]{0:T(1024)S(1)} %get-tuple-element.123), kind=kOutput, calls=%fused_computation.20 | convolution fusion | flops 1613742080 | bytes 688128 | tf_op jit(solution)/shard_map/dot_general | solution.py:35
  15.3 0.6 scatter_custom_fusion
  16.8 0.6 scatter_custom_fusion.8
  17.5 0.7 fusion.203
  18.2 8.2 %broadcast_and_fusion.4 = (s32[8192]{0:T(1024)S(1)}, s32[8192]{0:T(1024)S(1)}) fusion(s32[]{:T(128)} %bitcast.85, s32[]{:T(128)} %bitcast.84, s32[]{:T(128)} %bitcast.83, s32[]{:T(128)} %bitcast.82, s32[]{:T(128)} %bitcast.81, s32[]{:T(128)} %bitcast.80, s32[]{:T(128)} %bitcast.79, s32[]{:T(128)} %bitcast.78, s32[]{:T(128)} %bitcast.77, s32[]{:T(128)} %bitcast.76, ...), kind=kLoop, calls=%fused_computation.184 | loop fusion | flops 434176 | bytes 65588 | tf_op jit(solution)/shard_map/and | solution.py:33
  26.4 0.3 iota_compare_fusion.8
  26.7 2.4 %fusion.17 = f32[2,8192]{1,0:T(2,128)S(1)} fusion(s32[8192]{0:T(1024)S(1)} %get-tuple-element.121, pred[64,8192]{1,0:T(8,128)(4,1)S(1)} %iota_compare_fusion.8, f32[1,64,128]{2,1,0:T(8,128)S(1)} %fusion.38, f32[1,64,128]{2,1,0:T(8,128)S(1)} %fusion.39), kind=kOutput, calls=%fused_computation.40 | convolution fusion | flops 1613758464 | bytes 688128 | tf_op jit(solution)/shard_map/dot_general | solution.py:35
  29.6 0.6 scatter_custom_fusion.1
  31.2 0.6 scatter_custom_fusion.7
  31.8 0.7 fusion.204
  32.5 8.2 %broadcast_and_fusion.3 = (s32[8192]{0:T(1024)S(1)}, s32[8192]{0:T(1024)S(1)}) fusion(s32[]{:T(128)} %bitcast.72, s32[]{:T(128)} %bitcast.71, s32[]{:T(128)} %bitcast.70, s32[]{:T(128)} %bitcast.69, s32[]{:T(128)} %bitcast.68, s32[]{:T(128)} %bitcast.67, s32[]{:T(128)} %bitcast.66, s32[]{:T(128)} %bitcast.65, s32[]{:T(128)} %bitcast.64, s32[]{:T(128)} %bitcast.63, ...), kind=kLoop, calls=%fused_computation.183 | loop fusion | flops 434176 | bytes 65588 | tf_op jit(solution)/shard_map/and | solution.py:33
  40.7 0.3 iota_compare_fusion.9
  41.0 3.0 %fusion.20 = f32[2,8192]{1,0:T(2,128)} fusion(s32[8192]{0:T(1024)S(1)} %get-tuple-element.119, pred[64,8192]{1,0:T(8,128)(4,1)S(1)} %iota_compare_fusion.9, f32[1,64,128]{2,1,0:T(8,128)S(1)} %fusion.36, f32[1,64,128]{2,1,0:T(8,128)S(1)} %fusion.37), kind=kOutput, calls=%fused_computation.41 | convolution fusion | flops 1613758464 | bytes 688128 | tf_op jit(solution)/shard_map/dot_general | solution.py:35
  44.1 16.0 %all-to-all-start = ((f32[2,64,128]{2,0,1:T(2,128)}), f32[2,64,128]{2,0,1:T(2,128)S(1)}, u32[]{:S(2)}, u32[]{:S(2)}) async-start(f32[2,64,128]{2,0,1:T(2,128)} %bitcast.116), calls=%async_computation | async-start | bytes 131072 | tf_op jit(solution)/shard_map/all_to_all | solution.py:241
  60.1 0.6 scatter_custom_fusion.2
  61.2 0.6 scatter_custom_fusion.3
  62.2 0.3 fusion.51
  62.5 0.3 fusion.55
  62.8 0.3 fusion.53
  63.6 0.7 scatter_custom_fusion.6
  64.3 0.7 fusion.205
  65.0 8.2 %broadcast_and_fusion.2 = (s32[8192]{0:T(1024)S(1)}, s32[8192]{0:T(1024)S(1)}) fusion(s32[]{:T(128)} %bitcast.59, s32[]{:T(128)} %bitcast.58, s32[]{:T(128)} %bitcast.57, s32[]{:T(128)} %bitcast.56, s32[]{:T(128)} %bitcast.55, s32[]{:T(128)} %bitcast.54, s32[]{:T(128)} %bitcast.53, s32[]{:T(128)} %bitcast.52, s32[]{:T(128)} %bitcast.51, s32[]{:T(128)} %bitcast.50, ...), kind=kLoop, calls=%fused_computation.182 | loop fusion | flops 434176 | bytes 65588 | tf_op jit(solution)/shard_map/and | solution.py:33
  73.2 0.3 iota_compare_fusion.10
  73.6 0.6 scatter_custom_fusion.4
  74.3 0.8 scatter_custom_fusion.5
  75.1 0.7 fusion.206
  75.8 8.2 %broadcast_and_fusion.1 = (s32[8192]{0:T(1024)S(1)}, s32[8192]{0:T(1024)S(1)}) fusion(s32[]{:T(128)} %bitcast.46, s32[]{:T(128)} %bitcast.45, s32[]{:T(128)} %bitcast.44, s32[]{:T(128)} %bitcast.43, s32[]{:T(128)} %bitcast.42, s32[]{:T(128)} %bitcast.41, s32[]{:T(128)} %bitcast.40, s32[]{:T(128)} %bitcast.39, s32[]{:T(128)} %bitcast.38, s32[]{:T(128)} %bitcast.37, ...), kind=kLoop, calls=%fused_computation.181 | loop fusion | flops 434176 | bytes 65588 | tf_op jit(solution)/shard_map/and | solution.py:33
  83.9 0.3 iota_compare_fusion.11
  84.4 0.7 fusion.207
  85.1 8.2 %broadcast_and_fusion = (s32[8192]{0:T(1024)S(1)}, s32[8192]{0:T(1024)S(1)}) fusion(s32[]{:T(128)} %bitcast.33, s32[]{:T(128)} %bitcast.32, s32[]{:T(128)} %bitcast.31, s32[]{:T(128)} %bitcast.30, s32[]{:T(128)} %bitcast.29, s32[]{:T(128)} %bitcast.28, s32[]{:T(128)} %bitcast.27, s32[]{:T(128)} %bitcast.26, s32[]{:T(128)} %bitcast.25, s32[]{:T(128)} %bitcast.24, ...), kind=kLoop, calls=%fused_computation.180 | loop fusion | flops 434176 | bytes 65588 | tf_op jit(solution)/shard_map/and | solution.py:33
  93.3 1.1 iota_compare_fusion.12
  94.3 0.7 fusion.201
  95.0 1.9 multiply_add_fusion.4
  97.1 0.4 fusion.48
  97.4 0.4 fusion.50
  97.8 0.4 fusion.54
  98.4 0.4 fusion.40
  98.8 0.4 fusion.44
  99.2 4.3 %multiply_add_fusion.3 = s32[4,32]{1,0:T(4,128)S(1)} fusion(s32[]{:T(128)} %bitcast.142, s32[]{:T(128)} %bitcast.141, s32[]{:T(128)} %bitcast.140, s32[]{:T(128)} %bitcast.139, s32[]{:T(128)} %bitcast.138, s32[]{:T(128)} %bitcast.137, s32[]{:T(128)} %bitcast.136), kind=kLoop, calls=%fused_computation.221 | loop fusion | flops 3712 | bytes 540 | tf_op jit(solution)/shard_map/add | solution.py:85
  103.8 0.4 fusion.46
  104.2 0.4 multiply_subtract_fusion.2
  104.6 2.4 %fusion.23 = f32[2,8192]{1,0:T(2,128)S(1)} fusion(s32[8192]{0:T(1024)S(1)} %get-tuple-element.117, pred[64,8192]{1,0:T(8,128)(4,1)S(1)} %iota_compare_fusion.10, f32[2,64,128]{2,0,1:T(2,128)S(1)} %all-to-all-done), kind=kOutput, calls=%fused_computation.42 | convolution fusion | flops 1613742080 | bytes 688128 | tf_op jit(solution)/shard_map/dot_general | solution.py:35
  108.1 2.4 %fusion.26 = f32[2,8192]{1,0:T(2,128)S(1)} fusion(s32[8192]{0:T(1024)S(1)} %get-tuple-element.115, pred[64,8192]{1,0:T(8,128)(4,1)S(1)} %iota_compare_fusion.11, f32[1,64,128]{2,1,0:T(8,128)S(1)} %fusion.34, f32[1,64,128]{2,1,0:T(8,128)S(1)} %fusion.35), kind=kOutput, calls=%fused_computation.43 | convolution fusion | flops 1613758464 | bytes 688128 | tf_op jit(solution)/shard_map/dot_general | solution.py:35
  111.5 2.4 %fusion.29 = f32[2,8192]{1,0:T(2,128)S(1)} fusion(s32[8192]{0:T(1024)S(1)} %get-tuple-element.113, pred[64,8192]{1,0:T(8,128)(4,1)S(1)} %copy-done.2, f32[1,64,128]{2,1,0:T(8,128)S(1)} %fusion.32, f32[1,64,128]{2,1,0:T(8,128)S(1)} %fusion.33), kind=kOutput, calls=%fused_computation.44 | convolution fusion | flops 1613758464 | bytes 688128 | tf_op jit(solution)/shard_map/dot_general | solution.py:35
  114.2 0.8 reshape.840
  115.0 23.7 %all-to-all-start.1 = ((f32[16,1,1024]{2,1,0:T(1,128)}), f32[16,1,1024]{2,1,0:T(1,128)S(1)}, u32[]{:S(2)}, u32[]{:S(2)}) async-start(f32[16,1,1024]{2,1,0:T(1,128)} %reshape.840), calls=%async_computation.1 | async-start | bytes 131072 | tf_op jit(solution)/shard_map/all_to_all | solution.py:205
  138.7 0.4 multiply_add_fusion
  139.2 24.7 %all-to-all-done.1 = f32[16,1,1024]{2,1,0:T(1,128)S(1)} async-done(((f32[16,1,1024]{2,1,0:T(1,128)}), f32[16,1,1024]{2,1,0:T(1,128)S(1)}, u32[]{:S(2)}, u32[]{:S(2)}) %all-to-all-start.1) | async-done | bytes 65568 | tf_op jit(solution)/shard_map/all_to_all | solution.py:205
  163.9 0.5 broadcast.2590
  164.4 0.8 reduce
  165.5 0.3 fusion.208
  165.8 0.4 fusion.209
  166.2 0.4 convolution_subtract_fusion.4
  166.7 0.4 convolution_add_fusion.4
  167.4 29.0 %all_to_all.15 = f32[16,1,1024]{2,1,0:T(1,128)S(1)} all-to-all(f32[16,1,1024]{2,1,0:T(1,128)S(1)} %reshape.842), channel_id=1, replica_groups=mesh['grp'=16,'dev'=64] {'grp'}, dimensions={0} | all-to-all | bytes 131072 | tf_op jit(solution)/shard_map/all_to_all | solution.py:215
  196.4 0.8 reduce.1
  197.5 0.8 reshape_reshape.6
  (95 shorter events, 8.9 us)
Async XLA Ops:
  0.0 12.3 %copy-start = (f32[2,1,1,8192]{3,2,1,0:T(1,128)S(1)}, f32[2,1,1,8192]{3,2,1,0:T(1,128)}, u32[]{:S(2)}) copy-start(f32[2,1,1,8192]{3,2,1,0:T(1,128)} %param.7) | copy-start | bytes 196612
  12.3 2.5 %copy-start.1 = (f32[4,2,128,128]{3,2,1,0:T(8,128)S(1)}, f32[4,2,128,128]{3,2,1,0:T(8,128)}, u32[]{:S(2)}) copy-start(f32[4,2,128,128]{3,2,1,0:T(8,128)} %param.8) | copy-start | bytes 1572868
  12.3 3.0 %copy-start.5 = (s32[23]{0:T(128)S(1)}, s32[23]{0:T(128)}, u32[]{:S(2)}) copy-start(s32[23]{0:T(128)} %param.10) | copy-start | bytes 280
  26.6 3.6 %copy-start.6 = (s32[23]{0:T(128)S(1)}, s32[23]{0:T(128)}, u32[]{:S(2)}) copy-start(s32[23]{0:T(128)} %param.11) | copy-start | bytes 280
  41.0 21.0 %copy-start.4 = (f32[2,4,4]{2,1,0:T(4,128)S(1)}, f32[2,4,4]{2,1,0:T(4,128)}, u32[]{:S(2)}) copy-start(f32[2,4,4]{2,1,0:T(4,128)} %param.9) | copy-start | bytes 388
  44.1 60.6 %all-to-all-start = ((f32[2,64,128]{2,0,1:T(2,128)}), f32[2,64,128]{2,0,1:T(2,128)S(1)}, u32[]{:S(2)}, u32[]{:S(2)}) async-start(f32[2,64,128]{2,0,1:T(2,128)} %bitcast.116), calls=%async_computation | async-start | bytes 131072 | tf_op jit(solution)/shard_map/all_to_all | solution.py:241
  83.9 10.4 %copy-start.3 = (s32[10]{0:T(128)S(1)}, s32[10]{0:T(128)}, u32[]{:S(2)}) copy-start(s32[10]{0:T(128)} %param.13) | copy-start | bytes 124
  110.5 1.1 copy-start.2
  115.0 48.9 %all-to-all-start.1 = ((f32[16,1,1024]{2,1,0:T(1,128)}), f32[16,1,1024]{2,1,0:T(1,128)S(1)}, u32[]{:S(2)}, u32[]{:S(2)}) async-start(f32[16,1,1024]{2,1,0:T(1,128)} %reshape.840), calls=%async_computation.1 | async-start | bytes 131072 | tf_op jit(solution)/shard_map/all_to_all | solution.py:205

commit v3 on v2

--- a/solution.py
+++ b/solution.py
@@ -146,28 +146,39 @@
 
 
 def pair_exchange(values, place_bit, bit_num, matrix):
-    count_all = values.shape[1]
+    length = values.shape[1]
+    lane_bits = 7
+    rows = length >> lane_bits
+    row_bit = place_bit - lane_bits
     own_bit = jnp.right_shift(lax.axis_index("grp"), bit_num) & 1
     received = swapped(values, "grp", bit_num)
-    shape = (2, count_all >> place_bit + 1, 2, 1 << place_bit)
-    own = values.reshape(shape)
-    other = received.reshape(shape)
-    same = jnp.where(own_bit == 0, matrix[:, 0::2, 0::2], matrix[:, 1::2, 1::2])
-    cross = jnp.where(own_bit == 0, matrix[:, 0::2, 1::2], matrix[:, 1::2, 0::2])
-    parts = []
-    for out_c in range(2):
-        real_part = 0.0
-        imag_part = 0.0
-        for in_c in range(2):
-            for coef, src in ((same, own), (cross, other)):
-                cr = coef[0, out_c, in_c]
-                ci = coef[1, out_c, in_c]
-                xr = src[0, :, in_c]
-                xi = src[1, :, in_c]
-                real_part = real_part + (cr * xr - ci * xi)
-                imag_part = imag_part + (cr * xi + ci * xr)
-        parts.append(jnp.stack([real_part, imag_part]))
-    return jnp.stack(parts, axis=2).reshape(2, count_all)
+    place = jnp.arange(rows, dtype=jnp.int32)
+    mask = 1 << row_bit
+    agree = (place[:, None] | mask) == (place[None, :] | mask)
+    pair_bit = jnp.right_shift(place, row_bit) & 1
+    states = jnp.arange(4, dtype=jnp.int32)
+    pick_out = ((own_bit + 2 * pair_bit)[:, None] == states[None, :]).astype(jnp.float32)
+    pick_par = ((1 - own_bit + 2 * pair_bit)[:, None] == states[None, :]).astype(jnp.float32)
+    blocks = []
+    for pick_in in (pick_out, pick_par):
+        for part in range(2):
+            coef = jnp.dot(
+                jnp.dot(pick_out, matrix[part], precision=HIGHEST), pick_in.T, precision=HIGHEST
+            )
+            blocks.append(jnp.where(agree, coef, 0.0))
+    own_re, own_im, par_re, par_im = blocks
+    operator = jnp.concatenate(
+        [
+            jnp.concatenate([own_re, -own_im, par_re, -par_im], axis=1),
+            jnp.concatenate([own_im, own_re, par_im, par_re], axis=1),
+        ],
+        axis=0,
+    )
+    stacked = jnp.concatenate(
+        [values.reshape(2 * rows, -1), received.reshape(2 * rows, -1)], axis=0
+    )
+    out = jnp.dot(operator, stacked, precision=HIGHEST, preferred_element_type=jnp.float32)
+    return out.reshape(2, length)
 
 
 def pair_operator(matrix, group_bits):
@@ -251,7 +262,8 @@
         ).reshape(2, length)
     values = reorder(values, position_of(layout, layout_out[:local_bits]))
     values = values * spare_sign(length, spare_values)
-    values = group_gates(values, local_bits, group_bits, pair_gate)
+    for bit_num in range(group_bits):
+        values = pair_exchange(values, local_bits - 1 - bit_num, bit_num, pair_gate)
     return values.reshape(amplitudes.shape)
 
 

time: 202 us -> 183 us (0.906); the launches traced: 198 us -> 182 us
  blocking collectives: 29 us -> 0 us
  starting transfers between devices: 39.7 us -> 55.9 us
  local copies, waits for them, and re-layouts: 15.8 us -> 12.9 us
  other arithmetic: 63.1 us -> 60.6 us
    ppermute x0 -> x4, starting transfers between devices: none -> 39.9 us  [swapped(): return lax.ppermute(value, axis, pairs)]
    all_to_all x1 -> x0, blocking collectives: 29 us -> none  [group_gates(): lax.all_to_all(shaped, 'grp', split_axis=2, concat_axis=2, tiled=True)]
    ppermute x0 -> x4, waiting for transfers between devices: none -> 25.3 us  [swapped(): return lax.ppermute(value, axis, pairs)]
    all_to_all x1 -> x0, waiting for transfers between devices: 24.7 us -> none  [group_gates(): lax.all_to_all(shaped, 'grp', split_axis=2, concat_axis=2, tiled=True)]
    all_to_all x1 -> x0, starting transfers between devices: 23.7 us -> none  [group_gates(): lax.all_to_all(shaped, 'grp', split_axis=2, concat_axis=2, tiled=True)]
    dot_general x20 -> x28, matrix products: 6.43 us -> 7.44 us  [the longest x16 3.89 us: pair_exchange(): jnp.dot(jnp.dot(pick_out, matrix[part], precision=HIGHEST), pick_in.T, pr...]
  transfers between devices with their start and end apart: 2 -> 5, of which waited for: 1 -> 4; matrix products, arithmetic and copies ran while one was open for 23% -> 24% of each run, Pallas kernels for 0% -> 0%
where the time goes in v3:
time: 183 us; the launch traced here: 182 us
  other arithmetic  60.6 us (33%)
  starting transfers between devices  55.9 us (31%)
  matrix products  26.3 us (14%)
  waiting for transfers between devices  25.3 us (14%)
  local copies, waits for them, and re-layouts  12.9 us (7%)
    and x6, other arithmetic, reorder(): picked & lanes - 1  49 us
    ppermute x4, starting transfers between devices, swapped(): return lax.ppermute(value, axis, pairs)  39.9 us
    ppermute x4, waiting for transfers between devices, swapped(): return lax.ppermute(value, axis, pairs)  25.3 us
    all_to_all x1, starting transfers between devices, per_device(): lax.all_to_all(shaped, 'dev', split_axis=1, concat_axis=1, tiled=True)  16 us
    dot_general x6, matrix products, reorder(): jnp.dot(values.reshape(2 * rows, lanes), one_hot, precision=HIGHEST, pref...  15 us
    add x1, other arithmetic, spare_sign(): lane_parity + spare_values[place_bit] * (jnp.right_shift(lane_pos, place_...  4.29 us
    slice x6, local copies, waits for them, and re-layouts, source_index(): bit_order[place_bit]  4.2 us
    dot_general x16, matrix products, pair_exchange(): jnp.dot(jnp.dot(pick_out, matrix[part], precision=HIGHEST), pick_in.T, pr...  3.89 us
  transfers between devices with their start and end apart: 5, of which 4 were waited for; matrix products, arithmetic and copies ran while one was open for 24% of the time, Pallas kernels for 0%

profile of v3, /device:TPU:24, one launch (start us, length us, event | category | flops | bytes accessed | tf_op | source)
XLA Modules:
  0.0 181.8 jit_solution(8940157047941308837)
XLA Ops:
  0.0 0.8 slice_bitcast_fusion
  0.8 0.7 compare_reduce_fusion.4
  1.6 0.7 fusion.202
  2.5 0.6 scatter_custom_fusion.9
  3.1 0.7 fusion.268
  3.8 8.2 %broadcast_and_fusion.5 = (s32[8192]{0:T(1024)S(1)}, s32[8192]{0:T(1024)S(1)}) fusion(s32[]{:T(128)} %bitcast.98, s32[]{:T(128)} %bitcast.97, s32[]{:T(128)} %bitcast.96, s32[]{:T(128)} %bitcast.95, s32[]{:T(128)} %bitcast.94, s32[]{:T(128)} %bitcast.93, s32[]{:T(128)} %bitcast.92, s32[]{:T(128)} %bitcast.91, s32[]{:T(128)} %bitcast.90, s32[]{:T(128)} %bitcast.89, ...), kind=kLoop, calls=%fused_computation.249 | loop fusion | flops 434176 | bytes 65588 | tf_op jit(solution)/shard_map/and | solution.py:33
  12.0 0.3 iota_compare_fusion.7
  12.4 2.4 %select_reduce_fusion = f32[2,8192]{1,0:T(2,128)S(1)} fusion(pred[64,8192]{1,0:T(8,128)(4,1)S(1)} %iota_compare_fusion.7, f32[128,128]{1,0:T(8,128)S(1)} %bitcast.325, s32[8192]{0:T(1024)S(1)} %get-tuple-element.141), kind=kOutput, calls=%fused_computation.20 | convolution fusion | flops 1613742080 | bytes 688128 | tf_op jit(solution)/shard_map/dot_general | solution.py:35
  15.3 0.6 scatter_custom_fusion
  16.4 0.2 fusion.39
  16.8 0.6 scatter_custom_fusion.8
  17.5 0.7 fusion.269
  18.2 8.2 %broadcast_and_fusion.4 = (s32[8192]{0:T(1024)S(1)}, s32[8192]{0:T(1024)S(1)}) fusion(s32[]{:T(128)} %bitcast.85, s32[]{:T(128)} %bitcast.84, s32[]{:T(128)} %bitcast.83, s32[]{:T(128)} %bitcast.82, s32[]{:T(128)} %bitcast.81, s32[]{:T(128)} %bitcast.80, s32[]{:T(128)} %bitcast.79, s32[]{:T(128)} %bitcast.78, s32[]{:T(128)} %bitcast.77, s32[]{:T(128)} %bitcast.76, ...), kind=kLoop, calls=%fused_computation.248 | loop fusion | flops 434176 | bytes 65588 | tf_op jit(solution)/shard_map/and | solution.py:33
  26.4 0.3 iota_compare_fusion.8
  26.7 2.4 %fusion.17 = f32[2,8192]{1,0:T(2,128)S(1)} fusion(s32[8192]{0:T(1024)S(1)} %get-tuple-element.139, pred[64,8192]{1,0:T(8,128)(4,1)S(1)} %iota_compare_fusion.8, f32[1,64,128]{2,1,0:T(8,128)S(1)} %fusion.38, f32[1,64,128]{2,1,0:T(8,128)S(1)} %fusion.39), kind=kOutput, calls=%fused_computation.40 | convolution fusion | flops 1613758464 | bytes 688128 | tf_op jit(solution)/shard_map/dot_general | solution.py:35
  29.6 0.6 scatter_custom_fusion.1
  30.7 0.2 fusion.36
  31.2 0.6 scatter_custom_fusion.7
  31.8 0.7 fusion.270
  32.5 8.2 %broadcast_and_fusion.3 = (s32[8192]{0:T(1024)S(1)}, s32[8192]{0:T(1024)S(1)}) fusion(s32[]{:T(128)} %bitcast.72, s32[]{:T(128)} %bitcast.71, s32[]{:T(128)} %bitcast.70, s32[]{:T(128)} %bitcast.69, s32[]{:T(128)} %bitcast.68, s32[]{:T(128)} %bitcast.67, s32[]{:T(128)} %bitcast.66, s32[]{:T(128)} %bitcast.65, s32[]{:T(128)} %bitcast.64, s32[]{:T(128)} %bitcast.63, ...), kind=kLoop, calls=%fused_computation.247 | loop fusion | flops 434176 | bytes 65588 | tf_op jit(solution)/shard_map/and | solution.py:33
  40.7 0.3 iota_compare_fusion.9
  41.0 3.0 %fusion.20 = f32[2,8192]{1,0:T(2,128)} fusion(s32[8192]{0:T(1024)S(1)} %get-tuple-element.137, pred[64,8192]{1,0:T(8,128)(4,1)S(1)} %iota_compare_fusion.9, f32[1,64,128]{2,1,0:T(8,128)S(1)} %fusion.36, f32[1,64,128]{2,1,0:T(8,128)S(1)} %fusion.37), kind=kOutput, calls=%fused_computation.41 | convolution fusion | flops 1613758464 | bytes 688128 | tf_op jit(solution)/shard_map/dot_general | solution.py:35
  44.1 16.0 %all-to-all-start = ((f32[2,64,128]{2,0,1:T(2,128)}), f32[2,64,128]{2,0,1:T(2,128)S(1)}, u32[]{:S(2)}, u32[]{:S(2)}) async-start(f32[2,64,128]{2,0,1:T(2,128)} %bitcast.116), calls=%async_computation | async-start | bytes 131072 | tf_op jit(solution)/shard_map/all_to_all | solution.py:252
  60.1 0.8 scatter_custom_fusion.2
  61.4 0.6 scatter_custom_fusion.3
  62.6 0.3 fusion.281
  62.9 0.2 fusion.280
  64.1 0.3 fusion.279
  65.6 0.6 scatter_custom_fusion.6
  66.2 0.7 fusion.271
  66.9 8.2 %broadcast_and_fusion.2 = (s32[8192]{0:T(1024)S(1)}, s32[8192]{0:T(1024)S(1)}) fusion(s32[]{:T(128)} %bitcast.59, s32[]{:T(128)} %bitcast.58, s32[]{:T(128)} %bitcast.57, s32[]{:T(128)} %bitcast.56, s32[]{:T(128)} %bitcast.55, s32[]{:T(128)} %bitcast.54, s32[]{:T(128)} %bitcast.53, s32[]{:T(128)} %bitcast.52, s32[]{:T(128)} %bitcast.51, s32[]{:T(128)} %bitcast.50, ...), kind=kLoop, calls=%fused_computation.246 | loop fusion | flops 434176 | bytes 65588 | tf_op jit(solution)/shard_map/and | solution.py:33
  75.1 0.3 iota_compare_fusion.10
  75.6 0.6 scatter_custom_fusion.4
  76.2 0.6 scatter_custom_fusion.5
  76.8 0.7 fusion.272
  77.5 8.2 %broadcast_and_fusion.1 = (s32[8192]{0:T(1024)S(1)}, s32[8192]{0:T(1024)S(1)}) fusion(s32[]{:T(128)} %bitcast.46, s32[]{:T(128)} %bitcast.45, s32[]{:T(128)} %bitcast.44, s32[]{:T(128)} %bitcast.43, s32[]{:T(128)} %bitcast.42, s32[]{:T(128)} %bitcast.41, s32[]{:T(128)} %bitcast.40, s32[]{:T(128)} %bitcast.39, s32[]{:T(128)} %bitcast.38, s32[]{:T(128)} %bitcast.37, ...), kind=kLoop, calls=%fused_computation.245 | loop fusion | flops 434176 | bytes 65588 | tf_op jit(solution)/shard_map/and | solution.py:33
  85.7 0.3 iota_compare_fusion.11
  86.2 0.7 fusion.273
  86.9 8.2 %broadcast_and_fusion = (s32[8192]{0:T(1024)S(1)}, s32[8192]{0:T(1024)S(1)}) fusion(s32[]{:T(128)} %bitcast.33, s32[]{:T(128)} %bitcast.32, s32[]{:T(128)} %bitcast.31, s32[]{:T(128)} %bitcast.30, s32[]{:T(128)} %bitcast.29, s32[]{:T(128)} %bitcast.28, s32[]{:T(128)} %bitcast.27, s32[]{:T(128)} %bitcast.26, s32[]{:T(128)} %bitcast.25, s32[]{:T(128)} %bitcast.24, ...), kind=kLoop, calls=%fused_computation.244 | loop fusion | flops 434176 | bytes 65588 | tf_op jit(solution)/shard_map/and | solution.py:33
  95.0 0.3 iota_compare_fusion.12
  95.3 0.7 fusion.267
  96.3 0.2 fusion.276
  96.9 2.0 %multiply_add_fusion.1 = s32[64]{0:T(128)S(1)} fusion(s32[]{:T(128)} %bitcast.134, s32[]{:T(128)} %bitcast.133, s32[]{:T(128)} %bitcast.132), kind=kLoop, calls=%fused_computation.335 | loop fusion | flops 704 | bytes 268 | tf_op jit(solution)/shard_map/add | solution.py:89
  98.9 4.3 %multiply_add_fusion = s32[128]{0:T(128)S(1)} fusion(s32[]{:T(128)} %bitcast.141, s32[]{:T(128)} %bitcast.140, s32[]{:T(128)} %bitcast.139, s32[]{:T(128)} %bitcast.138, s32[]{:T(128)} %bitcast.137, s32[]{:T(128)} %bitcast.136, s32[]{:T(128)} %bitcast.135), kind=kLoop, calls=%fused_computation.334 | loop fusion | flops 3456 | bytes 540 | tf_op jit(solution)/shard_map/add | solution.py:85
  103.3 0.2 fusion.275
  103.6 0.2 fusion.274
  103.8 2.4 %fusion.23 = f32[2,8192]{1,0:T(2,128)S(1)} fusion(s32[8192]{0:T(1024)S(1)} %get-tuple-element.135, pred[64,8192]{1,0:T(8,128)(4,1)S(1)} %iota_compare_fusion.10, f32[2,64,128]{2,0,1:T(2,128)S(1)} %all-to-all-done), kind=kOutput, calls=%fused_computation.42 | convolution fusion | flops 1613742080 | bytes 688128 | tf_op jit(solution)/shard_map/dot_general | solution.py:35
  106.8 0.2 fusion.35
  107.0 0.2 fusion.34
  107.3 2.4 %fusion.26 = f32[2,8192]{1,0:T(2,128)S(1)} fusion(s32[8192]{0:T(1024)S(1)} %get-tuple-element.133, pred[64,8192]{1,0:T(8,128)(4,1)S(1)} %iota_compare_fusion.11, f32[1,64,128]{2,1,0:T(8,128)S(1)} %fusion.34, f32[1,64,128]{2,1,0:T(8,128)S(1)} %fusion.35), kind=kOutput, calls=%fused_computation.43 | convolution fusion | flops 1613758464 | bytes 688128 | tf_op jit(solution)/shard_map/dot_general | solution.py:35
  110.5 0.2 fusion.32
  110.7 2.4 %fusion.29 = f32[2,8192]{1,0:T(2,128)S(1)} fusion(s32[8192]{0:T(1024)S(1)} %get-tuple-element.131, pred[64,8192]{1,0:T(8,128)(4,1)S(1)} %iota_compare_fusion.12, f32[1,64,128]{2,1,0:T(8,128)S(1)} %fusion.32, f32[1,64,128]{2,1,0:T(8,128)S(1)} %fusion.33), kind=kOutput, calls=%fused_computation.44 | convolution fusion | flops 1613758464 | bytes 688128 | tf_op jit(solution)/shard_map/dot_general | solution.py:35
  113.2 15.7 %collective-permute-start = (f32[2,8192]{1,0:T(2,128)S(1)}, f32[2,8192]{1,0:T(2,128)S(1)}, u32[]{:S(2)}, u32[]{:S(2)}) collective-permute-start(f32[2,8192]{1,0:T(2,128)S(1)} %broadcast_multiply_fusion), channel_id=1, source_target_pairs={{0,64},{64,0},{128,192},{192,128},{256,320},{320,256},{384,448},{4... | collective-permute-start | bytes 196616 | tf_op jit(solution)/shard_map/ppermute | solution.py:12
  129.2 11.8 %collective-permute-done = f32[2,8192]{1,0:T(2,128)S(1)} collective-permute-done((f32[2,8192]{1,0:T(2,128)S(1)}, f32[2,8192]{1,0:T(2,128)S(1)}, u32[]{:S(2)}, u32[]{:S(2)}) %collective-permute-start) | collective-permute-done | bytes 65568 | tf_op jit(solution)/shard_map/ppermute | solution.py:12
  141.1 0.3 fusion.88
  141.4 18.4 %collective-permute-start.1 = (f32[2,8192]{1,0:T(2,128)S(1)}, f32[2,8192]{1,0:T(2,128)S(1)}, u32[]{:S(2)}, u32[]{:S(2)}) collective-permute-start(f32[2,8192]{1,0:T(2,128)S(1)} %reshape.777), channel_id=1, source_target_pairs={{0,128},{64,192},{128,0},{192,64},{256,384},{320,448},{384,256},{4... | collective-permute-start | bytes 196616 | tf_op jit(solution)/shard_map/ppermute | solution.py:12
  160.1 6.0 %collective-permute-done.1 = f32[2,8192]{1,0:T(2,128)S(1)} collective-permute-done((f32[2,8192]{1,0:T(2,128)S(1)}, f32[2,8192]{1,0:T(2,128)S(1)}, u32[]{:S(2)}, u32[]{:S(2)}) %collective-permute-start.1) | collective-permute-done | bytes 65568 | tf_op jit(solution)/shard_map/ppermute | solution.py:12
  166.1 0.3 fusion.72
  166.5 2.7 %collective-permute-start.2 = (f32[2,8192]{1,0:T(2,128)S(1)}, f32[2,8192]{1,0:T(2,128)S(1)}, u32[]{:S(2)}, u32[]{:S(2)}) collective-permute-start(f32[2,8192]{1,0:T(2,128)S(1)} %reshape.779), channel_id=1, source_target_pairs={{0,256},{64,320},{128,384},{192,448},{256,0},{320,64},{384,128},{4... | collective-permute-start | bytes 196616 | tf_op jit(solution)/shard_map/ppermute | solution.py:12
  169.4 3.3 %collective-permute-done.2 = f32[2,8192]{1,0:T(2,128)S(1)} collective-permute-done((f32[2,8192]{1,0:T(2,128)S(1)}, f32[2,8192]{1,0:T(2,128)S(1)}, u32[]{:S(2)}, u32[]{:S(2)}) %collective-permute-start.2) | collective-permute-done | bytes 65568 | tf_op jit(solution)/shard_map/ppermute | solution.py:12
  172.7 0.3 fusion.56
  173.1 3.1 %collective-permute-start.3 = (f32[2,8192]{1,0:T(2,128)S(1)}, f32[2,8192]{1,0:T(2,128)S(1)}, u32[]{:S(2)}, u32[]{:S(2)}) collective-permute-start(f32[2,8192]{1,0:T(2,128)S(1)} %reshape.781), channel_id=1, source_target_pairs={{0,512},{64,576},{128,640},{192,704},{256,768},{320,832},{384,896}... | collective-permute-start | bytes 196616 | tf_op jit(solution)/shard_map/ppermute | solution.py:12
  176.5 4.3 %collective-permute-done.3 = f32[2,8192]{1,0:T(2,128)S(1)} collective-permute-done((f32[2,8192]{1,0:T(2,128)S(1)}, f32[2,8192]{1,0:T(2,128)S(1)}, u32[]{:S(2)}, u32[]{:S(2)}) %collective-permute-start.3) | collective-permute-done | bytes 65568 | tf_op jit(solution)/shard_map/ppermute | solution.py:12
  180.8 1.0 fusion.40
  (97 shorter events, 9.6 us)
Async XLA Ops:
  0.0 12.3 %copy-start = (f32[2,1,1,8192]{3,2,1,0:T(1,128)S(1)}, f32[2,1,1,8192]{3,2,1,0:T(1,128)}, u32[]{:S(2)}) copy-start(f32[2,1,1,8192]{3,2,1,0:T(1,128)} %param.7) | copy-start | bytes 196612
  12.3 2.5 %copy-start.1 = (f32[4,2,128,128]{3,2,1,0:T(8,128)S(1)}, f32[4,2,128,128]{3,2,1,0:T(8,128)}, u32[]{:S(2)}) copy-start(f32[4,2,128,128]{3,2,1,0:T(8,128)} %param.8) | copy-start | bytes 1572868
  12.3 3.0 %copy-start.4 = (s32[23]{0:T(128)S(1)}, s32[23]{0:T(128)}, u32[]{:S(2)}) copy-start(s32[23]{0:T(128)} %param.10) | copy-start | bytes 280
  26.6 3.6 %copy-start.5 = (s32[23]{0:T(128)S(1)}, s32[23]{0:T(128)}, u32[]{:S(2)}) copy-start(s32[23]{0:T(128)} %param.11) | copy-start | bytes 280
  41.0 21.2 %copy-start.3 = (f32[2,4,4]{2,1,0:T(4,128)S(1)}, f32[2,4,4]{2,1,0:T(4,128)}, u32[]{:S(2)}) copy-start(f32[2,4,4]{2,1,0:T(4,128)} %param.9) | copy-start | bytes 388
  44.1 59.8 %all-to-all-start = ((f32[2,64,128]{2,0,1:T(2,128)}), f32[2,64,128]{2,0,1:T(2,128)S(1)}, u32[]{:S(2)}, u32[]{:S(2)}) async-start(f32[2,64,128]{2,0,1:T(2,128)} %bitcast.116), calls=%async_computation | async-start | bytes 131072 | tf_op jit(solution)/shard_map/all_to_all | solution.py:252
  85.7 9.6 %copy-start.2 = (s32[10]{0:T(128)S(1)}, s32[10]{0:T(128)}, u32[]{:S(2)}) copy-start(s32[10]{0:T(128)} %param.13) | copy-start | bytes 124
  113.2 27.9 %collective-permute-start = (f32[2,8192]{1,0:T(2,128)S(1)}, f32[2,8192]{1,0:T(2,128)S(1)}, u32[]{:S(2)}, u32[]{:S(2)}) collective-permute-start(f32[2,8192]{1,0:T(2,128)S(1)} %broadcast_multiply_fusion), channel_id=1, source_target_pairs={{0,64},{64,0},{128,192},{192,128},{256,320},{320,256},{384,448},{4... | collective-permute-start | bytes 196616 | tf_op jit(solution)/shard_map/ppermute | solution.py:12
  141.4 24.6 %collective-permute-start.1 = (f32[2,8192]{1,0:T(2,128)S(1)}, f32[2,8192]{1,0:T(2,128)S(1)}, u32[]{:S(2)}, u32[]{:S(2)}) collective-permute-start(f32[2,8192]{1,0:T(2,128)S(1)} %reshape.777), channel_id=1, source_target_pairs={{0,128},{64,192},{128,0},{192,64},{256,384},{320,448},{384,256},{4... | collective-permute-start | bytes 196616 | tf_op jit(solution)/shard_map/ppermute | solution.py:12
  166.5 6.2 %collective-permute-start.2 = (f32[2,8192]{1,0:T(2,128)S(1)}, f32[2,8192]{1,0:T(2,128)S(1)}, u32[]{:S(2)}, u32[]{:S(2)}) collective-permute-start(f32[2,8192]{1,0:T(2,128)S(1)} %reshape.779), channel_id=1, source_target_pairs={{0,256},{64,320},{128,384},{192,448},{256,0},{320,64},{384,128},{4... | collective-permute-start | bytes 196616 | tf_op jit(solution)/shard_map/ppermute | solution.py:12
  173.1 7.7 %collective-permute-start.3 = (f32[2,8192]{1,0:T(2,128)S(1)}, f32[2,8192]{1,0:T(2,128)S(1)}, u32[]{:S(2)}, u32[]{:S(2)}) collective-permute-start(f32[2,8192]{1,0:T(2,128)S(1)} %reshape.781), channel_id=1, source_target_pairs={{0,512},{64,576},{128,640},{192,704},{256,768},{320,832},{384,896}... | collective-permute-start | bytes 196616 | tf_op jit(solution)/shard_map/ppermute | solution.py:12

commit v4 on v3

--- a/solution.py
+++ b/solution.py
@@ -12,14 +12,20 @@
     return lax.ppermute(value, axis, pairs)
 
 
+def bit_table(bit_count):
+    place = jnp.arange(2**bit_count, dtype=jnp.int32)[:, None]
+    return jnp.right_shift(place, jnp.arange(bit_count, dtype=jnp.int32)[None, :]) & 1
+
+
 def source_index(bit_order, bit_count):
-    position = jnp.arange(2**bit_count, dtype=jnp.int32)
-    source = jnp.zeros((2**bit_count,), jnp.int32)
-    for place_bit in range(bit_count):
-        source = source + jnp.left_shift(
-            jnp.right_shift(position, place_bit) & 1, bit_order[place_bit]
-        )
-    return source
+    lane_bits = min(7, bit_count)
+    lane_part = jnp.sum(
+        jnp.left_shift(bit_table(lane_bits), bit_order[None, :lane_bits]), axis=1
+    )
+    row_part = jnp.sum(
+        jnp.left_shift(bit_table(bit_count - lane_bits), bit_order[None, lane_bits:]), axis=1
+    )
+    return (row_part[:, None] + lane_part[None, :]).reshape(2**bit_count)
 
 
 def reorder(values, source):
@@ -74,23 +80,14 @@
 
 def spare_sign(count_all, spare_values):
     lane_bits = 7
-    lanes = 2**lane_bits
-    rows = count_all // lanes
-    lane_pos = jnp.arange(lanes, dtype=jnp.int32)
-    row_pos = jnp.arange(rows, dtype=jnp.int32)
-    lane_parity = jnp.zeros((lanes,), jnp.int32)
-    row_parity = jnp.zeros((rows,), jnp.int32)
-    for place_bit in range(spare_values.shape[0]):
-        if place_bit < lane_bits:
-            lane_parity = lane_parity + spare_values[place_bit] * (
-                jnp.right_shift(lane_pos, place_bit) & 1
-            )
-        else:
-            row_parity = row_parity + spare_values[place_bit] * (
-                jnp.right_shift(row_pos, place_bit - lane_bits) & 1
-            )
+    spare_count = spare_values.shape[0]
+    row_bits = spare_count - lane_bits
+    lane_parity = jnp.sum(bit_table(lane_bits) * spare_values[None, :lane_bits], axis=1)
+    row_parity = jnp.sum(bit_table(row_bits) * spare_values[None, lane_bits:], axis=1)
+    repeat = count_all // (2**spare_count)
     parity = row_parity[:, None] + lane_parity[None, :]
-    return (1 - 2 * (parity & 1)).astype(jnp.float32).reshape(count_all)
+    sign = (1 - 2 * (parity & 1)).astype(jnp.float32).reshape(1, 2**spare_count)
+    return jnp.broadcast_to(sign, (repeat, 2**spare_count)).reshape(count_all)
 
 
 def position_of(layout, wanted):
@@ -119,8 +116,9 @@
         jnp.where(trail_any, trail_rank, lead_count + jnp.cumsum(remaining) - 1),
     )
     places = jnp.arange(layout_len, dtype=jnp.int32)
-    source = jnp.zeros((layout_len,), jnp.int32).at[target].set(places)
-    new_layout = jnp.zeros((layout_len,), jnp.int32).at[target].set(layout)
+    lands = target[None, :] == places[:, None]
+    source = jnp.sum(jnp.where(lands, places[None, :], 0), axis=1)
+    new_layout = jnp.sum(jnp.where(lands, layout[None, :], 0), axis=1)
     return (new_layout, source)
 
 

time: 183 us -> 131 us (0.72)
  other arithmetic: 60.6 us -> 8.19 us
  waiting for transfers between devices: 25.3 us -> 36.9 us
  local copies, waits for them, and re-layouts: 12.9 us -> 2.19 us
    and x6 -> x1, other arithmetic: 49 us -> 0.08 us  [reorder(): picked & lanes - 1]
    ppermute x4, waiting for transfers between devices: 25.3 us -> 32.8 us  [swapped(): return lax.ppermute(value, axis, pairs)]
    scatter x10 -> x0, local copies, waits for them, and re-layouts: 6.31 us -> none  [the longest x5 3.24 us: arrange(): new_layout = jnp.zeros((layout_len,), jnp.int32).at[target].set(layout)]
    add x2 -> x0, other arithmetic: 6.28 us -> none  [the longest x1 4.29 us: spare_sign(): lane_parity + spare_values[place_bit] * (jnp.right_shift(lane_pos, place_...]
    slice x7, local copies, waits for them, and re-layouts: 4.9 us -> 0.55 us  [the longest x6 0.48 us: source_index(): bit_order[None, lane_bits:]]
    all_to_all x1, waiting for transfers between devices: 0.01 us -> 4.13 us  [per_device(): lax.all_to_all(shaped, 'dev', split_axis=1, concat_axis=1, tiled=True)]
    reduce_sum x0 -> x19, other arithmetic: none -> 2.44 us  [the longest x5 1.24 us: arrange(): source = jnp.sum(jnp.where(lands, places[None, :], 0), axis=1)]
  transfers between devices with their start and end apart: 5 -> 5, of which waited for: 4 -> 5; matrix products, arithmetic and copies ran while one was open for 24% -> 7% of each run, Pallas kernels for 0% -> 0%
where the time goes in v4:
time: 131 us; the launch traced here: 130 us
  starting transfers between devices  55.9 us (43%)
  waiting for transfers between devices  36.9 us (28%)
  matrix products  26.3 us (20%)
  other arithmetic  8.19 us (6%)
  local copies, waits for them, and re-layouts  2.19 us (2%)
    ppermute x4, starting transfers between devices, swapped(): return lax.ppermute(value, axis, pairs)  39.7 us
    ppermute x4, waiting for transfers between devices, swapped(): return lax.ppermute(value, axis, pairs)  32.8 us
    all_to_all x1, starting transfers between devices, per_device(): lax.all_to_all(shaped, 'dev', split_axis=1, concat_axis=1, tiled=True)  16.2 us
    dot_general x6, matrix products, reorder(): jnp.dot(values.reshape(2 * rows, lanes), one_hot, precision=HIGHEST, pref...  15 us
    all_to_all x1, waiting for transfers between devices, per_device(): lax.all_to_all(shaped, 'dev', split_axis=1, concat_axis=1, tiled=True)  4.13 us
    dot_general x16, matrix products, pair_exchange(): jnp.dot(jnp.dot(pick_out, matrix[part], precision=HIGHEST), pick_in.T, pr...  3.93 us
  transfers between devices with their start and end apart: 5, of which 5 were waited for; matrix products, arithmetic and copies ran while one was open for 7% of the time, Pallas kernels for 0%

profile of v4, /device:TPU:24, one launch (start us, length us, event | category | flops | bytes accessed | tf_op | source)
XLA Modules:
  0.0 130.2 jit_solution(11888860985514133318)
XLA Ops:
  0.0 0.8 slice_bitcast_fusion
  0.8 0.7 compare_reduce_fusion.4
  1.6 0.7 fusion.213
  2.5 0.8 select_reduce_fusion.1
  3.8 0.3 iota_compare_fusion.7
  4.1 2.4 %select_reduce_fusion = f32[2,8192]{1,0:T(2,128)S(1)} fusion(pred[64,8192]{1,0:T(8,128)(4,1)S(1)} %iota_compare_fusion.7, f32[128,128]{1,0:T(8,128)S(1)} %bitcast.220, s32[8192]{0:T(1024)S(1)} %get-tuple-element.29), kind=kOutput, calls=%fused_computation.10 | convolution fusion | flops 1613742080 | bytes 688128 | tf_op jit(solution)/shard_map/dot_general | solution.py:41
  6.6 0.2 fusion.146
  6.8 0.2 fusion.150
  7.7 0.3 iota_compare_fusion.8
  8.0 0.2 fusion.38
  8.3 0.2 fusion.39
  8.5 2.4 %fusion.17 = f32[2,8192]{1,0:T(2,128)S(1)} fusion(s32[8192]{0:T(1024)S(1)} %get-tuple-element.32, pred[64,8192]{1,0:T(8,128)(4,1)S(1)} %iota_compare_fusion.8, f32[1,64,128]{2,1,0:T(8,128)S(1)} %fusion.38, f32[1,64,128]{2,1,0:T(8,128)S(1)} %fusion.39), kind=kOutput, calls=%fused_computation.30 | convolution fusion | flops 1613758464 | bytes 688128 | tf_op jit(solution)/shard_map/dot_general | solution.py:41
  11.0 0.2 fusion.144
  11.2 0.2 fusion.140
  11.7 0.2 fusion.37
  12.0 0.2 fusion.36
  12.9 0.3 iota_compare_fusion.9
  13.2 3.0 %fusion.20 = f32[2,8192]{1,0:T(2,128)} fusion(s32[8192]{0:T(1024)S(1)} %get-tuple-element.34, pred[64,8192]{1,0:T(8,128)(4,1)S(1)} %iota_compare_fusion.9, f32[1,64,128]{2,1,0:T(8,128)S(1)} %fusion.36, f32[1,64,128]{2,1,0:T(8,128)S(1)} %fusion.37), kind=kOutput, calls=%fused_computation.31 | convolution fusion | flops 1613758464 | bytes 688128 | tf_op jit(solution)/shard_map/dot_general | solution.py:41
  16.2 16.2 %all-to-all-start = ((f32[2,64,128]{2,0,1:T(2,128)}), f32[2,64,128]{2,0,1:T(2,128)S(1)}, u32[]{:S(2)}, u32[]{:S(2)}) async-start(f32[2,64,128]{2,0,1:T(2,128)} %bitcast.42), calls=%async_computation | async-start | bytes 131072 | tf_op jit(solution)/shard_map/all_to_all | solution.py:250
  33.5 0.2 fusion.182
  33.7 0.3 fusion.260
  34.0 0.2 fusion.259
  34.2 0.2 convolution_select_fusion.8
  34.5 0.2 convolution_select_fusion.6
  34.9 0.2 fusion.184
  35.2 0.3 fusion.258
  35.4 0.2 fusion.257
  35.7 0.2 convolution_select_fusion.12
  35.9 0.2 convolution_select_fusion.10
  37.0 0.3 iota_compare_fusion.10
  37.9 0.3 iota_compare_fusion.11
  38.7 0.3 iota_compare_fusion.12
  39.4 0.2 fusion.256
  39.6 0.2 fusion.255
  39.9 0.2 convolution_select_fusion.16
  40.3 0.3 fusion.254
  40.6 0.2 fusion.253
  40.9 4.1 %all-to-all-done = f32[2,64,128]{2,0,1:T(2,128)S(1)} async-done(((f32[2,64,128]{2,0,1:T(2,128)}), f32[2,64,128]{2,0,1:T(2,128)S(1)}, u32[]{:S(2)}, u32[]{:S(2)}) %all-to-all-start) | async-done | bytes 65568 | tf_op jit(solution)/shard_map/all_to_all | solution.py:250
  45.0 2.4 %fusion.23 = f32[2,8192]{1,0:T(2,128)S(1)} fusion(s32[8192]{0:T(1024)S(1)} %get-tuple-element.36, pred[64,8192]{1,0:T(8,128)(4,1)S(1)} %iota_compare_fusion.10, f32[2,64,128]{2,0,1:T(2,128)S(1)} %all-to-all-done), kind=kOutput, calls=%fused_computation.32 | convolution fusion | flops 1613742080 | bytes 688128 | tf_op jit(solution)/shard_map/dot_general | solution.py:41
  47.5 0.2 fusion.138
  47.7 0.2 fusion.134
  47.9 0.2 fusion.35
  48.2 0.2 fusion.34
  48.4 2.4 %fusion.26 = f32[2,8192]{1,0:T(2,128)S(1)} fusion(s32[8192]{0:T(1024)S(1)} %get-tuple-element.38, pred[64,8192]{1,0:T(8,128)(4,1)S(1)} %iota_compare_fusion.11, f32[1,64,128]{2,1,0:T(8,128)S(1)} %fusion.34, f32[1,64,128]{2,1,0:T(8,128)S(1)} %fusion.35), kind=kOutput, calls=%fused_computation.33 | convolution fusion | flops 1613758464 | bytes 688128 | tf_op jit(solution)/shard_map/dot_general | solution.py:41
  50.9 0.2 fusion.132
  51.1 0.2 fusion.128
  51.4 0.2 fusion.33
  51.6 0.2 fusion.32
  51.9 2.4 %fusion.29 = f32[2,8192]{1,0:T(2,128)S(1)} fusion(s32[8192]{0:T(1024)S(1)} %get-tuple-element.40, pred[64,8192]{1,0:T(8,128)(4,1)S(1)} %iota_compare_fusion.12, f32[1,64,128]{2,1,0:T(8,128)S(1)} %fusion.32, f32[1,64,128]{2,1,0:T(8,128)S(1)} %fusion.33), kind=kOutput, calls=%fused_computation.34 | convolution fusion | flops 1613758464 | bytes 688128 | tf_op jit(solution)/shard_map/dot_general | solution.py:41
  54.3 15.7 %collective-permute-start = (f32[2,8192]{1,0:T(2,128)S(1)}, f32[2,8192]{1,0:T(2,128)S(1)}, u32[]{:S(2)}, u32[]{:S(2)}) collective-permute-start(f32[2,8192]{1,0:T(2,128)S(1)} %broadcast_multiply_fusion), channel_id=1, source_target_pairs={{0,64},{64,0},{128,192},{192,128},{256,320},{320,256},{384,448},{4... | collective-permute-start | bytes 196616 | tf_op jit(solution)/shard_map/ppermute | solution.py:12
  70.1 0.2 convolution_select_fusion.14
  70.4 11.7 %collective-permute-done = f32[2,8192]{1,0:T(2,128)S(1)} collective-permute-done((f32[2,8192]{1,0:T(2,128)S(1)}, f32[2,8192]{1,0:T(2,128)S(1)}, u32[]{:S(2)}, u32[]{:S(2)}) %collective-permute-start) | collective-permute-done | bytes 65568 | tf_op jit(solution)/shard_map/ppermute | solution.py:12
  82.1 0.3 fusion.88
  82.5 18.2 %collective-permute-start.1 = (f32[2,8192]{1,0:T(2,128)S(1)}, f32[2,8192]{1,0:T(2,128)S(1)}, u32[]{:S(2)}, u32[]{:S(2)}) collective-permute-start(f32[2,8192]{1,0:T(2,128)S(1)} %reshape.699), channel_id=1, source_target_pairs={{0,128},{64,192},{128,0},{192,64},{256,384},{320,448},{384,256},{4... | collective-permute-start | bytes 196616 | tf_op jit(solution)/shard_map/ppermute | solution.py:12
  100.9 13.6 %collective-permute-done.1 = f32[2,8192]{1,0:T(2,128)S(1)} collective-permute-done((f32[2,8192]{1,0:T(2,128)S(1)}, f32[2,8192]{1,0:T(2,128)S(1)}, u32[]{:S(2)}, u32[]{:S(2)}) %collective-permute-start.1) | collective-permute-done | bytes 65568 | tf_op jit(solution)/shard_map/ppermute | solution.py:12
  114.5 0.3 fusion.72
  114.9 2.7 %collective-permute-start.2 = (f32[2,8192]{1,0:T(2,128)S(1)}, f32[2,8192]{1,0:T(2,128)S(1)}, u32[]{:S(2)}, u32[]{:S(2)}) collective-permute-start(f32[2,8192]{1,0:T(2,128)S(1)} %reshape.701), channel_id=1, source_target_pairs={{0,256},{64,320},{128,384},{192,448},{256,0},{320,64},{384,128},{4... | collective-permute-start | bytes 196616 | tf_op jit(solution)/shard_map/ppermute | solution.py:12
  117.6 0.2 convolution_select_fusion.20
  117.8 3.3 %collective-permute-done.2 = f32[2,8192]{1,0:T(2,128)S(1)} collective-permute-done((f32[2,8192]{1,0:T(2,128)S(1)}, f32[2,8192]{1,0:T(2,128)S(1)}, u32[]{:S(2)}, u32[]{:S(2)}) %collective-permute-start.2) | collective-permute-done | bytes 65568 | tf_op jit(solution)/shard_map/ppermute | solution.py:12
  121.1 0.3 fusion.56
  121.5 3.1 %collective-permute-start.3 = (f32[2,8192]{1,0:T(2,128)S(1)}, f32[2,8192]{1,0:T(2,128)S(1)}, u32[]{:S(2)}, u32[]{:S(2)}) collective-permute-start(f32[2,8192]{1,0:T(2,128)S(1)} %reshape.703), channel_id=1, source_target_pairs={{0,512},{64,576},{128,640},{192,704},{256,768},{320,832},{384,896}... | collective-permute-start | bytes 196616 | tf_op jit(solution)/shard_map/ppermute | solution.py:12
  124.6 0.2 convolution_select_fusion.18
  124.9 4.3 %collective-permute-done.3 = f32[2,8192]{1,0:T(2,128)S(1)} collective-permute-done((f32[2,8192]{1,0:T(2,128)S(1)}, f32[2,8192]{1,0:T(2,128)S(1)}, u32[]{:S(2)}, u32[]{:S(2)}) %collective-permute-start.3) | collective-permute-done | bytes 65568 | tf_op jit(solution)/shard_map/ppermute | solution.py:12
  129.2 1.0 fusion.40
  (102 shorter events, 6.8 us)
Async XLA Ops:
  0.0 4.1 %copy-start = (f32[2,1,1,8192]{3,2,1,0:T(1,128)S(1)}, f32[2,1,1,8192]{3,2,1,0:T(1,128)}, u32[]{:S(2)}) copy-start(f32[2,1,1,8192]{3,2,1,0:T(1,128)} %param.7) | copy-start | bytes 196612
  4.1 2.5 %copy-start.1 = (f32[4,2,128,128]{3,2,1,0:T(8,128)S(1)}, f32[4,2,128,128]{3,2,1,0:T(8,128)}, u32[]{:S(2)}) copy-start(f32[4,2,128,128]{3,2,1,0:T(8,128)} %param.8) | copy-start | bytes 1572868
  8.5 3.0 %copy-start.4 = (s32[23]{0:T(128)S(1)}, s32[23]{0:T(128)}, u32[]{:S(2)}) copy-start(s32[23]{0:T(128)} %param.11) | copy-start | bytes 280
  13.2 19.2 %copy-start.2 = (s32[23]{0:T(128)S(1)}, s32[23]{0:T(128)}, u32[]{:S(2)}) copy-start(s32[23]{0:T(128)} %param.10) | copy-start | bytes 280
  13.2 20.1 %copy-start.3 = (f32[2,4,4]{2,1,0:T(4,128)S(1)}, f32[2,4,4]{2,1,0:T(4,128)}, u32[]{:S(2)}) copy-start(f32[2,4,4]{2,1,0:T(4,128)} %param.9) | copy-start | bytes 388
  16.2 28.8 %all-to-all-start = ((f32[2,64,128]{2,0,1:T(2,128)}), f32[2,64,128]{2,0,1:T(2,128)S(1)}, u32[]{:S(2)}, u32[]{:S(2)}) async-start(f32[2,64,128]{2,0,1:T(2,128)} %bitcast.42), calls=%async_computation | async-start | bytes 131072 | tf_op jit(solution)/shard_map/all_to_all | solution.py:250
  37.9 1.1 copy-start.5
  54.3 27.7 %collective-permute-start = (f32[2,8192]{1,0:T(2,128)S(1)}, f32[2,8192]{1,0:T(2,128)S(1)}, u32[]{:S(2)}, u32[]{:S(2)}) collective-permute-start(f32[2,8192]{1,0:T(2,128)S(1)} %broadcast_multiply_fusion), channel_id=1, source_target_pairs={{0,64},{64,0},{128,192},{192,128},{256,320},{320,256},{384,448},{4... | collective-permute-start | bytes 196616 | tf_op jit(solution)/shard_map/ppermute | solution.py:12
  82.5 32.0 %collective-permute-start.1 = (f32[2,8192]{1,0:T(2,128)S(1)}, f32[2,8192]{1,0:T(2,128)S(1)}, u32[]{:S(2)}, u32[]{:S(2)}) collective-permute-start(f32[2,8192]{1,0:T(2,128)S(1)} %reshape.699), channel_id=1, source_target_pairs={{0,128},{64,192},{128,0},{192,64},{256,384},{320,448},{384,256},{4... | collective-permute-start | bytes 196616 | tf_op jit(solution)/shard_map/ppermute | solution.py:12
  114.9 6.2 %collective-permute-start.2 = (f32[2,8192]{1,0:T(2,128)S(1)}, f32[2,8192]{1,0:T(2,128)S(1)}, u32[]{:S(2)}, u32[]{:S(2)}) collective-permute-start(f32[2,8192]{1,0:T(2,128)S(1)} %reshape.701), channel_id=1, source_target_pairs={{0,256},{64,320},{128,384},{192,448},{256,0},{320,64},{384,128},{4... | collective-permute-start | bytes 196616 | tf_op jit(solution)/shard_map/ppermute | solution.py:12
  121.5 7.7 %collective-permute-start.3 = (f32[2,8192]{1,0:T(2,128)S(1)}, f32[2,8192]{1,0:T(2,128)S(1)}, u32[]{:S(2)}, u32[]{:S(2)}) collective-permute-start(f32[2,8192]{1,0:T(2,128)S(1)} %reshape.703), channel_id=1, source_target_pairs={{0,512},{64,576},{128,640},{192,704},{256,768},{320,832},{384,896}... | collective-permute-start | bytes 196616 | tf_op jit(solution)/shard_map/ppermute | solution.py:12

commit v5 on v4

--- a/solution.py
+++ b/solution.py
@@ -179,6 +179,70 @@
     return out.reshape(2, length)
 
 
+def row_pair_operator(matrix, rows, pairs):
+    place = jnp.arange(rows, dtype=jnp.int32)
+    states = jnp.arange(4, dtype=jnp.int32)
+    touched = 0
+    real_part = None
+    imag_part = None
+    for bit_a, bit_c in pairs:
+        touched = touched | 1 << bit_a | 1 << bit_c
+        pair_state = (jnp.right_shift(place, bit_a) & 1) + 2 * (jnp.right_shift(place, bit_c) & 1)
+        pick = (pair_state[:, None] == states[None, :]).astype(jnp.float32)
+        factor_re = jnp.dot(jnp.dot(pick, matrix[0], precision=HIGHEST), pick.T, precision=HIGHEST)
+        factor_im = jnp.dot(jnp.dot(pick, matrix[1], precision=HIGHEST), pick.T, precision=HIGHEST)
+        if real_part is None:
+            real_part, imag_part = factor_re, factor_im
+        else:
+            real_part, imag_part = (
+                real_part * factor_re - imag_part * factor_im,
+                real_part * factor_im + imag_part * factor_re,
+            )
+    agree = (place[:, None] | touched) == (place[None, :] | touched)
+    real_part = jnp.where(agree, real_part, 0.0)
+    imag_part = jnp.where(agree, imag_part, 0.0)
+    return jnp.concatenate(
+        [
+            jnp.concatenate([real_part, -imag_part], axis=1),
+            jnp.concatenate([imag_part, real_part], axis=1),
+        ],
+        axis=0,
+    )
+
+
+def field_exchange(values, field_bits):
+    width = 2**field_bits
+    own = lax.axis_index("grp") & width - 1
+    shaped = values.reshape(2, -1, width, 2**7)
+    received = {}
+    for flip in range(1, width):
+        outgoing = lax.dynamic_index_in_dim(shaped, own ^ flip, axis=2, keepdims=False)
+        pairs = [(source, source ^ flip) for source in range(lax.axis_size("grp"))]
+        received[flip] = lax.ppermute(outgoing, "grp", pairs)
+    parts = []
+    for place in range(width):
+        chosen = shaped[:, :, place]
+        for flip in range(1, width):
+            chosen = jnp.where((own ^ place) == flip, received[flip], chosen)
+        parts.append(chosen)
+    return jnp.stack(parts, axis=2).reshape(values.shape)
+
+
+def field_pair_gates(values, local_bits, field_bits, matrix):
+    lane_bits = 7
+    rows = values.shape[1] >> lane_bits
+    pairs = [(bit_num, local_bits - 1 - bit_num - lane_bits) for bit_num in range(field_bits)]
+    operator = row_pair_operator(matrix, rows, pairs)
+    values = field_exchange(values, field_bits)
+    values = jnp.dot(
+        operator,
+        values.reshape(2 * rows, -1),
+        precision=HIGHEST,
+        preferred_element_type=jnp.float32,
+    ).reshape(values.shape)
+    return field_exchange(values, field_bits)
+
+
 def pair_operator(matrix, group_bits):
     size = 2 ** (2 * group_bits)
     place = jnp.arange(size, dtype=jnp.int32)
@@ -260,7 +324,9 @@
         ).reshape(2, length)
     values = reorder(values, position_of(layout, layout_out[:local_bits]))
     values = values * spare_sign(length, spare_values)
-    for bit_num in range(group_bits):
+    field_bits = 2
+    values = field_pair_gates(values, local_bits, field_bits, pair_gate)
+    for bit_num in range(field_bits, group_bits):
         values = pair_exchange(values, local_bits - 1 - bit_num, bit_num, pair_gate)
     return values.reshape(amplitudes.shape)
 

time: 131 us -> 147 us (1.12)
  starting transfers between devices: 55.9 us -> 78.1 us
  waiting for transfers between devices: 36.9 us -> 31.8 us
    ppermute x0 -> x6, starting transfers between devices: none -> 56.4 us  [field_exchange(): received[flip] = lax.ppermute(outgoing, 'grp', pairs)]
    ppermute x4 -> x2, starting transfers between devices: 39.7 us -> 5.54 us  [swapped(): return lax.ppermute(value, axis, pairs)]
    ppermute x4 -> x2, waiting for transfers between devices: 32.8 us -> 8.03 us  [swapped(): return lax.ppermute(value, axis, pairs)]
    ppermute x0 -> x6, waiting for transfers between devices: none -> 19 us  [field_exchange(): received[flip] = lax.ppermute(outgoing, 'grp', pairs)]
    dot_general x0 -> x9, matrix products: none -> 1.99 us  [the longest x2 0.51 us: row_pair_operator(): jnp.dot(jnp.dot(pick, matrix[0], precision=HIGHEST), pick.T, precision=HI...]
    dot_general x16 -> x8, matrix products: 3.93 us -> 1.99 us  [pair_exchange(): jnp.dot(jnp.dot(pick_out, matrix[part], precision=HIGHEST), pick_in.T, pr...]
  transfers between devices with their start and end apart: 5 -> 9, of which waited for: 5 -> 7; matrix products, arithmetic and copies ran while one was open for 7% -> 6% of each run, Pallas kernels for 0% -> 0%
where the time goes in v5:
time: 147 us; the launch traced here: 146 us
  starting transfers between devices  78.1 us (53%)
  waiting for transfers between devices  31.8 us (22%)
  matrix products  24.9 us (17%)
  other arithmetic  8.29 us (6%)
  local copies, waits for them, and re-layouts  2.32 us (2%)
    ppermute x6, starting transfers between devices, field_exchange(): received[flip] = lax.ppermute(outgoing, 'grp', pairs)  56.4 us
    ppermute x6, waiting for transfers between devices, field_exchange(): received[flip] = lax.ppermute(outgoing, 'grp', pairs)  19 us
    all_to_all x1, starting transfers between devices, per_device(): lax.all_to_all(shaped, 'dev', split_axis=1, concat_axis=1, tiled=True)  16.2 us
    dot_general x6, matrix products, reorder(): jnp.dot(values.reshape(2 * rows, lanes), one_hot, precision=HIGHEST, pref...  15 us
    ppermute x2, waiting for transfers between devices, swapped(): return lax.ppermute(value, axis, pairs)  8.03 us
    ppermute x2, starting transfers between devices, swapped(): return lax.ppermute(value, axis, pairs)  5.54 us
    all_to_all x1, waiting for transfers between devices, per_device(): lax.all_to_all(shaped, 'dev', split_axis=1, concat_axis=1, tiled=True)  4.75 us
  transfers between devices with their start and end apart: 9, of which 7 were waited for; matrix products, arithmetic and copies ran while one was open for 6% of the time, Pallas kernels for 0%

profile of v5, /device:TPU:24, one launch (start us, length us, event | category | flops | bytes accessed | tf_op | source)
XLA Modules:
  0.0 146.1 jit_solution(6449378739220469096)
XLA Ops:
  0.0 0.8 slice_bitcast_fusion.8
  0.8 0.7 compare_reduce_fusion.4
  1.6 0.7 fusion.209
  2.5 0.8 select_reduce_fusion.1
  3.8 0.3 iota_compare_fusion.7
  4.1 2.4 %select_reduce_fusion = f32[2,8192]{1,0:T(2,128)S(1)} fusion(pred[64,8192]{1,0:T(8,128)(4,1)S(1)} %iota_compare_fusion.7, f32[128,128]{1,0:T(8,128)S(1)} %bitcast.328, s32[8192]{0:T(1024)S(1)} %get-tuple-element.44), kind=kOutput, calls=%fused_computation.10 | convolution fusion | flops 1613742080 | bytes 688128 | tf_op jit(solution)/shard_map/dot_general | solution.py:41
  6.6 0.2 fusion.108
  6.8 0.2 fusion.112
  7.7 0.3 iota_compare_fusion.8
  8.0 0.2 fusion.38
  8.3 0.2 fusion.39
  8.5 2.4 %fusion.17 = f32[2,8192]{1,0:T(2,128)S(1)} fusion(s32[8192]{0:T(1024)S(1)} %get-tuple-element.47, pred[64,8192]{1,0:T(8,128)(4,1)S(1)} %iota_compare_fusion.8, f32[1,64,128]{2,1,0:T(8,128)S(1)} %fusion.38, f32[1,64,128]{2,1,0:T(8,128)S(1)} %fusion.39), kind=kOutput, calls=%fused_computation.30 | convolution fusion | flops 1613758464 | bytes 688128 | tf_op jit(solution)/shard_map/dot_general | solution.py:41
  11.0 0.2 fusion.106
  11.2 0.2 fusion.102
  11.7 0.2 fusion.37
  12.0 0.2 fusion.36
  12.9 0.3 iota_compare_fusion.9
  13.2 3.0 %fusion.20 = f32[2,8192]{1,0:T(2,128)} fusion(s32[8192]{0:T(1024)S(1)} %get-tuple-element.49, pred[64,8192]{1,0:T(8,128)(4,1)S(1)} %iota_compare_fusion.9, f32[1,64,128]{2,1,0:T(8,128)S(1)} %fusion.36, f32[1,64,128]{2,1,0:T(8,128)S(1)} %fusion.37), kind=kOutput, calls=%fused_computation.31 | convolution fusion | flops 1613758464 | bytes 688128 | tf_op jit(solution)/shard_map/dot_general | solution.py:41
  16.2 16.2 %all-to-all-start = ((f32[2,64,128]{2,0,1:T(2,128)}), f32[2,64,128]{2,0,1:T(2,128)S(1)}, u32[]{:S(2)}, u32[]{:S(2)}) async-start(f32[2,64,128]{2,0,1:T(2,128)} %bitcast.43), calls=%async_computation | async-start | bytes 131072 | tf_op jit(solution)/shard_map/all_to_all | solution.py:314
  33.5 0.2 fusion.148
  33.7 0.2 fusion.153
  34.2 0.3 fusion.258
  34.5 0.2 fusion.257
  34.7 0.2 convolution_select_fusion.8
  34.9 0.2 convolution_select_fusion.6
  35.5 0.3 iota_compare_fusion.10
  36.5 0.3 iota_compare_fusion.11
  37.3 0.3 iota_compare_fusion.12
  38.2 0.3 fusion.151
  38.5 0.2 fusion.145
  38.7 0.2 fusion.147
  39.3 0.2 fusion.256
  39.7 0.3 fusion.255
  40.0 0.2 fusion.250
  40.2 4.8 %all-to-all-done = f32[2,64,128]{2,0,1:T(2,128)S(1)} async-done(((f32[2,64,128]{2,0,1:T(2,128)}), f32[2,64,128]{2,0,1:T(2,128)S(1)}, u32[]{:S(2)}, u32[]{:S(2)}) %all-to-all-start) | async-done | bytes 65568 | tf_op jit(solution)/shard_map/all_to_all | solution.py:314
  45.0 2.4 %fusion.23 = f32[2,8192]{1,0:T(2,128)S(1)} fusion(s32[8192]{0:T(1024)S(1)} %get-tuple-element.51, pred[64,8192]{1,0:T(8,128)(4,1)S(1)} %iota_compare_fusion.10, f32[2,64,128]{2,0,1:T(2,128)S(1)} %all-to-all-done), kind=kOutput, calls=%fused_computation.32 | convolution fusion | flops 1613742080 | bytes 688128 | tf_op jit(solution)/shard_map/dot_general | solution.py:41
  47.5 0.2 fusion.100
  47.7 0.2 fusion.96
  47.9 0.2 fusion.35
  48.2 0.2 fusion.34
  48.4 2.4 %fusion.26 = f32[2,8192]{1,0:T(2,128)S(1)} fusion(s32[8192]{0:T(1024)S(1)} %get-tuple-element.53, pred[64,8192]{1,0:T(8,128)(4,1)S(1)} %iota_compare_fusion.11, f32[1,64,128]{2,1,0:T(8,128)S(1)} %fusion.34, f32[1,64,128]{2,1,0:T(8,128)S(1)} %fusion.35), kind=kOutput, calls=%fused_computation.33 | convolution fusion | flops 1613758464 | bytes 688128 | tf_op jit(solution)/shard_map/dot_general | solution.py:41
  50.9 0.2 fusion.94
  51.1 0.2 fusion.90
  51.4 0.2 fusion.33
  51.6 0.2 fusion.32
  51.9 2.4 %fusion.29 = f32[2,8192]{1,0:T(2,128)S(1)} fusion(s32[8192]{0:T(1024)S(1)} %get-tuple-element.55, pred[64,8192]{1,0:T(8,128)(4,1)S(1)} %iota_compare_fusion.12, f32[1,64,128]{2,1,0:T(8,128)S(1)} %fusion.32, f32[1,64,128]{2,1,0:T(8,128)S(1)} %fusion.33), kind=kOutput, calls=%fused_computation.34 | convolution fusion | flops 1613758464 | bytes 688128 | tf_op jit(solution)/shard_map/dot_general | solution.py:41
  54.4 15.5 %collective-permute-start = (f32[2,16,128]{2,1,0:T(8,128)S(1)}, f32[2,16,128]{2,1,0:T(8,128)S(1)}, u32[]{:S(2)}, u32[]{:S(2)}) collective-permute-start(f32[2,16,128]{2,1,0:T(8,128)S(1)} %get-tuple-element.31), channel_id=1, source_target_pairs={{0,192},{64,128},{128,64},{192,0},{256,448},{320,384},{384,320},{4... | collective-permute-start | bytes 49160 | tf_op jit(solution)/shard_map/ppermute | solution.py:221
  69.9 12.3 %collective-permute-start.1 = (f32[2,16,128]{2,1,0:T(8,128)S(1)}, f32[2,16,128]{2,1,0:T(8,128)S(1)}, u32[]{:S(2)}, u32[]{:S(2)}) collective-permute-start(f32[2,16,128]{2,1,0:T(8,128)S(1)} %get-tuple-element.30), channel_id=1, source_target_pairs={{0,128},{64,192},{128,0},{192,64},{256,384},{320,448},{384,256},{4... | collective-permute-start | bytes 49160 | tf_op jit(solution)/shard_map/ppermute | solution.py:221
  82.2 1.9 %collective-permute-start.2 = (f32[2,16,128]{2,1,0:T(8,128)S(1)}, f32[2,16,128]{2,1,0:T(8,128)S(1)}, u32[]{:S(2)}, u32[]{:S(2)}) collective-permute-start(f32[2,16,128]{2,1,0:T(8,128)S(1)} %get-tuple-element.29), channel_id=1, source_target_pairs={{0,64},{64,0},{128,192},{192,128},{256,320},{320,256},{384,448},{4... | collective-permute-start | bytes 49160 | tf_op jit(solution)/shard_map/ppermute | solution.py:221
  84.3 9.6 %collective-permute-done.1 = f32[2,16,128]{2,1,0:T(8,128)S(1)} collective-permute-done((f32[2,16,128]{2,1,0:T(8,128)S(1)}, f32[2,16,128]{2,1,0:T(8,128)S(1)}, u32[]{:S(2)}, u32[]{:S(2)}) %collective-permute-start.1) | collective-permute-done | bytes 16416 | tf_op jit(solution)/shard_map/ppermute | solution.py:221
  93.9 3.6 %collective-permute-done.2 = f32[2,16,128]{2,1,0:T(8,128)S(1)} collective-permute-done((f32[2,16,128]{2,1,0:T(8,128)S(1)}, f32[2,16,128]{2,1,0:T(8,128)S(1)}, u32[]{:S(2)}, u32[]{:S(2)}) %collective-permute-start.2) | collective-permute-done | bytes 16416 | tf_op jit(solution)/shard_map/ppermute | solution.py:221
  97.8 7.3 %collective-permute-start.3 = (f32[2,16,128]{2,1,0:T(8,128)S(1)}, f32[2,16,128]{2,1,0:T(8,128)S(1)}, u32[]{:S(2)}, u32[]{:S(2)}) collective-permute-start(f32[2,16,128]{2,1,0:T(8,128)S(1)} %get-tuple-element.28), channel_id=1, source_target_pairs={{0,192},{64,128},{128,64},{192,0},{256,448},{320,384},{384,320},{4... | collective-permute-start | bytes 49160 | tf_op jit(solution)/shard_map/ppermute | solution.py:221
  105.1 9.6 %collective-permute-start.4 = (f32[2,16,128]{2,1,0:T(8,128)S(1)}, f32[2,16,128]{2,1,0:T(8,128)S(1)}, u32[]{:S(2)}, u32[]{:S(2)}) collective-permute-start(f32[2,16,128]{2,1,0:T(8,128)S(1)} %get-tuple-element.27), channel_id=1, source_target_pairs={{0,128},{64,192},{128,0},{192,64},{256,384},{320,448},{384,256},{4... | collective-permute-start | bytes 49160 | tf_op jit(solution)/shard_map/ppermute | solution.py:221
  114.7 9.7 %collective-permute-start.5 = (f32[2,16,128]{2,1,0:T(8,128)S(1)}, f32[2,16,128]{2,1,0:T(8,128)S(1)}, u32[]{:S(2)}, u32[]{:S(2)}) collective-permute-start(f32[2,16,128]{2,1,0:T(8,128)S(1)} %get-tuple-element.26), channel_id=1, source_target_pairs={{0,64},{64,0},{128,192},{192,128},{256,320},{320,256},{384,448},{4... | collective-permute-start | bytes 49160 | tf_op jit(solution)/shard_map/ppermute | solution.py:221
  124.6 4.7 %collective-permute-done.4 = f32[2,16,128]{2,1,0:T(8,128)S(1)} collective-permute-done((f32[2,16,128]{2,1,0:T(8,128)S(1)}, f32[2,16,128]{2,1,0:T(8,128)S(1)}, u32[]{:S(2)}, u32[]{:S(2)}) %collective-permute-start.4) | collective-permute-done | bytes 16416 | tf_op jit(solution)/shard_map/ppermute | solution.py:221
  129.3 1.1 collective-permute-done.5
  130.6 2.7 %collective-permute-start.6 = (f32[2,8192]{1,0:T(2,128)S(1)}, f32[2,8192]{1,0:T(2,128)S(1)}, u32[]{:S(2)}, u32[]{:S(2)}) collective-permute-start(f32[2,8192]{1,0:T(2,128)S(1)} %reshape.683), channel_id=1, source_target_pairs={{0,256},{64,320},{128,384},{192,448},{256,0},{320,64},{384,128},{4... | collective-permute-start | bytes 196616 | tf_op jit(solution)/shard_map/ppermute | solution.py:12
  133.3 0.2 convolution_select_fusion.12
  133.5 3.5 %collective-permute-done.6 = f32[2,8192]{1,0:T(2,128)S(1)} collective-permute-done((f32[2,8192]{1,0:T(2,128)S(1)}, f32[2,8192]{1,0:T(2,128)S(1)}, u32[]{:S(2)}, u32[]{:S(2)}) %collective-permute-start.6) | collective-permute-done | bytes 65568 | tf_op jit(solution)/shard_map/ppermute | solution.py:12
  137.1 0.3 fusion.56
  137.4 2.9 %collective-permute-start.7 = (f32[2,8192]{1,0:T(2,128)S(1)}, f32[2,8192]{1,0:T(2,128)S(1)}, u32[]{:S(2)}, u32[]{:S(2)}) collective-permute-start(f32[2,8192]{1,0:T(2,128)S(1)} %reshape.685), channel_id=1, source_target_pairs={{0,512},{64,576},{128,640},{192,704},{256,768},{320,832},{384,896}... | collective-permute-start | bytes 196616 | tf_op jit(solution)/shard_map/ppermute | solution.py:12
  140.3 0.2 convolution_select_fusion.10
  140.6 4.5 %collective-permute-done.7 = f32[2,8192]{1,0:T(2,128)S(1)} collective-permute-done((f32[2,8192]{1,0:T(2,128)S(1)}, f32[2,8192]{1,0:T(2,128)S(1)}, u32[]{:S(2)}, u32[]{:S(2)}) %collective-permute-start.7) | collective-permute-done | bytes 65568 | tf_op jit(solution)/shard_map/ppermute | solution.py:12
  145.2 1.0 fusion.40
  (108 shorter events, 7.2 us)
Async XLA Ops:
  0.0 4.1 %copy-start = (f32[2,1,1,8192]{3,2,1,0:T(1,128)S(1)}, f32[2,1,1,8192]{3,2,1,0:T(1,128)}, u32[]{:S(2)}) copy-start(f32[2,1,1,8192]{3,2,1,0:T(1,128)} %param.7) | copy-start | bytes 196612
  4.1 2.5 %copy-start.1 = (f32[4,2,128,128]{3,2,1,0:T(8,128)S(1)}, f32[4,2,128,128]{3,2,1,0:T(8,128)}, u32[]{:S(2)}) copy-start(f32[4,2,128,128]{3,2,1,0:T(8,128)} %param.8) | copy-start | bytes 1572868
  8.5 3.0 %copy-start.4 = (s32[23]{0:T(128)S(1)}, s32[23]{0:T(128)}, u32[]{:S(2)}) copy-start(s32[23]{0:T(128)} %param.11) | copy-start | bytes 280
  13.2 19.2 %copy-start.2 = (s32[23]{0:T(128)S(1)}, s32[23]{0:T(128)}, u32[]{:S(2)}) copy-start(s32[23]{0:T(128)} %param.10) | copy-start | bytes 280
  13.2 20.1 %copy-start.3 = (f32[2,4,4]{2,1,0:T(4,128)S(1)}, f32[2,4,4]{2,1,0:T(4,128)}, u32[]{:S(2)}) copy-start(f32[2,4,4]{2,1,0:T(4,128)} %param.9) | copy-start | bytes 388
  16.2 28.8 %all-to-all-start = ((f32[2,64,128]{2,0,1:T(2,128)}), f32[2,64,128]{2,0,1:T(2,128)S(1)}, u32[]{:S(2)}, u32[]{:S(2)}) async-start(f32[2,64,128]{2,0,1:T(2,128)} %bitcast.43), calls=%async_computation | async-start | bytes 131072 | tf_op jit(solution)/shard_map/all_to_all | solution.py:314
  36.5 1.1 copy-start.5
  54.4 29.9 %collective-permute-start = (f32[2,16,128]{2,1,0:T(8,128)S(1)}, f32[2,16,128]{2,1,0:T(8,128)S(1)}, u32[]{:S(2)}, u32[]{:S(2)}) collective-permute-start(f32[2,16,128]{2,1,0:T(8,128)S(1)} %get-tuple-element.31), channel_id=1, source_target_pairs={{0,192},{64,128},{128,64},{192,0},{256,448},{320,384},{384,320},{4... | collective-permute-start | bytes 49160 | tf_op jit(solution)/shard_map/ppermute | solution.py:221
  69.9 24.0 %collective-permute-start.1 = (f32[2,16,128]{2,1,0:T(8,128)S(1)}, f32[2,16,128]{2,1,0:T(8,128)S(1)}, u32[]{:S(2)}, u32[]{:S(2)}) collective-permute-start(f32[2,16,128]{2,1,0:T(8,128)S(1)} %get-tuple-element.30), channel_id=1, source_target_pairs={{0,128},{64,192},{128,0},{192,64},{256,384},{320,448},{384,256},{4... | collective-permute-start | bytes 49160 | tf_op jit(solution)/shard_map/ppermute | solution.py:221
  82.2 15.2 %collective-permute-start.2 = (f32[2,16,128]{2,1,0:T(8,128)S(1)}, f32[2,16,128]{2,1,0:T(8,128)S(1)}, u32[]{:S(2)}, u32[]{:S(2)}) collective-permute-start(f32[2,16,128]{2,1,0:T(8,128)S(1)} %get-tuple-element.29), channel_id=1, source_target_pairs={{0,64},{64,0},{128,192},{192,128},{256,320},{320,256},{384,448},{4... | collective-permute-start | bytes 49160 | tf_op jit(solution)/shard_map/ppermute | solution.py:221
  97.8 26.9 %collective-permute-start.3 = (f32[2,16,128]{2,1,0:T(8,128)S(1)}, f32[2,16,128]{2,1,0:T(8,128)S(1)}, u32[]{:S(2)}, u32[]{:S(2)}) collective-permute-start(f32[2,16,128]{2,1,0:T(8,128)S(1)} %get-tuple-element.28), channel_id=1, source_target_pairs={{0,192},{64,128},{128,64},{192,0},{256,448},{320,384},{384,320},{4... | collective-permute-start | bytes 49160 | tf_op jit(solution)/shard_map/ppermute | solution.py:221
  105.1 24.2 %collective-permute-start.4 = (f32[2,16,128]{2,1,0:T(8,128)S(1)}, f32[2,16,128]{2,1,0:T(8,128)S(1)}, u32[]{:S(2)}, u32[]{:S(2)}) collective-permute-start(f32[2,16,128]{2,1,0:T(8,128)S(1)} %get-tuple-element.27), channel_id=1, source_target_pairs={{0,128},{64,192},{128,0},{192,64},{256,384},{320,448},{384,256},{4... | collective-permute-start | bytes 49160 | tf_op jit(solution)/shard_map/ppermute | solution.py:221
  114.7 15.7 %collective-permute-start.5 = (f32[2,16,128]{2,1,0:T(8,128)S(1)}, f32[2,16,128]{2,1,0:T(8,128)S(1)}, u32[]{:S(2)}, u32[]{:S(2)}) collective-permute-start(f32[2,16,128]{2,1,0:T(8,128)S(1)} %get-tuple-element.26), channel_id=1, source_target_pairs={{0,64},{64,0},{128,192},{192,128},{256,320},{320,256},{384,448},{4... | collective-permute-start | bytes 49160 | tf_op jit(solution)/shard_map/ppermute | solution.py:221
  130.6 6.4 %collective-permute-start.6 = (f32[2,8192]{1,0:T(2,128)S(1)}, f32[2,8192]{1,0:T(2,128)S(1)}, u32[]{:S(2)}, u32[]{:S(2)}) collective-permute-start(f32[2,8192]{1,0:T(2,128)S(1)} %reshape.683), channel_id=1, source_target_pairs={{0,256},{64,320},{128,384},{192,448},{256,0},{320,64},{384,128},{4... | collective-permute-start | bytes 196616 | tf_op jit(solution)/shard_map/ppermute | solution.py:12
  137.4 7.7 %collective-permute-start.7 = (f32[2,8192]{1,0:T(2,128)S(1)}, f32[2,8192]{1,0:T(2,128)S(1)}, u32[]{:S(2)}, u32[]{:S(2)}) collective-permute-start(f32[2,8192]{1,0:T(2,128)S(1)} %reshape.685), channel_id=1, source_target_pairs={{0,512},{64,576},{128,640},{192,704},{256,768},{320,832},{384,896}... | collective-permute-start | bytes 196616 | tf_op jit(solution)/shard_map/ppermute | solution.py:12

commit v6 on v4

--- a/solution.py
+++ b/solution.py
@@ -179,6 +179,55 @@
     return out.reshape(2, length)
 
 
+def gathered_pair_gates(values, local_bits, group_bits, matrix):
+    length = values.shape[1]
+    groups = 2**group_bits
+    field = 2**group_bits
+    rest = length // field
+    own = lax.axis_index("grp")
+    gathered = lax.all_gather(values, "grp", axis=0, tiled=False)
+    block = gathered.reshape(groups, 2, field, rest).transpose(1, 0, 2, 3)
+    block = block.reshape(2, groups * field, rest)
+    out_place = jnp.arange(field, dtype=jnp.int32)
+    in_place = jnp.arange(groups * field, dtype=jnp.int32)
+    states = jnp.arange(4, dtype=jnp.int32)
+    real_part = None
+    imag_part = None
+    for bit_num in range(group_bits):
+        c_bit = group_bits - 1 - bit_num
+        out_state = (jnp.right_shift(own, bit_num) & 1) + 2 * (
+            jnp.right_shift(out_place, c_bit) & 1
+        )
+        in_state = (jnp.right_shift(in_place, group_bits + bit_num) & 1) + 2 * (
+            jnp.right_shift(in_place, c_bit) & 1
+        )
+        pick_out = (out_state[:, None] == states[None, :]).astype(jnp.float32)
+        pick_in = (in_state[:, None] == states[None, :]).astype(jnp.float32)
+        factor_re = jnp.dot(jnp.dot(pick_out, matrix[0], precision=HIGHEST), pick_in.T, precision=HIGHEST)
+        factor_im = jnp.dot(jnp.dot(pick_out, matrix[1], precision=HIGHEST), pick_in.T, precision=HIGHEST)
+        if real_part is None:
+            real_part, imag_part = factor_re, factor_im
+        else:
+            real_part, imag_part = (
+                real_part * factor_re - imag_part * factor_im,
+                real_part * factor_im + imag_part * factor_re,
+            )
+    operator = jnp.concatenate(
+        [
+            jnp.concatenate([real_part, -imag_part], axis=1),
+            jnp.concatenate([imag_part, real_part], axis=1),
+        ],
+        axis=0,
+    )
+    out = jnp.dot(
+        operator,
+        block.reshape(2 * groups * field, rest),
+        precision=HIGHEST,
+        preferred_element_type=jnp.float32,
+    )
+    return out.reshape(2, length)
+
+
 def pair_operator(matrix, group_bits):
     size = 2 ** (2 * group_bits)
     place = jnp.arange(size, dtype=jnp.int32)
@@ -260,8 +309,7 @@
         ).reshape(2, length)
     values = reorder(values, position_of(layout, layout_out[:local_bits]))
     values = values * spare_sign(length, spare_values)
-    for bit_num in range(group_bits):
-        values = pair_exchange(values, local_bits - 1 - bit_num, bit_num, pair_gate)
+    values = gathered_pair_gates(values, local_bits, group_bits, pair_gate)
     return values.reshape(amplitudes.shape)
 
 

time: 131 us -> 201 us (1.53)
  waiting for transfers between devices: 36.9 us -> 134 us
  starting transfers between devices: 55.9 us -> 16.2 us
  between operations: 0.66 us -> 13.8 us
  matrix products: 26.3 us -> 23.3 us
  local copies, waits for them, and re-layouts: 2.19 us -> 4.65 us
    all_gather x0 -> x1, waiting for transfers between devices: none -> 127 us  [gathered_pair_gates(): gathered = lax.all_gather(values, 'grp', axis=0, tiled=False)]
    ppermute x4 -> x0, starting transfers between devices: 39.7 us -> none  [swapped(): return lax.ppermute(value, axis, pairs)]
    ppermute x4 -> x0, waiting for transfers between devices: 32.8 us -> none  [swapped(): return lax.ppermute(value, axis, pairs)]
    dot_general x28 -> x17, matrix products: 7.48 us -> 4.42 us  [the longest x4 1.08 us: gathered_pair_gates(): jnp.dot(jnp.dot(pick_out, matrix[1], precision=HIGHEST), pick_in.T, preci...]
    all_to_all x1, waiting for transfers between devices: 4.13 us -> 7.09 us  [per_device(): lax.all_to_all(shaped, 'dev', split_axis=1, concat_axis=1, tiled=True)]
  transfers between devices with their start and end apart: 5 -> 2, of which waited for: 5 -> 2; matrix products, arithmetic and copies ran while one was open for 7% -> 4% of each run, Pallas kernels for 0% -> 0%
where the time goes in v6:
time: 201 us
  waiting for transfers between devices  134 us (67%)
  matrix products  23.3 us (12%)
  starting transfers between devices  16.2 us (8%)
  between operations  13.8 us (7%)
  other arithmetic  8.85 us (4%)
  local copies, waits for them, and re-layouts  4.65 us (2%)
    all_gather x1, waiting for transfers between devices, gathered_pair_gates(): gathered = lax.all_gather(values, 'grp', axis=0, tiled=False)  127 us
    all_to_all x1, starting transfers between devices, per_device(): lax.all_to_all(shaped, 'dev', split_axis=1, concat_axis=1, tiled=True)  16 us
    dot_general x6, matrix products, reorder(): jnp.dot(values.reshape(2 * rows, lanes), one_hot, precision=HIGHEST, pref...  15 us
    all_to_all x1, waiting for transfers between devices, per_device(): lax.all_to_all(shaped, 'dev', split_axis=1, concat_axis=1, tiled=True)  7.09 us
  transfers between devices with their start and end apart: 2, of which 2 were waited for; matrix products, arithmetic and copies ran while one was open for 4% of the time, Pallas kernels for 0%

profile of v6, /device:TPU:24, one launch (start us, length us, event | category | flops | bytes accessed | tf_op | source)
XLA Modules:
  0.0 200.6 jit_solution(8231063767831381916)
XLA Ops:
  6.5 0.8 slice_bitcast_fusion
  7.4 0.7 compare_reduce_fusion.4
  8.1 0.7 fusion.137
  8.9 0.2 reduce-window.40
  9.1 0.8 select_reduce_fusion.1
  10.3 0.3 iota_compare_fusion.7
  10.6 2.4 %select_reduce_fusion = f32[2,8192]{1,0:T(2,128)S(1)} fusion(pred[64,8192]{1,0:T(8,128)(4,1)S(1)} %iota_compare_fusion.7, f32[128,128]{1,0:T(8,128)S(1)} %bitcast.213, s32[8192]{0:T(1024)S(1)} %get-tuple-element.33), kind=kOutput, calls=%fused_computation.10 | convolution fusion | flops 1613742080 | bytes 688128 | tf_op jit(solution)/shard_map/dot_general | solution.py:41
  13.1 0.2 fusion.86
  13.4 0.2 fusion.90
  13.6 0.2 reduce-window.41
  13.8 0.1 select_reduce_fusion.2
  14.2 0.3 iota_compare_fusion.8
  14.5 0.2 fusion.38
  14.8 0.2 fusion.39
  15.0 2.4 %fusion.17 = f32[2,8192]{1,0:T(2,128)S(1)} fusion(s32[8192]{0:T(1024)S(1)} %get-tuple-element.36, pred[64,8192]{1,0:T(8,128)(4,1)S(1)} %iota_compare_fusion.8, f32[1,64,128]{2,1,0:T(8,128)S(1)} %fusion.38, f32[1,64,128]{2,1,0:T(8,128)S(1)} %fusion.39), kind=kOutput, calls=%fused_computation.30 | convolution fusion | flops 1613758464 | bytes 688128 | tf_op jit(solution)/shard_map/dot_general | solution.py:41
  17.5 0.2 fusion.84
  17.8 0.2 fusion.80
  18.3 0.2 fusion.37
  18.5 0.2 fusion.36
  18.8 0.2 reduce-window.42
  19.0 0.1 select_reduce_fusion.3
  19.4 0.3 iota_compare_fusion.9
  19.7 3.0 %fusion.20 = f32[2,8192]{1,0:T(2,128)} fusion(s32[8192]{0:T(1024)S(1)} %get-tuple-element.38, pred[64,8192]{1,0:T(8,128)(4,1)S(1)} %iota_compare_fusion.9, f32[1,64,128]{2,1,0:T(8,128)S(1)} %fusion.36, f32[1,64,128]{2,1,0:T(8,128)S(1)} %fusion.37), kind=kOutput, calls=%fused_computation.31 | convolution fusion | flops 1613758464 | bytes 688128 | tf_op jit(solution)/shard_map/dot_general | solution.py:41
  22.8 16.0 %all-to-all-start = ((f32[2,64,128]{2,0,1:T(2,128)}), f32[2,64,128]{2,0,1:T(2,128)S(1)}, u32[]{:S(2)}, u32[]{:S(2)}) async-start(f32[2,64,128]{2,0,1:T(2,128)} %bitcast.42), calls=%async_computation | async-start | bytes 131072 | tf_op jit(solution)/shard_map/all_to_all | solution.py:299
  38.8 0.2 all-gather.2.cloned.1.call-start
  39.3 0.2 reduce-window.43
  39.9 0.2 fusion.133
  40.0 0.2 fusion.134
  40.3 0.2 fusion.136
  40.5 0.2 fusion.135
  40.7 0.2 fusion.131
  40.9 0.2 fusion.132
  41.4 0.3 iota_compare_fusion.10
  41.7 0.2 reduce-window.44
  42.4 0.3 iota_compare_fusion.11
  42.6 0.2 select_reduce_fusion.6
  43.2 0.3 iota_compare_fusion.12
  43.8 0.2 fusion.129
  44.0 0.2 fusion.130
  44.2 0.2 fusion.44
  44.4 7.1 %all-to-all-done = f32[2,64,128]{2,0,1:T(2,128)S(1)} async-done(((f32[2,64,128]{2,0,1:T(2,128)}), f32[2,64,128]{2,0,1:T(2,128)S(1)}, u32[]{:S(2)}, u32[]{:S(2)}) %all-to-all-start) | async-done | bytes 65568 | tf_op jit(solution)/shard_map/all_to_all | solution.py:299
  51.5 2.4 %fusion.23 = f32[2,8192]{1,0:T(2,128)S(1)} fusion(s32[8192]{0:T(1024)S(1)} %get-tuple-element.40, pred[64,8192]{1,0:T(8,128)(4,1)S(1)} %iota_compare_fusion.10, f32[2,64,128]{2,0,1:T(2,128)S(1)} %all-to-all-done), kind=kOutput, calls=%fused_computation.32 | convolution fusion | flops 1613742080 | bytes 688128 | tf_op jit(solution)/shard_map/dot_general | solution.py:41
  54.0 0.2 fusion.78
  54.2 0.2 fusion.74
  54.5 0.2 fusion.35
  54.7 0.2 fusion.34
  55.0 2.4 %fusion.26 = f32[2,8192]{1,0:T(2,128)S(1)} fusion(s32[8192]{0:T(1024)S(1)} %get-tuple-element.42, pred[64,8192]{1,0:T(8,128)(4,1)S(1)} %iota_compare_fusion.11, f32[1,64,128]{2,1,0:T(8,128)S(1)} %fusion.34, f32[1,64,128]{2,1,0:T(8,128)S(1)} %fusion.35), kind=kOutput, calls=%fused_computation.33 | convolution fusion | flops 1613758464 | bytes 688128 | tf_op jit(solution)/shard_map/dot_general | solution.py:41
  57.4 0.2 fusion.72
  57.7 0.2 fusion.68
  57.9 0.2 fusion.33
  58.2 0.2 fusion.32
  58.4 2.4 %fusion.29 = f32[2,8192]{1,0:T(2,128)S(1)} fusion(s32[8192]{0:T(1024)S(1)} %get-tuple-element.44, pred[64,8192]{1,0:T(8,128)(4,1)S(1)} %iota_compare_fusion.12, f32[1,64,128]{2,1,0:T(8,128)S(1)} %fusion.32, f32[1,64,128]{2,1,0:T(8,128)S(1)} %fusion.33), kind=kOutput, calls=%fused_computation.34 | convolution fusion | flops 1613758464 | bytes 688128 | tf_op jit(solution)/shard_map/dot_general | solution.py:41
  60.8 0.7 bitcast_multiply_fusion
  61.5 0.2 fusion.45
  61.7 0.3 fusion.42
  62.0 0.3 fusion.43
  62.3 0.3 fusion.47
  62.6 0.3 fusion.40
  62.8 0.3 multiply_subtract_fusion.2
  63.1 0.3 fusion.192
  63.5 126.7 %all-gather.2.cloned.1.call-done = f32[16,2,8192]{2,1,0:T(2,128)} async-done(((f32[1,2,8192]{2,1,0:T(2,128)}), f32[16,2,8192]{2,1,0:T(2,128)}) %all-gather.2.cloned.1.call-update) | async-done | bytes 1048592 | tf_op jit(solution)/shard_map/all_gather | solution.py:188
  190.1 2.1 %reshape.704 = f32[16,2,16,512]{3,2,1,0:T(8,128)S(1)} reshape(f32[16,2,8192]{2,1,0:T(2,128)} %all-gather.2.cloned.1.call-done) | data formatting | bytes 2097152 | tf_op jit(solution)/shard_map/reshape | solution.py:189
  192.4 0.7 fusion.48
  193.1 0.7 reshape_reshape.17
  (80 shorter events, 3.9 us)
Async XLA Ops:
  6.5 4.1 %copy-start = (f32[2,1,1,8192]{3,2,1,0:T(1,128)S(1)}, f32[2,1,1,8192]{3,2,1,0:T(1,128)}, u32[]{:S(2)}) copy-start(f32[2,1,1,8192]{3,2,1,0:T(1,128)} %param.7) | copy-start | bytes 196612
  6.5 6.6 %copy-start.1 = (f32[4,2,128,128]{3,2,1,0:T(8,128)S(1)}, f32[4,2,128,128]{3,2,1,0:T(8,128)}, u32[]{:S(2)}) copy-start(f32[4,2,128,128]{3,2,1,0:T(8,128)} %param.8) | copy-start | bytes 1572868
  15.0 3.0 %copy-start.4 = (s32[23]{0:T(128)S(1)}, s32[23]{0:T(128)}, u32[]{:S(2)}) copy-start(s32[23]{0:T(128)} %param.11) | copy-start | bytes 280
  19.7 19.3 %copy-start.2 = (s32[23]{0:T(128)S(1)}, s32[23]{0:T(128)}, u32[]{:S(2)}) copy-start(s32[23]{0:T(128)} %param.10) | copy-start | bytes 280
  19.7 20.1 %copy-start.3 = (f32[2,4,4]{2,1,0:T(4,128)S(1)}, f32[2,4,4]{2,1,0:T(4,128)}, u32[]{:S(2)}) copy-start(f32[2,4,4]{2,1,0:T(4,128)} %param.9) | copy-start | bytes 388
  22.8 28.8 %all-to-all-start = ((f32[2,64,128]{2,0,1:T(2,128)}), f32[2,64,128]{2,0,1:T(2,128)S(1)}, u32[]{:S(2)}, u32[]{:S(2)}) async-start(f32[2,64,128]{2,0,1:T(2,128)} %bitcast.42), calls=%async_computation | async-start | bytes 131072 | tf_op jit(solution)/shard_map/all_to_all | solution.py:299
  38.8 151.4 %all-gather.2.cloned.1.call-start = ((), (), s32[]{:S(2)}) async-start(), calls=%async_computation.1 | async-start | bytes 1114112 | tf_op jit(solution)/shard_map/all_gather | solution.py:188
  40.5 3.0 %copy-start.5 = (s32[10]{0:T(128)S(1)}, s32[10]{0:T(128)}, u32[]{:S(2)}) copy-start(s32[10]{0:T(128)} %param.13) | copy-start | bytes 124
Sparse Core Ops, SparseCore 0:
  61.6 128.4 all-gather.1

commit v7 on v4

--- a/solution.py
+++ b/solution.py
@@ -260,8 +260,16 @@
         ).reshape(2, length)
     values = reorder(values, position_of(layout, layout_out[:local_bits]))
     values = values * spare_sign(length, spare_values)
-    for bit_num in range(group_bits):
-        values = pair_exchange(values, local_bits - 1 - bit_num, bit_num, pair_gate)
+    split_bit = 7
+    shaped = values.reshape(2, length >> split_bit + 1, 2, 1 << split_bit)
+    orders = (tuple(range(group_bits)), tuple(reversed(range(group_bits))))
+    halves_out = []
+    for half_num in range(2):
+        half = shaped[:, :, half_num].reshape(2, length // 2)
+        for bit_num in orders[half_num]:
+            half = pair_exchange(half, local_bits - 2 - bit_num, bit_num, pair_gate)
+        halves_out.append(half.reshape(2, length >> split_bit + 1, 1 << split_bit))
+    values = jnp.stack(halves_out, axis=2).reshape(2, length)
     return values.reshape(amplitudes.shape)
 
 

time: 131 us -> 146 us (1.11)
  starting transfers between devices: 55.9 us -> 88.8 us
  waiting for transfers between devices: 36.9 us -> 18 us
    ppermute x4 -> x8, starting transfers between devices: 39.7 us -> 72.6 us  [swapped(): return lax.ppermute(value, axis, pairs)]
    ppermute x4 -> x8, waiting for transfers between devices: 32.8 us -> 14.1 us  [swapped(): return lax.ppermute(value, axis, pairs)]
  transfers between devices with their start and end apart: 5 -> 9, of which waited for: 5 -> 5; matrix products, arithmetic and copies ran while one was open for 7% -> 8% of each run, Pallas kernels for 0% -> 0%
where the time goes in v7:
time: 146 us; the launch traced here: 145 us
  starting transfers between devices  88.8 us (61%)
  matrix products  26 us (18%)
  waiting for transfers between devices  18 us (12%)
  other arithmetic  8.17 us (6%)
  local copies, waits for them, and re-layouts  3.22 us (2%)
    ppermute x8, starting transfers between devices, swapped(): return lax.ppermute(value, axis, pairs)  72.6 us
    all_to_all x1, starting transfers between devices, per_device(): lax.all_to_all(shaped, 'dev', split_axis=1, concat_axis=1, tiled=True)  16.2 us
    dot_general x6, matrix products, reorder(): jnp.dot(values.reshape(2 * rows, lanes), one_hot, precision=HIGHEST, pref...  15 us
    ppermute x8, waiting for transfers between devices, swapped(): return lax.ppermute(value, axis, pairs)  14.1 us
    all_to_all x1, waiting for transfers between devices, per_device(): lax.all_to_all(shaped, 'dev', split_axis=1, concat_axis=1, tiled=True)  3.83 us
    dot_general x16, matrix products, pair_exchange(): jnp.dot(jnp.dot(pick_out, matrix[part], precision=HIGHEST), pick_in.T, pr...  3.65 us
  transfers between devices with their start and end apart: 9, of which 5 were waited for; matrix products, arithmetic and copies ran while one was open for 8% of the time, Pallas kernels for 0%

profile of v7, /device:TPU:24, one launch (start us, length us, event | category | flops | bytes accessed | tf_op | source)
XLA Modules:
  0.0 144.9 jit_solution(16253968744348929314)
XLA Ops:
  0.0 0.8 slice_bitcast_fusion
  0.8 0.7 compare_reduce_fusion.4
  1.6 0.7 fusion.169
  2.5 0.8 select_reduce_fusion.1
  3.8 0.3 iota_compare_fusion.7
  4.1 2.4 %select_reduce_fusion = f32[2,8192]{1,0:T(2,128)S(1)} fusion(pred[64,8192]{1,0:T(8,128)(4,1)S(1)} %iota_compare_fusion.7, f32[128,128]{1,0:T(8,128)S(1)} %bitcast.225, s32[8192]{0:T(1024)S(1)} %get-tuple-element.31), kind=kOutput, calls=%fused_computation.10 | convolution fusion | flops 1613742080 | bytes 688128 | tf_op jit(solution)/shard_map/dot_general | solution.py:41
  6.6 0.2 fusion.102
  6.8 0.2 fusion.106
  7.7 0.3 iota_compare_fusion.8
  8.0 0.2 fusion.38
  8.3 0.2 fusion.39
  8.5 2.4 %fusion.17 = f32[2,8192]{1,0:T(2,128)S(1)} fusion(s32[8192]{0:T(1024)S(1)} %get-tuple-element.34, pred[64,8192]{1,0:T(8,128)(4,1)S(1)} %iota_compare_fusion.8, f32[1,64,128]{2,1,0:T(8,128)S(1)} %fusion.38, f32[1,64,128]{2,1,0:T(8,128)S(1)} %fusion.39), kind=kOutput, calls=%fused_computation.30 | convolution fusion | flops 1613758464 | bytes 688128 | tf_op jit(solution)/shard_map/dot_general | solution.py:41
  11.0 0.2 fusion.100
  11.2 0.2 fusion.96
  11.7 0.2 fusion.37
  12.0 0.2 fusion.36
  12.9 0.3 iota_compare_fusion.9
  13.2 3.0 %fusion.20 = f32[2,8192]{1,0:T(2,128)} fusion(s32[8192]{0:T(1024)S(1)} %get-tuple-element.36, pred[64,8192]{1,0:T(8,128)(4,1)S(1)} %iota_compare_fusion.9, f32[1,64,128]{2,1,0:T(8,128)S(1)} %fusion.36, f32[1,64,128]{2,1,0:T(8,128)S(1)} %fusion.37), kind=kOutput, calls=%fused_computation.31 | convolution fusion | flops 1613758464 | bytes 688128 | tf_op jit(solution)/shard_map/dot_general | solution.py:41
  16.2 16.2 %all-to-all-start = ((f32[2,64,128]{2,0,1:T(2,128)}), f32[2,64,128]{2,0,1:T(2,128)S(1)}, u32[]{:S(2)}, u32[]{:S(2)}) async-start(f32[2,64,128]{2,0,1:T(2,128)} %bitcast.42), calls=%async_computation | async-start | bytes 131072 | tf_op jit(solution)/shard_map/all_to_all | solution.py:250
  33.7 0.2 fusion.218
  33.9 0.2 fusion.217
  35.0 0.2 fusion.216
  35.3 0.2 fusion.215
  36.4 0.2 fusion.214
  36.6 0.2 fusion.213
  37.6 0.3 iota_compare_fusion.10
  38.6 0.3 iota_compare_fusion.11
  39.4 0.3 iota_compare_fusion.12
  40.3 0.2 convolution_select_fusion.20
  40.7 0.2 fusion.212
  40.9 0.2 fusion.211
  41.2 3.8 %all-to-all-done = f32[2,64,128]{2,0,1:T(2,128)S(1)} async-done(((f32[2,64,128]{2,0,1:T(2,128)}), f32[2,64,128]{2,0,1:T(2,128)S(1)}, u32[]{:S(2)}, u32[]{:S(2)}) %all-to-all-start) | async-done | bytes 65568 | tf_op jit(solution)/shard_map/all_to_all | solution.py:250
  45.0 2.4 %fusion.23 = f32[2,8192]{1,0:T(2,128)S(1)} fusion(s32[8192]{0:T(1024)S(1)} %get-tuple-element.38, pred[64,8192]{1,0:T(8,128)(4,1)S(1)} %iota_compare_fusion.10, f32[2,64,128]{2,0,1:T(2,128)S(1)} %all-to-all-done), kind=kOutput, calls=%fused_computation.32 | convolution fusion | flops 1613742080 | bytes 688128 | tf_op jit(solution)/shard_map/dot_general | solution.py:41
  47.5 0.2 fusion.94
  47.7 0.2 fusion.90
  47.9 0.2 fusion.35
  48.2 0.2 fusion.34
  48.4 2.4 %fusion.26 = f32[2,8192]{1,0:T(2,128)S(1)} fusion(s32[8192]{0:T(1024)S(1)} %get-tuple-element.40, pred[64,8192]{1,0:T(8,128)(4,1)S(1)} %iota_compare_fusion.11, f32[1,64,128]{2,1,0:T(8,128)S(1)} %fusion.34, f32[1,64,128]{2,1,0:T(8,128)S(1)} %fusion.35), kind=kOutput, calls=%fused_computation.33 | convolution fusion | flops 1613758464 | bytes 688128 | tf_op jit(solution)/shard_map/dot_general | solution.py:41
  50.9 0.2 fusion.88
  51.1 0.2 fusion.84
  51.4 0.2 fusion.33
  51.6 0.2 fusion.32
  51.9 2.4 %fusion.29 = f32[2,8192]{1,0:T(2,128)S(1)} fusion(s32[8192]{0:T(1024)S(1)} %get-tuple-element.42, pred[64,8192]{1,0:T(8,128)(4,1)S(1)} %iota_compare_fusion.12, f32[1,64,128]{2,1,0:T(8,128)S(1)} %fusion.32, f32[1,64,128]{2,1,0:T(8,128)S(1)} %fusion.33), kind=kOutput, calls=%fused_computation.34 | convolution fusion | flops 1613758464 | bytes 688128 | tf_op jit(solution)/shard_map/dot_general | solution.py:41
  54.6 15.7 %collective-permute-start = (f32[2,4096]{1,0:T(2,128)S(1)}, f32[2,4096]{1,0:T(2,128)S(1)}, u32[]{:S(2)}, u32[]{:S(2)}) collective-permute-start(f32[2,4096]{1,0:T(2,128)S(1)} %bitcast.252), channel_id=1, source_target_pairs={{0,64},{64,0},{128,192},{192,128},{256,320},{320,256},{384,448},{4... | collective-permute-start | bytes 98312 | tf_op jit(solution)/shard_map/ppermute | solution.py:12
  70.6 3.1 %collective-permute-start.4 = (f32[2,4096]{1,0:T(2,128)S(1)}, f32[2,4096]{1,0:T(2,128)S(1)}, u32[]{:S(2)}, u32[]{:S(2)}) collective-permute-start(f32[2,4096]{1,0:T(2,128)S(1)} %bitcast.251), channel_id=1, source_target_pairs={{0,512},{64,576},{128,640},{192,704},{256,768},{320,832},{384,896}... | collective-permute-start | bytes 98312 | tf_op jit(solution)/shard_map/ppermute | solution.py:12
  73.8 3.0 %collective-permute-done = f32[2,4096]{1,0:T(2,128)S(1)} collective-permute-done((f32[2,4096]{1,0:T(2,128)S(1)}, f32[2,4096]{1,0:T(2,128)S(1)}, u32[]{:S(2)}, u32[]{:S(2)}) %collective-permute-start) | collective-permute-done | bytes 32800 | tf_op jit(solution)/shard_map/ppermute | solution.py:12
  76.8 0.2 fusion.52
  77.0 18.1 %collective-permute-start.1 = (f32[2,4096]{1,0:T(2,128)S(1)}, f32[2,4096]{1,0:T(2,128)S(1)}, u32[]{:S(2)}, u32[]{:S(2)}) collective-permute-start(f32[2,4096]{1,0:T(2,128)S(1)} %reshape.723), channel_id=1, source_target_pairs={{0,128},{64,192},{128,0},{192,64},{256,384},{320,448},{384,256},{4... | collective-permute-start | bytes 98312 | tf_op jit(solution)/shard_map/ppermute | solution.py:12
  95.2 0.2 fusion.68
  95.5 2.7 %collective-permute-start.5 = (f32[2,4096]{1,0:T(2,128)S(1)}, f32[2,4096]{1,0:T(2,128)S(1)}, u32[]{:S(2)}, u32[]{:S(2)}) collective-permute-start(f32[2,4096]{1,0:T(2,128)S(1)} %reshape.730), channel_id=1, source_target_pairs={{0,256},{64,320},{128,384},{192,448},{256,0},{320,64},{384,128},{4... | collective-permute-start | bytes 98312 | tf_op jit(solution)/shard_map/ppermute | solution.py:12
  98.1 3.1 %collective-permute-done.1 = f32[2,4096]{1,0:T(2,128)S(1)} collective-permute-done((f32[2,4096]{1,0:T(2,128)S(1)}, f32[2,4096]{1,0:T(2,128)S(1)}, u32[]{:S(2)}, u32[]{:S(2)}) %collective-permute-start.1) | collective-permute-done | bytes 32800 | tf_op jit(solution)/shard_map/ppermute | solution.py:12
  101.3 0.2 fusion.56
  101.6 2.7 %collective-permute-start.2 = (f32[2,4096]{1,0:T(2,128)S(1)}, f32[2,4096]{1,0:T(2,128)S(1)}, u32[]{:S(2)}, u32[]{:S(2)}) collective-permute-start(f32[2,4096]{1,0:T(2,128)S(1)} %reshape.725), channel_id=1, source_target_pairs={{0,256},{64,320},{128,384},{192,448},{256,0},{320,64},{384,128},{4... | collective-permute-start | bytes 98312 | tf_op jit(solution)/shard_map/ppermute | solution.py:12
  104.3 0.2 fusion.72
  104.6 18.6 %collective-permute-start.6 = (f32[2,4096]{1,0:T(2,128)S(1)}, f32[2,4096]{1,0:T(2,128)S(1)}, u32[]{:S(2)}, u32[]{:S(2)}) collective-permute-start(f32[2,4096]{1,0:T(2,128)S(1)} %reshape.732), channel_id=1, source_target_pairs={{0,128},{64,192},{128,0},{192,64},{256,384},{320,448},{384,256},{4... | collective-permute-start | bytes 98312 | tf_op jit(solution)/shard_map/ppermute | solution.py:12
  123.2 0.2 fusion.60
  123.5 3.9 %collective-permute-start.3 = (f32[2,4096]{1,0:T(2,128)S(1)}, f32[2,4096]{1,0:T(2,128)S(1)}, u32[]{:S(2)}, u32[]{:S(2)}) collective-permute-start(f32[2,4096]{1,0:T(2,128)S(1)} %reshape.727), channel_id=1, source_target_pairs={{0,512},{64,576},{128,640},{192,704},{256,768},{320,832},{384,896}... | collective-permute-start | bytes 98312 | tf_op jit(solution)/shard_map/ppermute | solution.py:12
  127.4 1.7 %collective-permute-done.6 = f32[2,4096]{1,0:T(2,128)S(1)} collective-permute-done((f32[2,4096]{1,0:T(2,128)S(1)}, f32[2,4096]{1,0:T(2,128)S(1)}, u32[]{:S(2)}, u32[]{:S(2)}) %collective-permute-start.6) | collective-permute-done | bytes 32800 | tf_op jit(solution)/shard_map/ppermute | solution.py:12
  129.1 0.2 fusion.76
  129.4 7.9 %collective-permute-start.7 = (f32[2,4096]{1,0:T(2,128)S(1)}, f32[2,4096]{1,0:T(2,128)S(1)}, u32[]{:S(2)}, u32[]{:S(2)}) collective-permute-start(f32[2,4096]{1,0:T(2,128)S(1)} %reshape.734), channel_id=1, source_target_pairs={{0,64},{64,0},{128,192},{192,128},{256,320},{320,256},{384,448},{4... | collective-permute-start | bytes 98312 | tf_op jit(solution)/shard_map/ppermute | solution.py:12
  137.3 0.2 fusion.64
  137.5 6.4 %collective-permute-done.7 = f32[2,4096]{1,0:T(2,128)S(1)} collective-permute-done((f32[2,4096]{1,0:T(2,128)S(1)}, f32[2,4096]{1,0:T(2,128)S(1)}, u32[]{:S(2)}, u32[]{:S(2)}) %collective-permute-start.7) | collective-permute-done | bytes 32800 | tf_op jit(solution)/shard_map/ppermute | solution.py:12
  143.9 0.2 fusion.80
  144.2 0.7 copy.13
  (124 shorter events, 9.1 us)
Async XLA Ops:
  0.0 4.1 %copy-start = (f32[2,1,1,8192]{3,2,1,0:T(1,128)S(1)}, f32[2,1,1,8192]{3,2,1,0:T(1,128)}, u32[]{:S(2)}) copy-start(f32[2,1,1,8192]{3,2,1,0:T(1,128)} %param.7) | copy-start | bytes 196612
  4.1 2.5 %copy-start.1 = (f32[4,2,128,128]{3,2,1,0:T(8,128)S(1)}, f32[4,2,128,128]{3,2,1,0:T(8,128)}, u32[]{:S(2)}) copy-start(f32[4,2,128,128]{3,2,1,0:T(8,128)} %param.8) | copy-start | bytes 1572868
  8.5 3.0 %copy-start.4 = (s32[23]{0:T(128)S(1)}, s32[23]{0:T(128)}, u32[]{:S(2)}) copy-start(s32[23]{0:T(128)} %param.11) | copy-start | bytes 280
  13.2 19.2 %copy-start.2 = (s32[23]{0:T(128)S(1)}, s32[23]{0:T(128)}, u32[]{:S(2)}) copy-start(s32[23]{0:T(128)} %param.10) | copy-start | bytes 280
  13.2 20.1 %copy-start.3 = (f32[2,4,4]{2,1,0:T(4,128)S(1)}, f32[2,4,4]{2,1,0:T(4,128)}, u32[]{:S(2)}) copy-start(f32[2,4,4]{2,1,0:T(4,128)} %param.9) | copy-start | bytes 388
  16.2 28.8 %all-to-all-start = ((f32[2,64,128]{2,0,1:T(2,128)}), f32[2,64,128]{2,0,1:T(2,128)S(1)}, u32[]{:S(2)}, u32[]{:S(2)}) async-start(f32[2,64,128]{2,0,1:T(2,128)} %bitcast.42), calls=%async_computation | async-start | bytes 131072 | tf_op jit(solution)/shard_map/all_to_all | solution.py:250
  38.6 1.1 copy-start.5
  54.6 22.1 %collective-permute-start = (f32[2,4096]{1,0:T(2,128)S(1)}, f32[2,4096]{1,0:T(2,128)S(1)}, u32[]{:S(2)}, u32[]{:S(2)}) collective-permute-start(f32[2,4096]{1,0:T(2,128)S(1)} %bitcast.252), channel_id=1, source_target_pairs={{0,64},{64,0},{128,192},{192,128},{256,320},{320,256},{384,448},{4... | collective-permute-start | bytes 98312 | tf_op jit(solution)/shard_map/ppermute | solution.py:12
  70.6 24.5 %collective-permute-start.4 = (f32[2,4096]{1,0:T(2,128)S(1)}, f32[2,4096]{1,0:T(2,128)S(1)}, u32[]{:S(2)}, u32[]{:S(2)}) collective-permute-start(f32[2,4096]{1,0:T(2,128)S(1)} %bitcast.251), channel_id=1, source_target_pairs={{0,512},{64,576},{128,640},{192,704},{256,768},{320,832},{384,896}... | collective-permute-start | bytes 98312 | tf_op jit(solution)/shard_map/ppermute | solution.py:12
  77.0 24.2 %collective-permute-start.1 = (f32[2,4096]{1,0:T(2,128)S(1)}, f32[2,4096]{1,0:T(2,128)S(1)}, u32[]{:S(2)}, u32[]{:S(2)}) collective-permute-start(f32[2,4096]{1,0:T(2,128)S(1)} %reshape.723), channel_id=1, source_target_pairs={{0,128},{64,192},{128,0},{192,64},{256,384},{320,448},{384,256},{4... | collective-permute-start | bytes 98312 | tf_op jit(solution)/shard_map/ppermute | solution.py:12
  95.5 8.8 %collective-permute-start.5 = (f32[2,4096]{1,0:T(2,128)S(1)}, f32[2,4096]{1,0:T(2,128)S(1)}, u32[]{:S(2)}, u32[]{:S(2)}) collective-permute-start(f32[2,4096]{1,0:T(2,128)S(1)} %reshape.730), channel_id=1, source_target_pairs={{0,256},{64,320},{128,384},{192,448},{256,0},{320,64},{384,128},{4... | collective-permute-start | bytes 98312 | tf_op jit(solution)/shard_map/ppermute | solution.py:12
  101.6 21.6 %collective-permute-start.2 = (f32[2,4096]{1,0:T(2,128)S(1)}, f32[2,4096]{1,0:T(2,128)S(1)}, u32[]{:S(2)}, u32[]{:S(2)}) collective-permute-start(f32[2,4096]{1,0:T(2,128)S(1)} %reshape.725), channel_id=1, source_target_pairs={{0,256},{64,320},{128,384},{192,448},{256,0},{320,64},{384,128},{4... | collective-permute-start | bytes 98312 | tf_op jit(solution)/shard_map/ppermute | solution.py:12
  104.6 24.5 %collective-permute-start.6 = (f32[2,4096]{1,0:T(2,128)S(1)}, f32[2,4096]{1,0:T(2,128)S(1)}, u32[]{:S(2)}, u32[]{:S(2)}) collective-permute-start(f32[2,4096]{1,0:T(2,128)S(1)} %reshape.732), channel_id=1, source_target_pairs={{0,128},{64,192},{128,0},{192,64},{256,384},{320,448},{384,256},{4... | collective-permute-start | bytes 98312 | tf_op jit(solution)/shard_map/ppermute | solution.py:12
  123.5 13.7 %collective-permute-start.3 = (f32[2,4096]{1,0:T(2,128)S(1)}, f32[2,4096]{1,0:T(2,128)S(1)}, u32[]{:S(2)}, u32[]{:S(2)}) collective-permute-start(f32[2,4096]{1,0:T(2,128)S(1)} %reshape.727), channel_id=1, source_target_pairs={{0,512},{64,576},{128,640},{192,704},{256,768},{320,832},{384,896}... | collective-permute-start | bytes 98312 | tf_op jit(solution)/shard_map/ppermute | solution.py:12
  129.4 14.5 %collective-permute-start.7 = (f32[2,4096]{1,0:T(2,128)S(1)}, f32[2,4096]{1,0:T(2,128)S(1)}, u32[]{:S(2)}, u32[]{:S(2)}) collective-permute-start(f32[2,4096]{1,0:T(2,128)S(1)} %reshape.734), channel_id=1, source_target_pairs={{0,64},{64,0},{128,192},{192,128},{256,320},{320,256},{384,448},{4... | collective-permute-start | bytes 98312 | tf_op jit(solution)/shard_map/ppermute | solution.py:12

commit v8 on v4

--- a/solution.py
+++ b/solution.py
@@ -31,7 +31,7 @@
 def reorder(values, source):
     bit_count = source.shape[0]
     length = 2**bit_count
-    lane_bits = 7
+    lane_bits = 8
     lanes = 2**lane_bits
     rows = length // lanes
     picked = source_index(source, bit_count)

time: 131 us -> 135 us (1.031)
  matrix products: 26.3 us -> 31.3 us
    dot_general x6, matrix products: 15 us -> 20 us  [reorder(): jnp.dot(values.reshape(2 * rows, lanes), one_hot, precision=HIGHEST, pref...]
where the time goes in v8:
time: 135 us
  starting transfers between devices  55.3 us (41%)
  waiting for transfers between devices  36.6 us (27%)
  matrix products  31.3 us (23%)
  other arithmetic  8.41 us (6%)
  local copies, waits for them, and re-layouts  2.37 us (2%)
    ppermute x4, starting transfers between devices, swapped(): return lax.ppermute(value, axis, pairs)  39.1 us
    ppermute x4, waiting for transfers between devices, swapped(): return lax.ppermute(value, axis, pairs)  32.1 us
    dot_general x6, matrix products, reorder(): jnp.dot(values.reshape(2 * rows, lanes), one_hot, precision=HIGHEST, pref...  20 us
    all_to_all x1, starting transfers between devices, per_device(): lax.all_to_all(shaped, 'dev', split_axis=1, concat_axis=1, tiled=True)  16.2 us
    all_to_all x1, waiting for transfers between devices, per_device(): lax.all_to_all(shaped, 'dev', split_axis=1, concat_axis=1, tiled=True)  4.54 us
    dot_general x16, matrix products, pair_exchange(): jnp.dot(jnp.dot(pick_out, matrix[part], precision=HIGHEST), pick_in.T, pr...  3.93 us
  transfers between devices with their start and end apart: 5, of which 5 were waited for; matrix products, arithmetic and copies ran while one was open for 7% of the time, Pallas kernels for 0%

profile of v8, /device:TPU:24, one launch (start us, length us, event | category | flops | bytes accessed | tf_op | source)
XLA Modules:
  0.0 134.7 jit_solution(14056937781146078158)
XLA Ops:
  0.0 0.8 slice_bitcast_fusion
  0.8 0.7 compare_reduce_fusion.4
  1.6 0.7 fusion.204
  2.5 0.8 select_reduce_fusion.1
  3.9 1.0 reduce
  5.0 3.2 %select_reduce_fusion = f32[2,8192]{1,0:T(2,128)S(1)} fusion(pred[32,8192]{1,0:T(8,128)(4,1)S(1)} %iota_compare_fusion.7, f32[64,256]{1,0:T(8,128)S(1)} %reshape_reshape.4, s32[8192]{0:T(1024)S(1)} %get-tuple-element.31), kind=kOutput, calls=%fused_computation.23 | convolution fusion | flops 1613742080 | bytes 425984 | tf_op jit(solution)/shard_map/dot_general | solution.py:41
  8.3 0.2 fusion.142
  8.6 0.2 fusion.138
  9.6 0.2 convolution_subtract_fusion.3
  9.9 0.2 convolution_add_fusion.3
  10.2 3.2 %fusion.17 = f32[2,8192]{1,0:T(2,128)S(1)} fusion(s32[8192]{0:T(1024)S(1)} %get-tuple-element.34, pred[32,8192]{1,0:T(8,128)(4,1)S(1)} %iota_compare_fusion.8, f32[1,32,256]{2,1,0:T(8,128)S(1)} %stack.37, f32[1,32,256]{2,1,0:T(8,128)S(1)} %stack.36), kind=kOutput, calls=%fused_computation.24 | convolution fusion | flops 1613758464 | bytes 425984 | tf_op jit(solution)/shard_map/dot_general | solution.py:41
  13.5 0.2 fusion.136
  13.7 0.2 fusion.132
  14.2 0.2 convolution_subtract_fusion.2
  14.5 0.2 convolution_add_fusion.2
  15.6 3.9 %fusion.20 = f32[2,8192]{1,0:T(2,128)} fusion(s32[8192]{0:T(1024)S(1)} %get-tuple-element.36, pred[32,8192]{1,0:T(8,128)(4,1)S(1)} %iota_compare_fusion.9, f32[1,32,256]{2,1,0:T(8,128)S(1)} %stack.40, f32[1,32,256]{2,1,0:T(8,128)S(1)} %stack.39), kind=kOutput, calls=%fused_computation.25 | convolution fusion | flops 1613758464 | bytes 425984 | tf_op jit(solution)/shard_map/dot_general | solution.py:41
  19.4 16.2 %all-to-all-start = ((f32[2,64,128]{2,0,1:T(2,128)}), f32[2,64,128]{2,0,1:T(2,128)S(1)}, u32[]{:S(2)}, u32[]{:S(2)}) async-start(f32[2,64,128]{2,0,1:T(2,128)} %bitcast.37), calls=%async_computation | async-start | bytes 131072 | tf_op jit(solution)/shard_map/all_to_all | solution.py:250
  36.5 0.2 fusion.172
  36.7 0.2 fusion.173
  36.9 0.3 fusion.251
  37.2 0.2 fusion.250
  37.4 0.2 convolution_select_fusion.8
  37.7 0.2 convolution_select_fusion.6
  37.9 0.2 fusion.174
  38.1 0.2 fusion.175
  38.4 0.3 fusion.249
  38.7 0.2 fusion.248
  38.9 0.2 convolution_select_fusion.12
  39.1 0.2 convolution_select_fusion.10
  39.6 0.2 fusion.177
  42.2 0.2 fusion.247
  42.4 0.2 fusion.246
  42.7 0.2 convolution_select_fusion.16
  42.9 0.2 fusion.178
  43.1 0.3 fusion.245
  43.4 0.2 fusion.244
  43.7 4.5 %all-to-all-done = f32[2,64,128]{2,0,1:T(2,128)S(1)} async-done(((f32[2,64,128]{2,0,1:T(2,128)}), f32[2,64,128]{2,0,1:T(2,128)S(1)}, u32[]{:S(2)}, u32[]{:S(2)}) %all-to-all-start) | async-done | bytes 65568 | tf_op jit(solution)/shard_map/all_to_all | solution.py:250
  48.2 3.2 %fusion.23 = f32[2,8192]{1,0:T(2,128)S(1)} fusion(f32[2,32,256]{2,1,0:T(8,128)S(1)} %dot_general.198, s32[8192]{0:T(1024)S(1)} %get-tuple-element.30, pred[32,8192]{1,0:T(8,128)(4,1)S(1)} %iota_compare_fusion.10), kind=kOutput, calls=%fused_computation.26 | convolution fusion | flops 1613742080 | bytes 425984 | tf_op jit(solution)/shard_map/dot_general | solution.py:41
  51.5 0.2 fusion.130
  51.8 0.2 fusion.126
  52.0 0.2 convolution_subtract_fusion.1
  52.3 0.2 convolution_add_fusion.1
  52.6 3.2 %fusion.26 = f32[2,8192]{1,0:T(2,128)S(1)} fusion(s32[8192]{0:T(1024)S(1)} %get-tuple-element.38, pred[32,8192]{1,0:T(8,128)(4,1)S(1)} %iota_compare_fusion.11, f32[1,32,256]{2,1,0:T(8,128)S(1)} %stack.43, f32[1,32,256]{2,1,0:T(8,128)S(1)} %stack.42), kind=kOutput, calls=%fused_computation.27 | convolution fusion | flops 1613758464 | bytes 425984 | tf_op jit(solution)/shard_map/dot_general | solution.py:41
  55.8 0.2 fusion.124
  56.1 0.2 fusion.120
  56.3 0.2 convolution_subtract_fusion
  56.6 0.2 convolution_add_fusion
  56.9 3.2 %fusion.29 = f32[2,8192]{1,0:T(2,128)S(1)} fusion(s32[8192]{0:T(1024)S(1)} %get-tuple-element.40, pred[32,8192]{1,0:T(8,128)(4,1)S(1)} %iota_compare_fusion.12, f32[1,32,256]{2,1,0:T(8,128)S(1)} %stack.46, f32[1,32,256]{2,1,0:T(8,128)S(1)} %stack.45), kind=kOutput, calls=%fused_computation.28 | convolution fusion | flops 1613758464 | bytes 425984 | tf_op jit(solution)/shard_map/dot_general | solution.py:41
  60.1 15.7 %collective-permute-start = (f32[2,8192]{1,0:T(2,128)S(1)}, f32[2,8192]{1,0:T(2,128)S(1)}, u32[]{:S(2)}, u32[]{:S(2)}) collective-permute-start(f32[2,8192]{1,0:T(2,128)S(1)} %broadcast_multiply_fusion), channel_id=1, source_target_pairs={{0,64},{64,0},{128,192},{192,128},{256,320},{320,256},{384,448},{4... | collective-permute-start | bytes 196616 | tf_op jit(solution)/shard_map/ppermute | solution.py:12
  75.9 0.2 convolution_select_fusion.14
  76.2 11.7 %collective-permute-done = f32[2,8192]{1,0:T(2,128)S(1)} collective-permute-done((f32[2,8192]{1,0:T(2,128)S(1)}, f32[2,8192]{1,0:T(2,128)S(1)}, u32[]{:S(2)}, u32[]{:S(2)}) %collective-permute-start) | collective-permute-done | bytes 65568 | tf_op jit(solution)/shard_map/ppermute | solution.py:12
  87.9 0.3 fusion.80
  88.3 18.1 %collective-permute-start.1 = (f32[2,8192]{1,0:T(2,128)S(1)}, f32[2,8192]{1,0:T(2,128)S(1)}, u32[]{:S(2)}, u32[]{:S(2)}) collective-permute-start(f32[2,8192]{1,0:T(2,128)S(1)} %reshape.715), channel_id=1, source_target_pairs={{0,128},{64,192},{128,0},{192,64},{256,384},{320,448},{384,256},{4... | collective-permute-start | bytes 196616 | tf_op jit(solution)/shard_map/ppermute | solution.py:12
  106.4 0.2 fusion.179
  106.6 11.9 %collective-permute-done.1 = f32[2,8192]{1,0:T(2,128)S(1)} collective-permute-done((f32[2,8192]{1,0:T(2,128)S(1)}, f32[2,8192]{1,0:T(2,128)S(1)}, u32[]{:S(2)}, u32[]{:S(2)}) %collective-permute-start.1) | collective-permute-done | bytes 65568 | tf_op jit(solution)/shard_map/ppermute | solution.py:12
  118.5 0.3 fusion.64
  118.9 2.7 %collective-permute-start.2 = (f32[2,8192]{1,0:T(2,128)S(1)}, f32[2,8192]{1,0:T(2,128)S(1)}, u32[]{:S(2)}, u32[]{:S(2)}) collective-permute-start(f32[2,8192]{1,0:T(2,128)S(1)} %reshape.717), channel_id=1, source_target_pairs={{0,256},{64,320},{128,384},{192,448},{256,0},{320,64},{384,128},{4... | collective-permute-start | bytes 196616 | tf_op jit(solution)/shard_map/ppermute | solution.py:12
  121.5 0.2 convolution_select_fusion.20
  121.8 3.8 %collective-permute-done.2 = f32[2,8192]{1,0:T(2,128)S(1)} collective-permute-done((f32[2,8192]{1,0:T(2,128)S(1)}, f32[2,8192]{1,0:T(2,128)S(1)}, u32[]{:S(2)}, u32[]{:S(2)}) %collective-permute-start.2) | collective-permute-done | bytes 65568 | tf_op jit(solution)/shard_map/ppermute | solution.py:12
  125.6 0.3 fusion.48
  126.0 2.6 %collective-permute-start.3 = (f32[2,8192]{1,0:T(2,128)S(1)}, f32[2,8192]{1,0:T(2,128)S(1)}, u32[]{:S(2)}, u32[]{:S(2)}) collective-permute-start(f32[2,8192]{1,0:T(2,128)S(1)} %reshape.719), channel_id=1, source_target_pairs={{0,512},{64,576},{128,640},{192,704},{256,768},{320,832},{384,896}... | collective-permute-start | bytes 196616 | tf_op jit(solution)/shard_map/ppermute | solution.py:12
  128.6 0.2 convolution_select_fusion.18
  128.9 4.8 %collective-permute-done.3 = f32[2,8192]{1,0:T(2,128)S(1)} collective-permute-done((f32[2,8192]{1,0:T(2,128)S(1)}, f32[2,8192]{1,0:T(2,128)S(1)}, u32[]{:S(2)}, u32[]{:S(2)}) %collective-permute-start.3) | collective-permute-done | bytes 65568 | tf_op jit(solution)/shard_map/ppermute | solution.py:12
  133.7 1.0 fusion.32
  (112 shorter events, 6.8 us)
Async XLA Ops:
  5.0 3.3 %copy-start = (f32[4,2,128,128]{3,2,1,0:T(8,128)S(1)}, f32[4,2,128,128]{3,2,1,0:T(8,128)}, u32[]{:S(2)}) copy-start(f32[4,2,128,128]{3,2,1,0:T(8,128)} %param.8) | copy-start | bytes 1572868
  10.2 3.8 %copy-start.3 = (s32[23]{0:T(128)S(1)}, s32[23]{0:T(128)}, u32[]{:S(2)}) copy-start(s32[23]{0:T(128)} %param.11) | copy-start | bytes 280
  15.6 20.1 %copy-start.1 = (s32[23]{0:T(128)S(1)}, s32[23]{0:T(128)}, u32[]{:S(2)}) copy-start(s32[23]{0:T(128)} %param.10) | copy-start | bytes 280
  15.6 20.9 %copy-start.2 = (f32[2,4,4]{2,1,0:T(4,128)S(1)}, f32[2,4,4]{2,1,0:T(4,128)}, u32[]{:S(2)}) copy-start(f32[2,4,4]{2,1,0:T(4,128)} %param.9) | copy-start | bytes 388
  19.4 28.8 %all-to-all-start = ((f32[2,64,128]{2,0,1:T(2,128)}), f32[2,64,128]{2,0,1:T(2,128)S(1)}, u32[]{:S(2)}, u32[]{:S(2)}) async-start(f32[2,64,128]{2,0,1:T(2,128)} %bitcast.37), calls=%async_computation | async-start | bytes 131072 | tf_op jit(solution)/shard_map/all_to_all | solution.py:250
  40.2 1.6 %copy-start.4 = (s32[10]{0:T(128)S(1)}, s32[10]{0:T(128)}, u32[]{:S(2)}) copy-start(s32[10]{0:T(128)} %param.13) | copy-start | bytes 124
  60.1 27.7 %collective-permute-start = (f32[2,8192]{1,0:T(2,128)S(1)}, f32[2,8192]{1,0:T(2,128)S(1)}, u32[]{:S(2)}, u32[]{:S(2)}) collective-permute-start(f32[2,8192]{1,0:T(2,128)S(1)} %broadcast_multiply_fusion), channel_id=1, source_target_pairs={{0,64},{64,0},{128,192},{192,128},{256,320},{320,256},{384,448},{4... | collective-permute-start | bytes 196616 | tf_op jit(solution)/shard_map/ppermute | solution.py:12
  88.3 30.2 %collective-permute-start.1 = (f32[2,8192]{1,0:T(2,128)S(1)}, f32[2,8192]{1,0:T(2,128)S(1)}, u32[]{:S(2)}, u32[]{:S(2)}) collective-permute-start(f32[2,8192]{1,0:T(2,128)S(1)} %reshape.715), channel_id=1, source_target_pairs={{0,128},{64,192},{128,0},{192,64},{256,384},{320,448},{384,256},{4... | collective-permute-start | bytes 196616 | tf_op jit(solution)/shard_map/ppermute | solution.py:12
  118.9 6.7 %collective-permute-start.2 = (f32[2,8192]{1,0:T(2,128)S(1)}, f32[2,8192]{1,0:T(2,128)S(1)}, u32[]{:S(2)}, u32[]{:S(2)}) collective-permute-start(f32[2,8192]{1,0:T(2,128)S(1)} %reshape.717), channel_id=1, source_target_pairs={{0,256},{64,320},{128,384},{192,448},{256,0},{320,64},{384,128},{4... | collective-permute-start | bytes 196616 | tf_op jit(solution)/shard_map/ppermute | solution.py:12
  126.0 7.7 %collective-permute-start.3 = (f32[2,8192]{1,0:T(2,128)S(1)}, f32[2,8192]{1,0:T(2,128)S(1)}, u32[]{:S(2)}, u32[]{:S(2)}) collective-permute-start(f32[2,8192]{1,0:T(2,128)S(1)} %reshape.719), channel_id=1, source_target_pairs={{0,512},{64,576},{128,640},{192,704},{256,768},{320,832},{384,896}... | collective-permute-start | bytes 196616 | tf_op jit(solution)/shard_map/ppermute | solution.py:12

commit v9 on v8

--- a/solution.py
+++ b/solution.py
@@ -31,7 +31,7 @@
 def reorder(values, source):
     bit_count = source.shape[0]
     length = 2**bit_count
-    lane_bits = 8
+    lane_bits = 6
     lanes = 2**lane_bits
     rows = length // lanes
     picked = source_index(source, bit_count)

time: 135 us -> 140 us (1.037)
  matrix products: 31.3 us -> 43 us
  waiting for transfers between devices: 36.6 us -> 25.3 us
  other arithmetic: 8.41 us -> 11 us
    dot_general x6, matrix products: 20 us -> 28 us  [reorder(): jnp.dot(values.reshape(2 * rows, lanes), one_hot, precision=HIGHEST, pref...]
    ppermute x4, waiting for transfers between devices: 32.1 us -> 25.3 us  [swapped(): return lax.ppermute(value, axis, pairs)]
    all_to_all x1, waiting for transfers between devices: 4.54 us -> 0.01 us  [per_device(): lax.all_to_all(shaped, 'dev', split_axis=1, concat_axis=1, tiled=True)]
    dot_general x16, matrix products: 3.93 us -> 7.59 us  [pair_exchange(): jnp.dot(jnp.dot(pick_out, matrix[part], precision=HIGHEST), pick_in.T, pr...]
    eq x6, other arithmetic: 0.86 us -> 4.3 us  [reorder(): lax.broadcasted_iota(jnp.int32, (rows, length), 0)]
  transfers between devices with their start and end apart: 5 -> 5, of which waited for: 5 -> 4; matrix products, arithmetic and copies ran while one was open for 7% -> 10% of each run, Pallas kernels for 0% -> 0%
where the time goes in v9:
time: 140 us
  starting transfers between devices  56.1 us (40%)
  matrix products  43 us (31%)
  waiting for transfers between devices  25.3 us (18%)
  other arithmetic  11 us (8%)
  local copies, waits for them, and re-layouts  3.58 us (3%)
    ppermute x4, starting transfers between devices, swapped(): return lax.ppermute(value, axis, pairs)  39.9 us
    dot_general x6, matrix products, reorder(): jnp.dot(values.reshape(2 * rows, lanes), one_hot, precision=HIGHEST, pref...  28 us
    ppermute x4, waiting for transfers between devices, swapped(): return lax.ppermute(value, axis, pairs)  25.3 us
    all_to_all x1, starting transfers between devices, per_device(): lax.all_to_all(shaped, 'dev', split_axis=1, concat_axis=1, tiled=True)  16.2 us
    dot_general x16, matrix products, pair_exchange(): jnp.dot(jnp.dot(pick_out, matrix[part], precision=HIGHEST), pick_in.T, pr...  7.59 us
    eq x6, other arithmetic, reorder(): lax.broadcasted_iota(jnp.int32, (rows, length), 0)  4.3 us
  transfers between devices with their start and end apart: 5, of which 4 were waited for; matrix products, arithmetic and copies ran while one was open for 10% of the time, Pallas kernels for 0%

profile of v9, /device:TPU:24, one launch (start us, length us, event | category | flops | bytes accessed | tf_op | source)
XLA Modules:
  0.0 139.7 jit_solution(9297509858910325243)
XLA Ops:
  0.0 0.8 slice_bitcast_fusion
  0.8 0.7 compare_reduce_fusion.4
  1.6 0.7 fusion.194
  2.5 0.8 select_reduce_fusion.1
  3.8 0.6 iota_compare_fusion
  4.7 4.3 %select_reduce_fusion = f32[2,8192]{1,0:T(2,128)S(1)} fusion(pred[128,8192]{1,0:T(8,128)(4,1)S(1)} %iota_compare_fusion, f32[256,64]{1,0:T(8,128)S(1)} %reshape_reshape.4, s32[8192]{0:T(1024)S(1)} %get-tuple-element.31), kind=kOutput, calls=%fused_computation.5 | convolution fusion | flops 1615314944 | bytes 1212416 | tf_op jit(solution)/shard_map/dot_general | solution.py:41
  9.1 0.2 fusion.132
  9.3 0.2 fusion.128
  10.2 0.5 iota_compare_fusion.1
  10.8 0.2 convolution_subtract_fusion.3
  11.2 0.3 convolution_add_fusion.3
  11.6 4.4 %fusion = f32[2,8192]{1,0:T(2,128)S(1)} fusion(pred[128,8192]{1,0:T(8,128)(4,1)S(1)} %iota_compare_fusion.1, s32[8192]{0:T(1024)S(1)} %get-tuple-element.33, f32[1,128,64]{1,2,0:T(8,128)S(1)} %copy.39, f32[1,128,64]{1,2,0:T(8,128)S(1)} %copy.38), kind=kOutput, calls=%fused_computation.12 | convolution fusion | flops 1615331328 | bytes 1212416 | tf_op jit(solution)/shard_map/dot_general | solution.py:41
  16.1 0.2 fusion.126
  16.3 0.2 fusion.122
  16.8 0.2 convolution_subtract_fusion.2
  17.2 0.3 convolution_add_fusion.2
  18.3 0.6 iota_compare_fusion.2
  18.9 5.1 %fusion.1 = f32[2,8192]{1,0:T(2,128)} fusion(pred[128,8192]{1,0:T(8,128)(4,1)S(1)} %iota_compare_fusion.2, s32[8192]{0:T(1024)S(1)} %get-tuple-element.35, f32[1,128,64]{1,2,0:T(8,128)S(1)} %copy.41, f32[1,128,64]{1,2,0:T(8,128)S(1)} %copy.40), kind=kOutput, calls=%fused_computation.13 | convolution fusion | flops 1615331328 | bytes 1212416 | tf_op jit(solution)/shard_map/dot_general | solution.py:41
  23.9 16.2 %all-to-all-start = ((f32[2,64,128]{2,0,1:T(2,128)}), f32[2,64,128]{2,0,1:T(2,128)S(1)}, u32[]{:S(2)}, u32[]{:S(2)}) async-start(f32[2,64,128]{2,0,1:T(2,128)} %bitcast.37), calls=%async_computation | async-start | bytes 131072 | tf_op jit(solution)/shard_map/all_to_all | solution.py:250
  41.2 0.2 fusion.163
  41.4 0.3 fusion.241
  41.7 0.2 fusion.240
  41.9 0.8 convolution_select_fusion.8
  42.8 0.8 convolution_select_fusion.6
  43.8 0.2 fusion.165
  44.1 0.3 fusion.239
  44.3 0.2 fusion.238
  44.6 0.8 convolution_select_fusion.12
  45.4 0.8 convolution_select_fusion.10
  46.5 0.2 fusion.167
  47.1 1.5 %iota_compare_fusion.3 = pred[128,8192]{1,0:T(8,128)(4,1)} fusion(s32[8192]{0:T(1024)S(1)} %get-tuple-element.30), kind=kLoop, calls=%fused_computation.9 | loop fusion | flops 1048576 | bytes 1081344 | tf_op jit(solution)/shard_map/eq | solution.py:47
  49.3 0.5 iota_compare_fusion.4
  50.3 0.5 iota_compare_fusion.5
  51.3 0.2 fusion.237
  51.5 0.9 fusion.236
  52.4 0.8 convolution_select_fusion.16
  53.4 0.3 fusion.235
  53.7 0.2 fusion.234
  54.1 5.4 %fusion.2 = f32[2,8192]{1,0:T(2,128)S(1)} fusion(f32[2,128,64]{2,1,0:T(8,128)S(1)} %dot_general.198, pred[128,8192]{1,0:T(8,128)(4,1)} %iota_compare_fusion.3, s32[8192]{0:T(1024)S(1)} %get-tuple-element.29), kind=kOutput, calls=%fused_computation.14 | convolution fusion | flops 1615314944 | bytes 1212416 | tf_op jit(solution)/shard_map/dot_general | solution.py:41
  59.5 0.2 fusion.120
  59.7 0.2 fusion.116
  60.0 0.2 convolution_subtract_fusion.1
  60.4 0.3 convolution_add_fusion.1
  60.8 4.4 %fusion.3 = f32[2,8192]{1,0:T(2,128)S(1)} fusion(pred[128,8192]{1,0:T(8,128)(4,1)S(1)} %iota_compare_fusion.4, s32[8192]{0:T(1024)S(1)} %get-tuple-element.37, f32[1,128,64]{1,2,0:T(8,128)S(1)} %copy.45, f32[1,128,64]{1,2,0:T(8,128)S(1)} %copy.44), kind=kOutput, calls=%fused_computation.15 | convolution fusion | flops 1615331328 | bytes 1212416 | tf_op jit(solution)/shard_map/dot_general | solution.py:41
  65.3 0.2 fusion.114
  65.5 0.2 fusion.110
  65.8 0.2 convolution_subtract_fusion
  66.2 0.3 convolution_add_fusion
  66.6 4.4 %fusion.4 = f32[2,8192]{1,0:T(2,128)S(1)} fusion(pred[128,8192]{1,0:T(8,128)(4,1)S(1)} %iota_compare_fusion.5, s32[8192]{0:T(1024)S(1)} %get-tuple-element.39, f32[1,128,64]{1,2,0:T(8,128)S(1)} %copy.47, f32[1,128,64]{1,2,0:T(8,128)S(1)} %copy.46), kind=kOutput, calls=%fused_computation.16 | convolution fusion | flops 1615331328 | bytes 1212416 | tf_op jit(solution)/shard_map/dot_general | solution.py:41
  71.1 15.7 %collective-permute-start = (f32[2,8192]{1,0:T(2,128)S(1)}, f32[2,8192]{1,0:T(2,128)S(1)}, u32[]{:S(2)}, u32[]{:S(2)}) collective-permute-start(f32[2,8192]{1,0:T(2,128)S(1)} %broadcast_multiply_fusion), channel_id=1, source_target_pairs={{0,64},{64,0},{128,192},{192,128},{256,320},{320,256},{384,448},{4... | collective-permute-start | bytes 196616 | tf_op jit(solution)/shard_map/ppermute | solution.py:12
  86.8 0.2 convolution_select_fusion.14
  87.2 11.7 %collective-permute-done = f32[2,8192]{1,0:T(2,128)S(1)} collective-permute-done((f32[2,8192]{1,0:T(2,128)S(1)}, f32[2,8192]{1,0:T(2,128)S(1)}, u32[]{:S(2)}, u32[]{:S(2)}) %collective-permute-start) | collective-permute-done | bytes 65568 | tf_op jit(solution)/shard_map/ppermute | solution.py:12
  99.0 0.3 fusion.70
  99.4 18.4 %collective-permute-start.1 = (f32[2,8192]{1,0:T(2,128)S(1)}, f32[2,8192]{1,0:T(2,128)S(1)}, u32[]{:S(2)}, u32[]{:S(2)}) collective-permute-start(f32[2,8192]{1,0:T(2,128)S(1)} %reshape.715), channel_id=1, source_target_pairs={{0,128},{64,192},{128,0},{192,64},{256,384},{320,448},{384,256},{4... | collective-permute-start | bytes 196616 | tf_op jit(solution)/shard_map/ppermute | solution.py:12
  117.9 6.0 %collective-permute-done.1 = f32[2,8192]{1,0:T(2,128)S(1)} collective-permute-done((f32[2,8192]{1,0:T(2,128)S(1)}, f32[2,8192]{1,0:T(2,128)S(1)}, u32[]{:S(2)}, u32[]{:S(2)}) %collective-permute-start.1) | collective-permute-done | bytes 65568 | tf_op jit(solution)/shard_map/ppermute | solution.py:12
  124.1 0.3 fusion.54
  124.4 2.7 %collective-permute-start.2 = (f32[2,8192]{1,0:T(2,128)S(1)}, f32[2,8192]{1,0:T(2,128)S(1)}, u32[]{:S(2)}, u32[]{:S(2)}) collective-permute-start(f32[2,8192]{1,0:T(2,128)S(1)} %reshape.717), channel_id=1, source_target_pairs={{0,256},{64,320},{128,384},{192,448},{256,0},{320,64},{384,128},{4... | collective-permute-start | bytes 196616 | tf_op jit(solution)/shard_map/ppermute | solution.py:12
  127.1 0.2 convolution_select_fusion.20
  127.3 3.3 %collective-permute-done.2 = f32[2,8192]{1,0:T(2,128)S(1)} collective-permute-done((f32[2,8192]{1,0:T(2,128)S(1)}, f32[2,8192]{1,0:T(2,128)S(1)}, u32[]{:S(2)}, u32[]{:S(2)}) %collective-permute-start.2) | collective-permute-done | bytes 65568 | tf_op jit(solution)/shard_map/ppermute | solution.py:12
  130.7 0.3 fusion.38
  131.1 3.1 %collective-permute-start.3 = (f32[2,8192]{1,0:T(2,128)S(1)}, f32[2,8192]{1,0:T(2,128)S(1)}, u32[]{:S(2)}, u32[]{:S(2)}) collective-permute-start(f32[2,8192]{1,0:T(2,128)S(1)} %reshape.719), channel_id=1, source_target_pairs={{0,512},{64,576},{128,640},{192,704},{256,768},{320,832},{384,896}... | collective-permute-start | bytes 196616 | tf_op jit(solution)/shard_map/ppermute | solution.py:12
  134.2 0.2 convolution_select_fusion.18
  134.5 4.3 %collective-permute-done.3 = f32[2,8192]{1,0:T(2,128)S(1)} collective-permute-done((f32[2,8192]{1,0:T(2,128)S(1)}, f32[2,8192]{1,0:T(2,128)S(1)}, u32[]{:S(2)}, u32[]{:S(2)}) %collective-permute-start.3) | collective-permute-done | bytes 65568 | tf_op jit(solution)/shard_map/ppermute | solution.py:12
  138.8 1.0 fusion.22
  (136 shorter events, 8.2 us)
Async XLA Ops:
  0.0 4.3 %copy-start.1 = (f32[2,1,1,8192]{3,2,1,0:T(1,128)S(1)}, f32[2,1,1,8192]{3,2,1,0:T(1,128)}, u32[]{:S(2)}) copy-start(f32[2,1,1,8192]{3,2,1,0:T(1,128)} %param.7) | copy-start | bytes 196612
  4.4 4.7 %copy-start = (f32[4,2,128,128]{3,2,1,0:T(8,128)S(1)}, f32[4,2,128,128]{3,2,1,0:T(8,128)}, u32[]{:S(2)}) copy-start(f32[4,2,128,128]{3,2,1,0:T(8,128)} %param.8) | copy-start | bytes 1572868
  11.6 5.0 %copy-start.4 = (s32[23]{0:T(128)S(1)}, s32[23]{0:T(128)}, u32[]{:S(2)}) copy-start(s32[23]{0:T(128)} %param.11) | copy-start | bytes 280
  18.9 21.3 %copy-start.2 = (s32[23]{0:T(128)S(1)}, s32[23]{0:T(128)}, u32[]{:S(2)}) copy-start(s32[23]{0:T(128)} %param.10) | copy-start | bytes 280
  18.9 22.1 %copy-start.3 = (f32[2,4,4]{2,1,0:T(4,128)S(1)}, f32[2,4,4]{2,1,0:T(4,128)}, u32[]{:S(2)}) copy-start(f32[2,4,4]{2,1,0:T(4,128)} %param.9) | copy-start | bytes 388
  23.9 30.0 %all-to-all-start = ((f32[2,64,128]{2,0,1:T(2,128)}), f32[2,64,128]{2,0,1:T(2,128)S(1)}, u32[]{:S(2)}, u32[]{:S(2)}) async-start(f32[2,64,128]{2,0,1:T(2,128)} %bitcast.37), calls=%async_computation | async-start | bytes 131072 | tf_op jit(solution)/shard_map/all_to_all | solution.py:250
  49.3 1.6 %copy-start.5 = (s32[10]{0:T(128)S(1)}, s32[10]{0:T(128)}, u32[]{:S(2)}) copy-start(s32[10]{0:T(128)} %param.13) | copy-start | bytes 124
  66.6 32.4 %copy-start.8 = (f32[64,64]{1,0:T(8,128)S(1)}, f32[64,64]{1,0:T(8,128)}, u32[]{:S(2)}) copy-start(f32[64,64]{1,0:T(8,128)} %convolution_select_fusion.8) | copy-start | bytes 49156
  66.6 32.4 %copy-start.9 = (f32[64,64]{1,0:T(8,128)S(1)}, f32[64,64]{1,0:T(8,128)}, u32[]{:S(2)}) copy-start(f32[64,64]{1,0:T(8,128)} %convolution_select_fusion.6) | copy-start | bytes 49156
  71.0 53.0 %copy-start.10 = (f32[64,64]{1,0:T(8,128)S(1)}, f32[64,64]{1,0:T(8,128)}, u32[]{:S(2)}) copy-start(f32[64,64]{1,0:T(8,128)} %convolution_select_fusion.12) | copy-start | bytes 49156
  71.0 53.0 %copy-start.11 = (f32[64,64]{1,0:T(8,128)S(1)}, f32[64,64]{1,0:T(8,128)}, u32[]{:S(2)}) copy-start(f32[64,64]{1,0:T(8,128)} %convolution_select_fusion.10) | copy-start | bytes 49156
  71.1 27.8 %collective-permute-start = (f32[2,8192]{1,0:T(2,128)S(1)}, f32[2,8192]{1,0:T(2,128)S(1)}, u32[]{:S(2)}, u32[]{:S(2)}) collective-permute-start(f32[2,8192]{1,0:T(2,128)S(1)} %broadcast_multiply_fusion), channel_id=1, source_target_pairs={{0,64},{64,0},{128,192},{192,128},{256,320},{320,256},{384,448},{4... | collective-permute-start | bytes 196616 | tf_op jit(solution)/shard_map/ppermute | solution.py:12
  87.2 43.5 %copy-start.6 = (f32[64,64]{1,0:T(8,128)S(1)}, f32[64,64]{1,0:T(8,128)}, u32[]{:S(2)}) copy-start(f32[64,64]{1,0:T(8,128)} %get-tuple-element.45) | copy-start | bytes 49156
  87.2 43.5 %copy-start.7 = (f32[64,64]{1,0:T(8,128)S(1)}, f32[64,64]{1,0:T(8,128)}, u32[]{:S(2)}) copy-start(f32[64,64]{1,0:T(8,128)} %get-tuple-element.46) | copy-start | bytes 49156
  87.2 43.5 %copy-start.12 = (f32[64,64]{1,0:T(8,128)S(1)}, f32[64,64]{1,0:T(8,128)}, u32[]{:S(2)}) copy-start(f32[64,64]{1,0:T(8,128)} %convolution_select_fusion.16) | copy-start | bytes 49156
  99.4 24.6 %collective-permute-start.1 = (f32[2,8192]{1,0:T(2,128)S(1)}, f32[2,8192]{1,0:T(2,128)S(1)}, u32[]{:S(2)}, u32[]{:S(2)}) collective-permute-start(f32[2,8192]{1,0:T(2,128)S(1)} %reshape.715), channel_id=1, source_target_pairs={{0,128},{64,192},{128,0},{192,64},{256,384},{320,448},{384,256},{4... | collective-permute-start | bytes 196616 | tf_op jit(solution)/shard_map/ppermute | solution.py:12
  124.4 6.2 %collective-permute-start.2 = (f32[2,8192]{1,0:T(2,128)S(1)}, f32[2,8192]{1,0:T(2,128)S(1)}, u32[]{:S(2)}, u32[]{:S(2)}) collective-permute-start(f32[2,8192]{1,0:T(2,128)S(1)} %reshape.717), channel_id=1, source_target_pairs={{0,256},{64,320},{128,384},{192,448},{256,0},{320,64},{384,128},{4... | collective-permute-start | bytes 196616 | tf_op jit(solution)/shard_map/ppermute | solution.py:12
  131.1 7.7 %collective-permute-start.3 = (f32[2,8192]{1,0:T(2,128)S(1)}, f32[2,8192]{1,0:T(2,128)S(1)}, u32[]{:S(2)}, u32[]{:S(2)}) collective-permute-start(f32[2,8192]{1,0:T(2,128)S(1)} %reshape.719), channel_id=1, source_target_pairs={{0,512},{64,576},{128,640},{192,704},{256,768},{320,832},{384,896}... | collective-permute-start | bytes 196616 | tf_op jit(solution)/shard_map/ppermute | solution.py:12

commit v10 on v4

--- a/solution.py
+++ b/solution.py
@@ -260,7 +260,7 @@
         ).reshape(2, length)
     values = reorder(values, position_of(layout, layout_out[:local_bits]))
     values = values * spare_sign(length, spare_values)
-    for bit_num in range(group_bits):
+    for bit_num in reversed(range(group_bits)):
         values = pair_exchange(values, local_bits - 1 - bit_num, bit_num, pair_gate)
     return values.reshape(amplitudes.shape)
 

time: 131 us -> 119 us (0.908)
  waiting for transfers between devices: 36.9 us -> 21.9 us
  starting transfers between devices: 55.9 us -> 59 us
    ppermute x4, waiting for transfers between devices: 32.8 us -> 17.8 us  [swapped(): return lax.ppermute(value, axis, pairs)]
    ppermute x4, starting transfers between devices: 39.7 us -> 42.9 us  [swapped(): return lax.ppermute(value, axis, pairs)]
  transfers between devices with their start and end apart: 5 -> 5, of which waited for: 5 -> 5; matrix products, arithmetic and copies ran while one was open for 7% -> 8% of each run, Pallas kernels for 0% -> 0%
where the time goes in v10:
time: 119 us; the launch traced here: 118 us
  starting transfers between devices  59 us (50%)
  matrix products  26.3 us (22%)
  waiting for transfers between devices  21.9 us (18%)
  other arithmetic  8.19 us (7%)
  local copies, waits for them, and re-layouts  2.19 us (2%)
    ppermute x4, starting transfers between devices, swapped(): return lax.ppermute(value, axis, pairs)  42.9 us
    ppermute x4, waiting for transfers between devices, swapped(): return lax.ppermute(value, axis, pairs)  17.8 us
    all_to_all x1, starting transfers between devices, per_device(): lax.all_to_all(shaped, 'dev', split_axis=1, concat_axis=1, tiled=True)  16.2 us
    dot_general x6, matrix products, reorder(): jnp.dot(values.reshape(2 * rows, lanes), one_hot, precision=HIGHEST, pref...  15 us
    all_to_all x1, waiting for transfers between devices, per_device(): lax.all_to_all(shaped, 'dev', split_axis=1, concat_axis=1, tiled=True)  4.14 us
    dot_general x16, matrix products, pair_exchange(): jnp.dot(jnp.dot(pick_out, matrix[part], precision=HIGHEST), pick_in.T, pr...  3.93 us
  transfers between devices with their start and end apart: 5, of which 5 were waited for; matrix products, arithmetic and copies ran while one was open for 8% of the time, Pallas kernels for 0%

profile of v10, /device:TPU:24, one launch (start us, length us, event | category | flops | bytes accessed | tf_op | source)
XLA Modules:
  0.0 118.3 jit_solution(5265756294474666854)
XLA Ops:
  0.0 0.8 slice_bitcast_fusion
  0.8 0.7 compare_reduce_fusion.4
  1.6 0.7 fusion.213
  2.5 0.8 select_reduce_fusion.1
  3.8 0.3 iota_compare_fusion.7
  4.1 2.4 %select_reduce_fusion = f32[2,8192]{1,0:T(2,128)S(1)} fusion(pred[64,8192]{1,0:T(8,128)(4,1)S(1)} %iota_compare_fusion.7, f32[128,128]{1,0:T(8,128)S(1)} %bitcast.220, s32[8192]{0:T(1024)S(1)} %get-tuple-element.29), kind=kOutput, calls=%fused_computation.10 | convolution fusion | flops 1613742080 | bytes 688128 | tf_op jit(solution)/shard_map/dot_general | solution.py:41
  6.6 0.2 fusion.146
  6.8 0.2 fusion.150
  7.7 0.3 iota_compare_fusion.8
  8.0 0.2 fusion.38
  8.3 0.2 fusion.39
  8.5 2.4 %fusion.17 = f32[2,8192]{1,0:T(2,128)S(1)} fusion(s32[8192]{0:T(1024)S(1)} %get-tuple-element.32, pred[64,8192]{1,0:T(8,128)(4,1)S(1)} %iota_compare_fusion.8, f32[1,64,128]{2,1,0:T(8,128)S(1)} %fusion.38, f32[1,64,128]{2,1,0:T(8,128)S(1)} %fusion.39), kind=kOutput, calls=%fused_computation.30 | convolution fusion | flops 1613758464 | bytes 688128 | tf_op jit(solution)/shard_map/dot_general | solution.py:41
  11.0 0.2 fusion.144
  11.2 0.2 fusion.140
  11.7 0.2 fusion.37
  12.0 0.2 fusion.36
  12.9 0.3 iota_compare_fusion.9
  13.2 3.0 %fusion.20 = f32[2,8192]{1,0:T(2,128)} fusion(s32[8192]{0:T(1024)S(1)} %get-tuple-element.34, pred[64,8192]{1,0:T(8,128)(4,1)S(1)} %iota_compare_fusion.9, f32[1,64,128]{2,1,0:T(8,128)S(1)} %fusion.36, f32[1,64,128]{2,1,0:T(8,128)S(1)} %fusion.37), kind=kOutput, calls=%fused_computation.31 | convolution fusion | flops 1613758464 | bytes 688128 | tf_op jit(solution)/shard_map/dot_general | solution.py:41
  16.2 16.2 %all-to-all-start = ((f32[2,64,128]{2,0,1:T(2,128)}), f32[2,64,128]{2,0,1:T(2,128)S(1)}, u32[]{:S(2)}, u32[]{:S(2)}) async-start(f32[2,64,128]{2,0,1:T(2,128)} %bitcast.42), calls=%async_computation | async-start | bytes 131072 | tf_op jit(solution)/shard_map/all_to_all | solution.py:250
  33.7 0.3 fusion.260
  34.0 0.2 fusion.259
  34.2 0.2 convolution_select_fusion.8
  34.5 0.2 convolution_select_fusion.6
  34.9 0.2 fusion.184
  35.2 0.3 fusion.258
  35.4 0.2 fusion.257
  35.7 0.2 convolution_select_fusion.12
  35.9 0.2 convolution_select_fusion.10
  36.4 0.2 fusion.186
  37.0 0.3 iota_compare_fusion.10
  37.9 0.3 iota_compare_fusion.11
  38.7 0.3 iota_compare_fusion.12
  39.4 0.2 fusion.256
  39.6 0.2 fusion.255
  39.9 0.2 convolution_select_fusion.16
  40.3 0.3 fusion.254
  40.6 0.2 fusion.253
  40.9 4.1 %all-to-all-done = f32[2,64,128]{2,0,1:T(2,128)S(1)} async-done(((f32[2,64,128]{2,0,1:T(2,128)}), f32[2,64,128]{2,0,1:T(2,128)S(1)}, u32[]{:S(2)}, u32[]{:S(2)}) %all-to-all-start) | async-done | bytes 65568 | tf_op jit(solution)/shard_map/all_to_all | solution.py:250
  45.0 2.4 %fusion.23 = f32[2,8192]{1,0:T(2,128)S(1)} fusion(s32[8192]{0:T(1024)S(1)} %get-tuple-element.36, pred[64,8192]{1,0:T(8,128)(4,1)S(1)} %iota_compare_fusion.10, f32[2,64,128]{2,0,1:T(2,128)S(1)} %all-to-all-done), kind=kOutput, calls=%fused_computation.32 | convolution fusion | flops 1613742080 | bytes 688128 | tf_op jit(solution)/shard_map/dot_general | solution.py:41
  47.5 0.2 fusion.138
  47.7 0.2 fusion.134
  47.9 0.2 fusion.35
  48.2 0.2 fusion.34
  48.4 2.4 %fusion.26 = f32[2,8192]{1,0:T(2,128)S(1)} fusion(s32[8192]{0:T(1024)S(1)} %get-tuple-element.38, pred[64,8192]{1,0:T(8,128)(4,1)S(1)} %iota_compare_fusion.11, f32[1,64,128]{2,1,0:T(8,128)S(1)} %fusion.34, f32[1,64,128]{2,1,0:T(8,128)S(1)} %fusion.35), kind=kOutput, calls=%fused_computation.33 | convolution fusion | flops 1613758464 | bytes 688128 | tf_op jit(solution)/shard_map/dot_general | solution.py:41
  50.9 0.2 fusion.132
  51.1 0.2 fusion.128
  51.4 0.2 fusion.33
  51.6 0.2 fusion.32
  51.9 2.4 %fusion.29 = f32[2,8192]{1,0:T(2,128)S(1)} fusion(s32[8192]{0:T(1024)S(1)} %get-tuple-element.40, pred[64,8192]{1,0:T(8,128)(4,1)S(1)} %iota_compare_fusion.12, f32[1,64,128]{2,1,0:T(8,128)S(1)} %fusion.32, f32[1,64,128]{2,1,0:T(8,128)S(1)} %fusion.33), kind=kOutput, calls=%fused_computation.34 | convolution fusion | flops 1613758464 | bytes 688128 | tf_op jit(solution)/shard_map/dot_general | solution.py:41
  54.3 3.1 %collective-permute-start = (f32[2,8192]{1,0:T(2,128)S(1)}, f32[2,8192]{1,0:T(2,128)S(1)}, u32[]{:S(2)}, u32[]{:S(2)}) collective-permute-start(f32[2,8192]{1,0:T(2,128)S(1)} %broadcast_multiply_fusion), channel_id=1, source_target_pairs={{0,512},{64,576},{128,640},{192,704},{256,768},{320,832},{384,896}... | collective-permute-start | bytes 196616 | tf_op jit(solution)/shard_map/ppermute | solution.py:12
  57.5 0.2 convolution_select_fusion.14
  57.8 4.2 %collective-permute-done = f32[2,8192]{1,0:T(2,128)S(1)} collective-permute-done((f32[2,8192]{1,0:T(2,128)S(1)}, f32[2,8192]{1,0:T(2,128)S(1)}, u32[]{:S(2)}, u32[]{:S(2)}) %collective-permute-start) | collective-permute-done | bytes 65568 | tf_op jit(solution)/shard_map/ppermute | solution.py:12
  62.0 0.3 fusion.88
  62.4 2.7 %collective-permute-start.1 = (f32[2,8192]{1,0:T(2,128)S(1)}, f32[2,8192]{1,0:T(2,128)S(1)}, u32[]{:S(2)}, u32[]{:S(2)}) collective-permute-start(f32[2,8192]{1,0:T(2,128)S(1)} %reshape.699), channel_id=1, source_target_pairs={{0,256},{64,320},{128,384},{192,448},{256,0},{320,64},{384,128},{4... | collective-permute-start | bytes 196616 | tf_op jit(solution)/shard_map/ppermute | solution.py:12
  65.3 3.3 %collective-permute-done.1 = f32[2,8192]{1,0:T(2,128)S(1)} collective-permute-done((f32[2,8192]{1,0:T(2,128)S(1)}, f32[2,8192]{1,0:T(2,128)S(1)}, u32[]{:S(2)}, u32[]{:S(2)}) %collective-permute-start.1) | collective-permute-done | bytes 65568 | tf_op jit(solution)/shard_map/ppermute | solution.py:12
  68.6 0.3 fusion.72
  69.0 21.5 %collective-permute-start.2 = (f32[2,8192]{1,0:T(2,128)S(1)}, f32[2,8192]{1,0:T(2,128)S(1)}, u32[]{:S(2)}, u32[]{:S(2)}) collective-permute-start(f32[2,8192]{1,0:T(2,128)S(1)} %reshape.701), channel_id=1, source_target_pairs={{0,128},{64,192},{128,0},{192,64},{256,384},{320,448},{384,256},{4... | collective-permute-start | bytes 196616 | tf_op jit(solution)/shard_map/ppermute | solution.py:12
  90.5 0.2 convolution_select_fusion.20
  90.7 3.0 %collective-permute-done.2 = f32[2,8192]{1,0:T(2,128)S(1)} collective-permute-done((f32[2,8192]{1,0:T(2,128)S(1)}, f32[2,8192]{1,0:T(2,128)S(1)}, u32[]{:S(2)}, u32[]{:S(2)}) %collective-permute-start.2) | collective-permute-done | bytes 65568 | tf_op jit(solution)/shard_map/ppermute | solution.py:12
  93.8 0.3 fusion.56
  94.2 15.6 %collective-permute-start.3 = (f32[2,8192]{1,0:T(2,128)S(1)}, f32[2,8192]{1,0:T(2,128)S(1)}, u32[]{:S(2)}, u32[]{:S(2)}) collective-permute-start(f32[2,8192]{1,0:T(2,128)S(1)} %reshape.703), channel_id=1, source_target_pairs={{0,64},{64,0},{128,192},{192,128},{256,320},{320,256},{384,448},{4... | collective-permute-start | bytes 196616 | tf_op jit(solution)/shard_map/ppermute | solution.py:12
  109.8 0.2 convolution_select_fusion.18
  110.0 7.3 %collective-permute-done.3 = f32[2,8192]{1,0:T(2,128)S(1)} collective-permute-done((f32[2,8192]{1,0:T(2,128)S(1)}, f32[2,8192]{1,0:T(2,128)S(1)}, u32[]{:S(2)}, u32[]{:S(2)}) %collective-permute-start.3) | collective-permute-done | bytes 65568 | tf_op jit(solution)/shard_map/ppermute | solution.py:12
  117.3 1.0 fusion.40
  (102 shorter events, 6.8 us)
Async XLA Ops:
  0.0 4.1 %copy-start = (f32[2,1,1,8192]{3,2,1,0:T(1,128)S(1)}, f32[2,1,1,8192]{3,2,1,0:T(1,128)}, u32[]{:S(2)}) copy-start(f32[2,1,1,8192]{3,2,1,0:T(1,128)} %param.7) | copy-start | bytes 196612
  4.1 2.5 %copy-start.1 = (f32[4,2,128,128]{3,2,1,0:T(8,128)S(1)}, f32[4,2,128,128]{3,2,1,0:T(8,128)}, u32[]{:S(2)}) copy-start(f32[4,2,128,128]{3,2,1,0:T(8,128)} %param.8) | copy-start | bytes 1572868
  8.5 3.0 %copy-start.4 = (s32[23]{0:T(128)S(1)}, s32[23]{0:T(128)}, u32[]{:S(2)}) copy-start(s32[23]{0:T(128)} %param.11) | copy-start | bytes 280
  13.2 19.2 %copy-start.2 = (s32[23]{0:T(128)S(1)}, s32[23]{0:T(128)}, u32[]{:S(2)}) copy-start(s32[23]{0:T(128)} %param.10) | copy-start | bytes 280
  13.2 20.1 %copy-start.3 = (f32[2,4,4]{2,1,0:T(4,128)S(1)}, f32[2,4,4]{2,1,0:T(4,128)}, u32[]{:S(2)}) copy-start(f32[2,4,4]{2,1,0:T(4,128)} %param.9) | copy-start | bytes 388
  16.2 28.8 %all-to-all-start = ((f32[2,64,128]{2,0,1:T(2,128)}), f32[2,64,128]{2,0,1:T(2,128)S(1)}, u32[]{:S(2)}, u32[]{:S(2)}) async-start(f32[2,64,128]{2,0,1:T(2,128)} %bitcast.42), calls=%async_computation | async-start | bytes 131072 | tf_op jit(solution)/shard_map/all_to_all | solution.py:250
  37.9 1.1 copy-start.5
  54.3 7.7 %collective-permute-start = (f32[2,8192]{1,0:T(2,128)S(1)}, f32[2,8192]{1,0:T(2,128)S(1)}, u32[]{:S(2)}, u32[]{:S(2)}) collective-permute-start(f32[2,8192]{1,0:T(2,128)S(1)} %broadcast_multiply_fusion), channel_id=1, source_target_pairs={{0,512},{64,576},{128,640},{192,704},{256,768},{320,832},{384,896}... | collective-permute-start | bytes 196616 | tf_op jit(solution)/shard_map/ppermute | solution.py:12
  62.4 6.2 %collective-permute-start.1 = (f32[2,8192]{1,0:T(2,128)S(1)}, f32[2,8192]{1,0:T(2,128)S(1)}, u32[]{:S(2)}, u32[]{:S(2)}) collective-permute-start(f32[2,8192]{1,0:T(2,128)S(1)} %reshape.699), channel_id=1, source_target_pairs={{0,256},{64,320},{128,384},{192,448},{256,0},{320,64},{384,128},{4... | collective-permute-start | bytes 196616 | tf_op jit(solution)/shard_map/ppermute | solution.py:12
  69.0 24.7 %collective-permute-start.2 = (f32[2,8192]{1,0:T(2,128)S(1)}, f32[2,8192]{1,0:T(2,128)S(1)}, u32[]{:S(2)}, u32[]{:S(2)}) collective-permute-start(f32[2,8192]{1,0:T(2,128)S(1)} %reshape.701), channel_id=1, source_target_pairs={{0,128},{64,192},{128,0},{192,64},{256,384},{320,448},{384,256},{4... | collective-permute-start | bytes 196616 | tf_op jit(solution)/shard_map/ppermute | solution.py:12
  94.2 23.1 %collective-permute-start.3 = (f32[2,8192]{1,0:T(2,128)S(1)}, f32[2,8192]{1,0:T(2,128)S(1)}, u32[]{:S(2)}, u32[]{:S(2)}) collective-permute-start(f32[2,8192]{1,0:T(2,128)S(1)} %reshape.703), channel_id=1, source_target_pairs={{0,64},{64,0},{128,192},{192,128},{256,320},{320,256},{384,448},{4... | collective-permute-start | bytes 196616 | tf_op jit(solution)/shard_map/ppermute | solution.py:12

commit v11 on v10

--- a/solution.py
+++ b/solution.py
@@ -260,7 +260,7 @@
         ).reshape(2, length)
     values = reorder(values, position_of(layout, layout_out[:local_bits]))
     values = values * spare_sign(length, spare_values)
-    for bit_num in reversed(range(group_bits)):
+    for bit_num in (3, 2, 0, 1)[:group_bits]:
         values = pair_exchange(values, local_bits - 1 - bit_num, bit_num, pair_gate)
     return values.reshape(amplitudes.shape)
 

time: 119 us -> 127 us (1.067)
  waiting for transfers between devices: 21.9 us -> 33 us
  starting transfers between devices: 59 us -> 56 us
    ppermute x4, waiting for transfers between devices: 17.8 us -> 28.9 us  [swapped(): return lax.ppermute(value, axis, pairs)]
    ppermute x4, starting transfers between devices: 42.9 us -> 39.8 us  [swapped(): return lax.ppermute(value, axis, pairs)]
  transfers between devices with their start and end apart: 5 -> 5, of which waited for: 5 -> 5; matrix products, arithmetic and copies ran while one was open for 8% -> 7% of each run, Pallas kernels for 0% -> 0%
where the time goes in v11:
time: 127 us; the launch traced here: 126 us
  starting transfers between devices  56 us (44%)
  waiting for transfers between devices  33 us (26%)
  matrix products  26.3 us (21%)
  other arithmetic  8.19 us (6%)
  local copies, waits for them, and re-layouts  2.19 us (2%)
    ppermute x4, starting transfers between devices, swapped(): return lax.ppermute(value, axis, pairs)  39.8 us
    ppermute x4, waiting for transfers between devices, swapped(): return lax.ppermute(value, axis, pairs)  28.9 us
    all_to_all x1, starting transfers between devices, per_device(): lax.all_to_all(shaped, 'dev', split_axis=1, concat_axis=1, tiled=True)  16.2 us
    dot_general x6, matrix products, reorder(): jnp.dot(values.reshape(2 * rows, lanes), one_hot, precision=HIGHEST, pref...  15 us
    all_to_all x1, waiting for transfers between devices, per_device(): lax.all_to_all(shaped, 'dev', split_axis=1, concat_axis=1, tiled=True)  4.14 us
    dot_general x16, matrix products, pair_exchange(): jnp.dot(jnp.dot(pick_out, matrix[part], precision=HIGHEST), pick_in.T, pr...  3.93 us
  transfers between devices with their start and end apart: 5, of which 5 were waited for; matrix products, arithmetic and copies ran while one was open for 7% of the time, Pallas kernels for 0%

profile of v11, /device:TPU:24, one launch (start us, length us, event | category | flops | bytes accessed | tf_op | source)
XLA Modules:
  0.0 126.4 jit_solution(16074037992203160149)
XLA Ops:
  0.0 0.8 slice_bitcast_fusion
  0.8 0.7 compare_reduce_fusion.4
  1.6 0.7 fusion.213
  2.5 0.8 select_reduce_fusion.1
  3.8 0.3 iota_compare_fusion.7
  4.1 2.4 %select_reduce_fusion = f32[2,8192]{1,0:T(2,128)S(1)} fusion(pred[64,8192]{1,0:T(8,128)(4,1)S(1)} %iota_compare_fusion.7, f32[128,128]{1,0:T(8,128)S(1)} %bitcast.220, s32[8192]{0:T(1024)S(1)} %get-tuple-element.29), kind=kOutput, calls=%fused_computation.10 | convolution fusion | flops 1613742080 | bytes 688128 | tf_op jit(solution)/shard_map/dot_general | solution.py:41
  6.6 0.2 fusion.146
  6.8 0.2 fusion.150
  7.7 0.3 iota_compare_fusion.8
  8.0 0.2 fusion.38
  8.3 0.2 fusion.39
  8.5 2.4 %fusion.17 = f32[2,8192]{1,0:T(2,128)S(1)} fusion(s32[8192]{0:T(1024)S(1)} %get-tuple-element.32, pred[64,8192]{1,0:T(8,128)(4,1)S(1)} %iota_compare_fusion.8, f32[1,64,128]{2,1,0:T(8,128)S(1)} %fusion.38, f32[1,64,128]{2,1,0:T(8,128)S(1)} %fusion.39), kind=kOutput, calls=%fused_computation.30 | convolution fusion | flops 1613758464 | bytes 688128 | tf_op jit(solution)/shard_map/dot_general | solution.py:41
  11.0 0.2 fusion.144
  11.2 0.2 fusion.140
  11.7 0.2 fusion.37
  12.0 0.2 fusion.36
  12.9 0.3 iota_compare_fusion.9
  13.2 3.0 %fusion.20 = f32[2,8192]{1,0:T(2,128)} fusion(s32[8192]{0:T(1024)S(1)} %get-tuple-element.34, pred[64,8192]{1,0:T(8,128)(4,1)S(1)} %iota_compare_fusion.9, f32[1,64,128]{2,1,0:T(8,128)S(1)} %fusion.36, f32[1,64,128]{2,1,0:T(8,128)S(1)} %fusion.37), kind=kOutput, calls=%fused_computation.31 | convolution fusion | flops 1613758464 | bytes 688128 | tf_op jit(solution)/shard_map/dot_general | solution.py:41
  16.2 16.2 %all-to-all-start = ((f32[2,64,128]{2,0,1:T(2,128)}), f32[2,64,128]{2,0,1:T(2,128)S(1)}, u32[]{:S(2)}, u32[]{:S(2)}) async-start(f32[2,64,128]{2,0,1:T(2,128)} %bitcast.42), calls=%async_computation | async-start | bytes 131072 | tf_op jit(solution)/shard_map/all_to_all | solution.py:250
  33.5 0.2 fusion.182
  33.7 0.3 fusion.260
  34.0 0.2 fusion.259
  34.2 0.2 convolution_select_fusion.8
  34.5 0.2 convolution_select_fusion.6
  34.9 0.2 fusion.184
  35.2 0.3 fusion.258
  35.4 0.2 fusion.257
  35.7 0.2 convolution_select_fusion.12
  35.9 0.2 convolution_select_fusion.10
  37.0 0.3 iota_compare_fusion.10
  37.9 0.3 iota_compare_fusion.11
  38.7 0.3 iota_compare_fusion.12
  39.4 0.2 fusion.256
  39.6 0.2 fusion.255
  39.9 0.2 convolution_select_fusion.16
  40.3 0.3 fusion.254
  40.6 0.2 fusion.253
  40.9 4.1 %all-to-all-done = f32[2,64,128]{2,0,1:T(2,128)S(1)} async-done(((f32[2,64,128]{2,0,1:T(2,128)}), f32[2,64,128]{2,0,1:T(2,128)S(1)}, u32[]{:S(2)}, u32[]{:S(2)}) %all-to-all-start) | async-done | bytes 65568 | tf_op jit(solution)/shard_map/all_to_all | solution.py:250
  45.0 2.4 %fusion.23 = f32[2,8192]{1,0:T(2,128)S(1)} fusion(s32[8192]{0:T(1024)S(1)} %get-tuple-element.36, pred[64,8192]{1,0:T(8,128)(4,1)S(1)} %iota_compare_fusion.10, f32[2,64,128]{2,0,1:T(2,128)S(1)} %all-to-all-done), kind=kOutput, calls=%fused_computation.32 | convolution fusion | flops 1613742080 | bytes 688128 | tf_op jit(solution)/shard_map/dot_general | solution.py:41
  47.5 0.2 fusion.138
  47.7 0.2 fusion.134
  47.9 0.2 fusion.35
  48.2 0.2 fusion.34
  48.4 2.4 %fusion.26 = f32[2,8192]{1,0:T(2,128)S(1)} fusion(s32[8192]{0:T(1024)S(1)} %get-tuple-element.38, pred[64,8192]{1,0:T(8,128)(4,1)S(1)} %iota_compare_fusion.11, f32[1,64,128]{2,1,0:T(8,128)S(1)} %fusion.34, f32[1,64,128]{2,1,0:T(8,128)S(1)} %fusion.35), kind=kOutput, calls=%fused_computation.33 | convolution fusion | flops 1613758464 | bytes 688128 | tf_op jit(solution)/shard_map/dot_general | solution.py:41
  50.9 0.2 fusion.132
  51.1 0.2 fusion.128
  51.4 0.2 fusion.33
  51.6 0.2 fusion.32
  51.9 2.4 %fusion.29 = f32[2,8192]{1,0:T(2,128)S(1)} fusion(s32[8192]{0:T(1024)S(1)} %get-tuple-element.40, pred[64,8192]{1,0:T(8,128)(4,1)S(1)} %iota_compare_fusion.12, f32[1,64,128]{2,1,0:T(8,128)S(1)} %fusion.32, f32[1,64,128]{2,1,0:T(8,128)S(1)} %fusion.33), kind=kOutput, calls=%fused_computation.34 | convolution fusion | flops 1613758464 | bytes 688128 | tf_op jit(solution)/shard_map/dot_general | solution.py:41
  54.3 3.1 %collective-permute-start = (f32[2,8192]{1,0:T(2,128)S(1)}, f32[2,8192]{1,0:T(2,128)S(1)}, u32[]{:S(2)}, u32[]{:S(2)}) collective-permute-start(f32[2,8192]{1,0:T(2,128)S(1)} %broadcast_multiply_fusion), channel_id=1, source_target_pairs={{0,512},{64,576},{128,640},{192,704},{256,768},{320,832},{384,896}... | collective-permute-start | bytes 196616 | tf_op jit(solution)/shard_map/ppermute | solution.py:12
  57.5 0.2 convolution_select_fusion.14
  57.8 4.2 %collective-permute-done = f32[2,8192]{1,0:T(2,128)S(1)} collective-permute-done((f32[2,8192]{1,0:T(2,128)S(1)}, f32[2,8192]{1,0:T(2,128)S(1)}, u32[]{:S(2)}, u32[]{:S(2)}) %collective-permute-start) | collective-permute-done | bytes 65568 | tf_op jit(solution)/shard_map/ppermute | solution.py:12
  62.0 0.3 fusion.88
  62.4 2.7 %collective-permute-start.1 = (f32[2,8192]{1,0:T(2,128)S(1)}, f32[2,8192]{1,0:T(2,128)S(1)}, u32[]{:S(2)}, u32[]{:S(2)}) collective-permute-start(f32[2,8192]{1,0:T(2,128)S(1)} %reshape.699), channel_id=1, source_target_pairs={{0,256},{64,320},{128,384},{192,448},{256,0},{320,64},{384,128},{4... | collective-permute-start | bytes 196616 | tf_op jit(solution)/shard_map/ppermute | solution.py:12
  65.3 3.3 %collective-permute-done.1 = f32[2,8192]{1,0:T(2,128)S(1)} collective-permute-done((f32[2,8192]{1,0:T(2,128)S(1)}, f32[2,8192]{1,0:T(2,128)S(1)}, u32[]{:S(2)}, u32[]{:S(2)}) %collective-permute-start.1) | collective-permute-done | bytes 65568 | tf_op jit(solution)/shard_map/ppermute | solution.py:12
  68.6 0.3 fusion.72
  69.0 15.7 %collective-permute-start.2 = (f32[2,8192]{1,0:T(2,128)S(1)}, f32[2,8192]{1,0:T(2,128)S(1)}, u32[]{:S(2)}, u32[]{:S(2)}) collective-permute-start(f32[2,8192]{1,0:T(2,128)S(1)} %reshape.701), channel_id=1, source_target_pairs={{0,64},{64,0},{128,192},{192,128},{256,320},{320,256},{384,448},{4... | collective-permute-start | bytes 196616 | tf_op jit(solution)/shard_map/ppermute | solution.py:12
  84.7 0.2 convolution_select_fusion.20
  85.0 9.4 %collective-permute-done.2 = f32[2,8192]{1,0:T(2,128)S(1)} collective-permute-done((f32[2,8192]{1,0:T(2,128)S(1)}, f32[2,8192]{1,0:T(2,128)S(1)}, u32[]{:S(2)}, u32[]{:S(2)}) %collective-permute-start.2) | collective-permute-done | bytes 65568 | tf_op jit(solution)/shard_map/ppermute | solution.py:12
  94.5 0.3 fusion.56
  94.9 18.3 %collective-permute-start.3 = (f32[2,8192]{1,0:T(2,128)S(1)}, f32[2,8192]{1,0:T(2,128)S(1)}, u32[]{:S(2)}, u32[]{:S(2)}) collective-permute-start(f32[2,8192]{1,0:T(2,128)S(1)} %reshape.703), channel_id=1, source_target_pairs={{0,128},{64,192},{128,0},{192,64},{256,384},{320,448},{384,256},{4... | collective-permute-start | bytes 196616 | tf_op jit(solution)/shard_map/ppermute | solution.py:12
  113.2 0.2 convolution_select_fusion.18
  113.4 12.0 %collective-permute-done.3 = f32[2,8192]{1,0:T(2,128)S(1)} collective-permute-done((f32[2,8192]{1,0:T(2,128)S(1)}, f32[2,8192]{1,0:T(2,128)S(1)}, u32[]{:S(2)}, u32[]{:S(2)}) %collective-permute-start.3) | collective-permute-done | bytes 65568 | tf_op jit(solution)/shard_map/ppermute | solution.py:12
  125.4 1.0 fusion.40
  (102 shorter events, 6.8 us)
Async XLA Ops:
  0.0 4.1 %copy-start = (f32[2,1,1,8192]{3,2,1,0:T(1,128)S(1)}, f32[2,1,1,8192]{3,2,1,0:T(1,128)}, u32[]{:S(2)}) copy-start(f32[2,1,1,8192]{3,2,1,0:T(1,128)} %param.7) | copy-start | bytes 196612
  4.1 2.5 %copy-start.1 = (f32[4,2,128,128]{3,2,1,0:T(8,128)S(1)}, f32[4,2,128,128]{3,2,1,0:T(8,128)}, u32[]{:S(2)}) copy-start(f32[4,2,128,128]{3,2,1,0:T(8,128)} %param.8) | copy-start | bytes 1572868
  8.5 3.0 %copy-start.4 = (s32[23]{0:T(128)S(1)}, s32[23]{0:T(128)}, u32[]{:S(2)}) copy-start(s32[23]{0:T(128)} %param.11) | copy-start | bytes 280
  13.2 19.2 %copy-start.2 = (s32[23]{0:T(128)S(1)}, s32[23]{0:T(128)}, u32[]{:S(2)}) copy-start(s32[23]{0:T(128)} %param.10) | copy-start | bytes 280
  13.2 20.1 %copy-start.3 = (f32[2,4,4]{2,1,0:T(4,128)S(1)}, f32[2,4,4]{2,1,0:T(4,128)}, u32[]{:S(2)}) copy-start(f32[2,4,4]{2,1,0:T(4,128)} %param.9) | copy-start | bytes 388
  16.2 28.8 %all-to-all-start = ((f32[2,64,128]{2,0,1:T(2,128)}), f32[2,64,128]{2,0,1:T(2,128)S(1)}, u32[]{:S(2)}, u32[]{:S(2)}) async-start(f32[2,64,128]{2,0,1:T(2,128)} %bitcast.42), calls=%async_computation | async-start | bytes 131072 | tf_op jit(solution)/shard_map/all_to_all | solution.py:250
  37.9 1.1 copy-start.5
  54.3 7.7 %collective-permute-start = (f32[2,8192]{1,0:T(2,128)S(1)}, f32[2,8192]{1,0:T(2,128)S(1)}, u32[]{:S(2)}, u32[]{:S(2)}) collective-permute-start(f32[2,8192]{1,0:T(2,128)S(1)} %broadcast_multiply_fusion), channel_id=1, source_target_pairs={{0,512},{64,576},{128,640},{192,704},{256,768},{320,832},{384,896}... | collective-permute-start | bytes 196616 | tf_op jit(solution)/shard_map/ppermute | solution.py:12
  62.4 6.2 %collective-permute-start.1 = (f32[2,8192]{1,0:T(2,128)S(1)}, f32[2,8192]{1,0:T(2,128)S(1)}, u32[]{:S(2)}, u32[]{:S(2)}) collective-permute-start(f32[2,8192]{1,0:T(2,128)S(1)} %reshape.699), channel_id=1, source_target_pairs={{0,256},{64,320},{128,384},{192,448},{256,0},{320,64},{384,128},{4... | collective-permute-start | bytes 196616 | tf_op jit(solution)/shard_map/ppermute | solution.py:12
  69.0 25.4 %collective-permute-start.2 = (f32[2,8192]{1,0:T(2,128)S(1)}, f32[2,8192]{1,0:T(2,128)S(1)}, u32[]{:S(2)}, u32[]{:S(2)}) collective-permute-start(f32[2,8192]{1,0:T(2,128)S(1)} %reshape.701), channel_id=1, source_target_pairs={{0,64},{64,0},{128,192},{192,128},{256,320},{320,256},{384,448},{4... | collective-permute-start | bytes 196616 | tf_op jit(solution)/shard_map/ppermute | solution.py:12
  94.9 30.5 %collective-permute-start.3 = (f32[2,8192]{1,0:T(2,128)S(1)}, f32[2,8192]{1,0:T(2,128)S(1)}, u32[]{:S(2)}, u32[]{:S(2)}) collective-permute-start(f32[2,8192]{1,0:T(2,128)S(1)} %reshape.703), channel_id=1, source_target_pairs={{0,128},{64,192},{128,0},{192,64},{256,384},{320,448},{384,256},{4... | collective-permute-start | bytes 196616 | tf_op jit(solution)/shard_map/ppermute | solution.py:12
